TPU v7x, 128 devices: a whole 4x4x4 slice. The times are simulated.
128 devices in a mesh: inline: 16 (over z, x), crosslin: 8 (over y, core).
Axes of the slice: x: 4, y: 4, z: 4, core: 2. Of those that a mesh axis runs over, the one named last changes fastest.
Arguments:
- grid_feat: bfloat16 [262144, 512], P(('inline', 'crosslin')), may hold values from -68 to 68
- cotangent: bfloat16 [262144, 512], P(('inline', 'crosslin')), may hold values from -6 to 6
- trace_feat: bfloat16 [16384, 512], P(('inline', 'crosslin')), may hold values from -6 to 6
- trace_dest: int32 [16384, 2], P(('inline', 'crosslin')), may hold values from 0 to 127, all different within a row; in each aligned block of 128 rows (0 to 127, 128 to 255, ...) at most 4 rows name the same one
- query_weight: bfloat16 [512, 512], replicated, may hold values from -0.25 to 0.25
- key_weight: bfloat16 [512, 512], replicated, may hold values from -0.25 to 0.25
- value_weight: bfloat16 [512, 512], replicated, may hold values from -0.25 to 0.25
- output_weight: bfloat16 [512, 512], replicated, may hold values from -0.25 to 0.25
Outputs:
- grad_grid: bfloat16 [262144, 512], P(('inline', 'crosslin'))
- grad_trace: float32 [16384, 512], P(('inline', 'crosslin'))
- grad_query: float32 [512, 512], replicated
- grad_key: float32 [512, 512], replicated
- grad_value: float32 [512, 512], replicated
- grad_output: float32 [512, 512], replicated
Inputs may be any that keep to these rules, and one draw needn't show every extreme that they name: `trace_dest`: in the 128 rows of one device no tile is named by more than 4 rows, a bound that some block reaches; a row names 2 different tiles; every tile is named by some row.
All inputs are finite; a program needn't handle non-finite values.
Results may differ from a plain program's by a relative error of at most 0.013.
The roundings to bfloat16 on the way count: a program that leaves them out, or rounds other values in their place, can miss the bound.
Values may be sent and summed in bfloat16 or wider, within the bound.
No kernel may reach another device: no remote copies, remote signals or barrier semaphores. Data moves between devices by JAX's collectives and lax.ppermute only.
A program may use at most 64 MiB of HBM per device.

v0:
```python
import jax
import jax.numpy as jnp
from jax import lax
from jax.sharding import PartitionSpec as P

HEADS = 8
TOP = 2


def slot_table(targets, tile_count, capacity):
    tile_ids = jnp.arange(tile_count, dtype=jnp.int32)
    named = jnp.any(targets[:, :, None] == tile_ids[None, None, :], axis=1)
    position = jnp.cumsum(named.astype(jnp.int32), axis=0) - 1
    places = jnp.arange(capacity, dtype=jnp.int32)
    chosen = named.T[:, None, :] & (position.T[:, None, :] == places[None, :, None])
    return (chosen, jnp.sum(named.astype(jnp.int32), axis=0))


def tile_grad(grid_rows, upstream, query_weight, output_weight, key_tile, value_tile, live_slots):
    model_width = grid_rows.shape[1]
    head_size = model_width // HEADS
    factor = head_size ** (-0.5)
    queries = jnp.dot(grid_rows, query_weight, preferred_element_type=jnp.float32).astype(
        jnp.bfloat16
    )
    out_grad = jnp.dot(upstream, output_weight.T, preferred_element_type=jnp.float32).astype(
        jnp.bfloat16
    )

    def one_head(head_index):
        offset = head_index * head_size
        query_head = lax.dynamic_slice_in_dim(queries, offset, head_size, 1)
        key_head = lax.dynamic_slice_in_dim(key_tile, offset, head_size, 1)
        value_head = lax.dynamic_slice_in_dim(value_tile, offset, head_size, 1)
        grad_head = lax.dynamic_slice_in_dim(out_grad, offset, head_size, 1)
        scores = jnp.dot(query_head, key_head.T, preferred_element_type=jnp.float32) * factor
        scores = jnp.where(live_slots[None, :], scores, -1e30)
        row_peak = jnp.max(scores, axis=1, keepdims=True)
        raised = jnp.exp(scores - row_peak)
        attention = raised / jnp.sum(raised, axis=1, keepdims=True)
        prob_half = attention.astype(jnp.bfloat16)
        head_out = jnp.dot(prob_half, value_head, preferred_element_type=jnp.float32).astype(
            jnp.bfloat16
        )
        prob_grad = jnp.dot(grad_head, value_head.T, preferred_element_type=jnp.float32)
        correction = jnp.sum(attention * prob_grad, axis=1, keepdims=True)
        score_grad = (attention * (prob_grad - correction) * factor).astype(jnp.bfloat16)
        query_grad = jnp.dot(score_grad, key_head, preferred_element_type=jnp.float32).astype(
            jnp.bfloat16
        )
        key_grad = jnp.dot(score_grad.T, query_head, preferred_element_type=jnp.float32).astype(
            jnp.bfloat16
        )
        value_grad = jnp.dot(prob_half.T, grad_head, preferred_element_type=jnp.float32).astype(
            jnp.bfloat16
        )
        return (head_out, query_grad, key_grad, value_grad)

    def join_heads(stacked):
        return jnp.transpose(stacked, (1, 0, 2)).reshape(stacked.shape[1], model_width)

    stacked = lax.map(one_head, jnp.arange(HEADS, dtype=jnp.int32))
    attn_out, query_grad, key_grad, value_grad = [
        join_heads(stacked_part) for stacked_part in stacked
    ]
    part_output = jnp.dot(attn_out.T, upstream, preferred_element_type=jnp.float32)
    grad_grid = jnp.dot(query_grad, query_weight.T, preferred_element_type=jnp.float32).astype(
        jnp.bfloat16
    )
    part_query = jnp.dot(grid_rows.T, query_grad, preferred_element_type=jnp.float32)
    return (grad_grid, key_grad, value_grad, part_output, part_query)


def send_slots(outgoing, counts):
    arrived, live_counts = (
        lax.all_to_all(outgoing, ("inline", "crosslin"), split_axis=0, concat_axis=0, tiled=True),
        lax.all_to_all(counts, ("inline", "crosslin"), split_axis=0, concat_axis=0, tiled=True),
    )
    return (arrived, live_counts)


def send_back(returned):
    result_rows = lax.all_to_all(
        returned, ("inline", "crosslin"), split_axis=0, concat_axis=0, tiled=True
    )
    return result_rows


def wide_return(
    key_grad, value_grad, picker, key_weight, value_weight, trace_feat, tile_count, capacity
):
    model_width = trace_feat.shape[1]
    returned = jnp.concatenate([key_grad, value_grad], axis=1).reshape(
        tile_count, capacity, 2 * model_width
    )
    returned = send_back(returned)
    key_back = returned[:, :, :model_width]
    value_back = returned[:, :, model_width:]
    slot_trace = jnp.einsum("tjd,ed->tje", key_back, key_weight, preferred_element_type=jnp.float32)
    slot_trace = slot_trace + jnp.einsum(
        "tjd,ed->tje", value_back, value_weight, preferred_element_type=jnp.float32
    )
    slot_trace = slot_trace.astype(jnp.bfloat16)
    grad_trace = jnp.einsum("tjr,tje->re", picker, slot_trace, preferred_element_type=jnp.float32)
    summed = jnp.einsum("tjr,tjd->rd", picker, returned, preferred_element_type=jnp.float32)
    trace_wide = trace_feat.astype(jnp.float32)
    part_key = jnp.dot(trace_wide.T, summed[:, :model_width], precision=lax.Precision.HIGHEST)
    part_value = jnp.dot(trace_wide.T, summed[:, model_width:], precision=lax.Precision.HIGHEST)
    return (grad_trace, part_key, part_value)


def on_device(
    grid_feat,
    cotangent,
    trace_feat,
    trace_dest,
    query_weight,
    key_weight,
    value_weight,
    output_weight,
):
    tile_count = lax.axis_size("inline") * lax.axis_size("crosslin")
    trace_rows = trace_feat.shape[0]
    model_width = trace_feat.shape[1]
    capacity = 2 * trace_rows * TOP // tile_count
    chosen, counts = slot_table(trace_dest, tile_count, capacity)
    picker = chosen.astype(jnp.bfloat16)
    places = jnp.arange(capacity, dtype=jnp.int32)
    key_rows = jnp.dot(trace_feat, key_weight, preferred_element_type=jnp.float32).astype(
        jnp.bfloat16
    )
    value_rows = jnp.dot(trace_feat, value_weight, preferred_element_type=jnp.float32).astype(
        jnp.bfloat16
    )
    key_value = jnp.concatenate([key_rows, value_rows], axis=1)
    outgoing = jnp.einsum(
        "tjr,rd->tjd", picker, key_value, preferred_element_type=jnp.float32
    ).astype(jnp.bfloat16)
    arrived, live_counts = send_slots(outgoing, counts.reshape(tile_count, 1))
    arrived = arrived.reshape(tile_count * capacity, 2 * model_width)
    key_tile = arrived[:, :model_width]
    value_tile = arrived[:, model_width:]
    live_slots = (places[None, :] < live_counts).reshape(-1)
    grad_grid, key_grad, value_grad, part_output, part_query = tile_grad(
        grid_feat, cotangent, query_weight, output_weight, key_tile, value_tile, live_slots
    )
    grad_trace, part_key, part_value = wide_return(
        key_grad, value_grad, picker, key_weight, value_weight, trace_feat, tile_count, capacity
    )
    grad_query, grad_key, grad_value, grad_output = lax.psum(
        (part_query, part_key, part_value, part_output), ("inline", "crosslin")
    )
    return (grad_grid, grad_trace, grad_query, grad_key, grad_value, grad_output)


def solution(mesh):
    in_specs = (
        P(("inline", "crosslin"), None),
        P(("inline", "crosslin"), None),
        P(("inline", "crosslin"), None),
        P(("inline", "crosslin"), None),
        P(),
        P(),
        P(),
        P(),
    )
    out_specs = (
        P(("inline", "crosslin"), None),
        P(("inline", "crosslin"), None),
        P(),
        P(),
        P(),
        P(),
    )
    return jax.shard_map(
        on_device, mesh=mesh, in_specs=in_specs, out_specs=out_specs, check_vma=False
    )
```

profile of v0, /device:TPU:1, one launch (start us, length us, event | category | flops | bytes accessed | tf_op | source)
XLA Modules:
  0.0 383.0 jit_solution(17440128705031874745)
XLA Ops:
  8.9 11.5 %all-to-all-start = ((s32[128,1,1]{2,1,0:T(1,128)}), s32[128,1,1]{2,1,0:T(1,128)S(1)}, u32[]{:S(2)}, u32[]{:S(2)}) async-start(s32[128,1,1]{2,1,0:T(1,128)} %copy.55), calls=%async_computation | async-start | bytes 131072 | tf_op jit(solution)/shard_map/all_to_all | solution.py:77
  25.6 4.4 %all-to-all-done = s32[128,1,1]{2,1,0:T(1,128)S(1)} async-done(((s32[128,1,1]{2,1,0:T(1,128)}), s32[128,1,1]{2,1,0:T(1,128)S(1)}, u32[]{:S(2)}, u32[]{:S(2)}) %all-to-all-start) | async-done | bytes 544 | tf_op jit(solution)/shard_map/all_to_all | solution.py:77
  29.9 5.4 %all-to-all-start.1 = ((bf16[128,4,1024]{2,1,0:T(4,128)(2,1)}), bf16[128,4,1024]{2,1,0:T(4,128)(2,1)S(1)}, u32[]{:S(2)}, u32[]{:S(2)}) async-start(bf16[128,4,1024]{2,1,0:T(4,128)(2,1)} %copy.54), calls=%async_computation.1 | async-start | bytes 2097152 | tf_op jit(solution)/shard_map/all_to_all | solution.py:76
  35.4 4.3 %convolution_convert_fusion.5 = bf16[2048,512]{1,0:T(8,128)(2,1)} fusion(bf16[2048,512]{1,0:T(8,128)(2,1)} %param.11, bf16[512,512]{1,0:T(8,128)(2,1)} %param.17), kind=kOutput, calls=%fused_computation.40 | convolution fusion | flops 1074790400 | bytes 4718592 | tf_op jit(solution)/shard_map/dot_general | solution.py:26
  39.7 2.6 convolution_convert_fusion.6
  42.3 2.3 reduce
  44.7 9.6 %all-to-all-done.1 = bf16[128,4,1024]{2,1,0:T(4,128)(2,1)S(1)} async-done(((bf16[128,4,1024]{2,1,0:T(4,128)(2,1)}), bf16[128,4,1024]{2,1,0:T(4,128)(2,1)S(1)}, u32[]{:S(2)}, u32[]{:S(2)}) %all-to-all-start.1) | async-done | bytes 1048608 | tf_op jit(solution)/shard_map/all_to_all | solution.py:76
  56.6 122.7 %while.17 = (s32[]{:T(128)}, bf16[8,2048,64]{1,2,0:T(8,128)(2,1)}, bf16[8,2048,64]{1,2,0:T(8,128)(2,1)}, bf16[8,512,64]{1,2,0:T(8,128)(2,1)}, bf16[8,512,64]{1,2...) while((s32[]{:T(128)}, bf16[8,2048,64]{1,2,0:T(8,128)(2,1)}, ...), condition=%wide.region_7.8_spmd.clone, body=%wide.region_3.7_spmd.clone.sunk | while | flops 838134272 | bytes 51627252 | solution.py:62
  58.1 2.0 fusion.102
  65.4 1.9 fusion.107
  67.4 2.6 fusion.106
  70.0 1.9 fusion.104
  73.4 2.0 fusion.102
  80.8 1.9 fusion.107
  82.7 2.6 fusion.106
  85.3 1.9 fusion.104
  88.7 2.0 fusion.102
  96.1 1.9 fusion.107
  98.0 2.6 fusion.106
  100.6 1.9 fusion.104
  104.0 2.0 fusion.102
  111.4 1.9 fusion.107
  113.4 2.6 fusion.106
  116.0 1.9 fusion.104
  119.4 2.0 fusion.102
  126.7 2.0 fusion.107
  128.7 2.6 fusion.106
  131.3 1.9 fusion.104
  134.7 2.0 fusion.102
  142.1 2.0 fusion.107
  144.0 2.6 fusion.106
  150.0 2.0 fusion.102
  157.4 2.0 fusion.107
  159.4 2.6 fusion.106
  165.4 2.0 fusion.102
  172.8 2.0 fusion.107
  174.7 2.6 fusion.106
  185.7 2.6 pad_maximum_fusion
  188.3 4.7 %all-to-all-start.2 = ((bf16[128,4,1024]{2,1,0:T(4,128)(2,1)}), bf16[128,4,1024]{2,1,0:T(4,128)(2,1)S(1)}, u32[]{:S(2)}, u32[]{:S(2)}) async-start(bf16[128,4,1024]{2,1,0:T(4,128)(2,1)} %pad_maximum_fusion), calls=%async_computation.2 | async-start | bytes 2097152 | tf_op jit(solution)/shard_map/all_to_all | solution.py:83
  193.1 4.0 %convolution_bitcast_fusion.2 = f32[512,512]{0,1:T(8,128)} fusion(bf16[2048,512]{0,1:T(8,128)(2,1)} %bitcast.87, bf16[2048,512]{1,0:T(8,128)(2,1)S(1)} %copy-done), kind=kOutput, calls=%fused_computation.45 | convolution fusion | flops 1073741824 | bytes 5242880 | tf_op jit(solution)/shard_map/dot_general | solution.py:70
  197.0 3.9 %fusion.61 = f32[512,512]{1,0:T(8,128)} fusion(bf16[2048,512]{0,1:T(8,128)(2,1)} %bitcast.17, bf16[2048,512]{1,0:T(8,128)(2,1)S(1)} %copy-done.5), kind=kOutput, calls=%fused_computation.79 | convolution fusion | flops 1073741824 | bytes 5242880 | tf_op jit(solution)/shard_map/dot_general | solution.py:66
  200.9 11.1 %all-to-all-done.2 = bf16[128,4,1024]{2,1,0:T(4,128)(2,1)S(1)} async-done(((bf16[128,4,1024]{2,1,0:T(4,128)(2,1)}), bf16[128,4,1024]{2,1,0:T(4,128)(2,1)S(1)}, u32[]{:S(2)}, u32[]{:S(2)}) %all-to-all-start.2) | async-done | bytes 1048608 | tf_op jit(solution)/shard_map/all_to_all | solution.py:83
  216.1 4.4 %convolution_convert_fusion.4 = bf16[2048,512]{1,0:T(8,128)(2,1)} fusion(bf16[2048,512]{0,1:T(8,128)(2,1)} %bitcast.88, bf16[512,512]{1,0:T(8,128)(2,1)} %param.14), kind=kOutput, calls=%fused_computation.39 | convolution fusion | flops 1074790400 | bytes 4718592 | tf_op jit(solution)/shard_map/dot_general | solution.py:67
  222.2 2.6 fusion.35
  224.8 142.8 %all-reduce.3.cloned.1.call-done = (f32[512,512]{0,1:T(8,128)}, f32[512,512]{0,1:T(8,128)}, f32[512,512]{0,1:T(8,128)}, f32[512,512]{1,0:T(8,128)}) async-done(((f32[512,512]{0,1:T(8,128)}, f32[512,512]{0,1:T(8,128)}, f32[512,512]{0,1:T(8,128)}, f32[512,512]{1,0:T(8,128)}), (f32[512,512]{0,1:T(8,128)}, f32[512,512]{0,1:T(8,128)}, f32[512,512]{0,1:T(8,128)}, ...) | async-done | bytes 4194320 | tf_op jit(solution)/shard_map/psum | solution.py:150
  367.5 2.6 copy.61
  370.1 2.5 copy.62
  372.7 2.5 copy.63
  (118 shorter events, 77.1 us)
Async XLA Ops:
  7.2 32.6 %copy-start = (bf16[2048,512]{1,0:T(8,128)(2,1)S(1)}, bf16[2048,512]{1,0:T(8,128)(2,1)}, u32[]{:S(2)}) copy-start(bf16[2048,512]{1,0:T(8,128)(2,1)} %param.10) | copy-start | bytes 6291460
  8.9 21.0 %all-to-all-start = ((s32[128,1,1]{2,1,0:T(1,128)}), s32[128,1,1]{2,1,0:T(1,128)S(1)}, u32[]{:S(2)}, u32[]{:S(2)}) async-start(s32[128,1,1]{2,1,0:T(1,128)} %copy.55), calls=%async_computation | async-start | bytes 131072 | tf_op jit(solution)/shard_map/all_to_all | solution.py:77
  29.9 24.3 %all-to-all-start.1 = ((bf16[128,4,1024]{2,1,0:T(4,128)(2,1)}), bf16[128,4,1024]{2,1,0:T(4,128)(2,1)S(1)}, u32[]{:S(2)}, u32[]{:S(2)}) async-start(bf16[128,4,1024]{2,1,0:T(4,128)(2,1)} %copy.54), calls=%async_computation.1 | async-start | bytes 2097152 | tf_op jit(solution)/shard_map/all_to_all | solution.py:76
  35.4 4.3 %copy-start.6 = (bf16[512,512]{1,0:T(8,128)(2,1)S(1)}, bf16[512,512]{1,0:T(8,128)(2,1)}, u32[]{:S(2)}) copy-start(bf16[512,512]{1,0:T(8,128)(2,1)} %param.14) | copy-start | bytes 1572868
  58.1 2.9 copy-start.7
  73.4 2.9 copy-start.7
  88.7 2.9 copy-start.7
  104.0 2.9 copy-start.7
  119.3 2.9 copy-start.7
  134.7 2.9 copy-start.7
  150.0 2.9 copy-start.7
  165.4 2.9 copy-start.7
  188.3 23.7 %all-to-all-start.2 = ((bf16[128,4,1024]{2,1,0:T(4,128)(2,1)}), bf16[128,4,1024]{2,1,0:T(4,128)(2,1)S(1)}, u32[]{:S(2)}, u32[]{:S(2)}) async-start(bf16[128,4,1024]{2,1,0:T(4,128)(2,1)} %pad_maximum_fusion), calls=%async_computation.2 | async-start | bytes 2097152 | tf_op jit(solution)/shard_map/all_to_all | solution.py:83
  193.0 174.5 %all-reduce.3.cloned.1.call-start = ((), (), s32[]{:S(2)}) async-start(), calls=%async_computation.3 | async-start | bytes 8388608 | tf_op jit(solution)/shard_map/psum | solution.py:150
  193.1 4.0 %copy-start.5 = (bf16[2048,512]{1,0:T(8,128)(2,1)S(1)}, bf16[2048,512]{1,0:T(8,128)(2,1)}, u32[]{:S(2)}) copy-start(bf16[2048,512]{1,0:T(8,128)(2,1)} %param.11) | copy-start | bytes 6291460
  197.0 15.8 %copy-start.3 = (bf16[128,512]{1,0:T(8,128)(2,1)S(1)}, bf16[128,512]{1,0:T(8,128)(2,1)}, u32[]{:S(2)}) copy-start(bf16[128,512]{1,0:T(8,128)(2,1)} %param.12) | copy-start | bytes 393220
  216.1 5.7 %copy-start.2 = (bf16[512,512]{1,0:T(8,128)(2,1)S(1)}, bf16[512,512]{1,0:T(8,128)(2,1)}, u32[]{:S(2)}) copy-start(bf16[512,512]{1,0:T(8,128)(2,1)} %param.15) | copy-start | bytes 1572868
  220.8 1.0 copy-start.1
  367.5 7.7 %copy-start.4 = (f32[512,512]{1,0:T(8,128)S(1)}, f32[512,512]{1,0:T(8,128)}, u32[]{:S(2)}) copy-start(f32[512,512]{1,0:T(8,128)} %get-tuple-element.282) | copy-start | bytes 3145732
Sparse Core Ops, SparseCore 0:
  216.2 151.2 all-reduce.2
where the time goes:
time: 384 us; the launch traced here: 383 us
  waiting for transfers between devices  168 us (44%)
  matrix products  119 us (31%)
  other arithmetic  27.3 us (7%)
  local copies, waits for them, and re-layouts  26.8 us (7%)
  starting transfers between devices  21.6 us (6%)
  between operations  14.2 us (4%)
  loops' own time  5.71 us (1%)
    psum x1, waiting for transfers between devices, on_device(): lax.psum((part_query, part_key, part_value, part_output), ('inline', 'cro...  143 us
    dot_general x8, matrix products, one_head(): jnp.dot(score_grad.T, query_head, preferred_element_type=jnp.float32)  21 us
    dot_general x8, matrix products, one_head(): jnp.dot(query_head, key_head.T, preferred_element_type=jnp.float32) * factor  16 us
    dot_general x8, matrix products, one_head(): jnp.dot(prob_half.T, grad_head, preferred_element_type=jnp.float32)  15.6 us
    dot_general x8, matrix products, one_head(): jnp.dot(prob_half, value_head, preferred_element_type=jnp.float32)  15.4 us
    convert_element_type x8, other arithmetic, one_head(): (attention * (prob_grad - correction) * factor).astype(jnp.bfloat16)  13.3 us
    dot_general x8, matrix products, one_head(): jnp.dot(grad_head, value_head.T, preferred_element_type=jnp.float32)  11.7 us
    all_to_all x1, starting transfers between devices, send_slots(): lax.all_to_all(counts, ('inline', 'crosslin'), split_axis=0, concat_axis=...  11.5 us
  transfers between devices with their start and end apart: 4, of which 4 were waited for; matrix products, arithmetic and copies ran while one was open for 8% of the time, Pallas kernels for 0%

commit v1 on v0

--- a/solution.py
+++ b/solution.py
@@ -71,12 +71,11 @@
     return (grad_grid, key_grad, value_grad, part_output, part_query)
 
 
-def send_slots(outgoing, counts):
-    arrived, live_counts = (
-        lax.all_to_all(outgoing, ("inline", "crosslin"), split_axis=0, concat_axis=0, tiled=True),
-        lax.all_to_all(counts, ("inline", "crosslin"), split_axis=0, concat_axis=0, tiled=True),
+def send_slots(outgoing):
+    arrived = lax.all_to_all(
+        outgoing, ("inline", "crosslin"), split_axis=0, concat_axis=0, tiled=True
     )
-    return (arrived, live_counts)
+    return arrived
 
 
 def send_back(returned):
@@ -84,29 +83,6 @@
         returned, ("inline", "crosslin"), split_axis=0, concat_axis=0, tiled=True
     )
     return result_rows
-
-
-def wide_return(
-    key_grad, value_grad, picker, key_weight, value_weight, trace_feat, tile_count, capacity
-):
-    model_width = trace_feat.shape[1]
-    returned = jnp.concatenate([key_grad, value_grad], axis=1).reshape(
-        tile_count, capacity, 2 * model_width
-    )
-    returned = send_back(returned)
-    key_back = returned[:, :, :model_width]
-    value_back = returned[:, :, model_width:]
-    slot_trace = jnp.einsum("tjd,ed->tje", key_back, key_weight, preferred_element_type=jnp.float32)
-    slot_trace = slot_trace + jnp.einsum(
-        "tjd,ed->tje", value_back, value_weight, preferred_element_type=jnp.float32
-    )
-    slot_trace = slot_trace.astype(jnp.bfloat16)
-    grad_trace = jnp.einsum("tjr,tje->re", picker, slot_trace, preferred_element_type=jnp.float32)
-    summed = jnp.einsum("tjr,tjd->rd", picker, returned, preferred_element_type=jnp.float32)
-    trace_wide = trace_feat.astype(jnp.float32)
-    part_key = jnp.dot(trace_wide.T, summed[:, :model_width], precision=lax.Precision.HIGHEST)
-    part_value = jnp.dot(trace_wide.T, summed[:, model_width:], precision=lax.Precision.HIGHEST)
-    return (grad_trace, part_key, part_value)
 
 
 def on_device(
@@ -125,31 +101,38 @@
     capacity = 2 * trace_rows * TOP // tile_count
     chosen, counts = slot_table(trace_dest, tile_count, capacity)
     picker = chosen.astype(jnp.bfloat16)
-    places = jnp.arange(capacity, dtype=jnp.int32)
     key_rows = jnp.dot(trace_feat, key_weight, preferred_element_type=jnp.float32).astype(
         jnp.bfloat16
     )
     value_rows = jnp.dot(trace_feat, value_weight, preferred_element_type=jnp.float32).astype(
         jnp.bfloat16
     )
-    key_value = jnp.concatenate([key_rows, value_rows], axis=1)
+    flag = jnp.ones((trace_rows, 128), jnp.bfloat16)
+    packed = jnp.concatenate([key_rows, value_rows, trace_feat, flag], axis=1)
     outgoing = jnp.einsum(
-        "tjr,rd->tjd", picker, key_value, preferred_element_type=jnp.float32
+        "tjr,rd->tjd", picker, packed, preferred_element_type=jnp.float32
     ).astype(jnp.bfloat16)
-    arrived, live_counts = send_slots(outgoing, counts.reshape(tile_count, 1))
-    arrived = arrived.reshape(tile_count * capacity, 2 * model_width)
+    arrived = send_slots(outgoing)
+    arrived = arrived.reshape(tile_count * capacity, packed.shape[1])
     key_tile = arrived[:, :model_width]
-    value_tile = arrived[:, model_width:]
-    live_slots = (places[None, :] < live_counts).reshape(-1)
+    value_tile = arrived[:, model_width : 2 * model_width]
+    feat_tile = arrived[:, 2 * model_width : 3 * model_width]
+    live_slots = arrived[:, 3 * model_width] > 0.5
     grad_grid, key_grad, value_grad, part_output, part_query = tile_grad(
         grid_feat, cotangent, query_weight, output_weight, key_tile, value_tile, live_slots
     )
-    grad_trace, part_key, part_value = wide_return(
-        key_grad, value_grad, picker, key_weight, value_weight, trace_feat, tile_count, capacity
-    )
+    part_key = jnp.dot(feat_tile.T, key_grad, preferred_element_type=jnp.float32)
+    part_value = jnp.dot(feat_tile.T, value_grad, preferred_element_type=jnp.float32)
     grad_query, grad_key, grad_value, grad_output = lax.psum(
         (part_query, part_key, part_value, part_output), ("inline", "crosslin")
     )
+    slot_trace = jnp.dot(key_grad, key_weight.T, preferred_element_type=jnp.float32)
+    slot_trace = slot_trace + jnp.dot(
+        value_grad, value_weight.T, preferred_element_type=jnp.float32
+    )
+    slot_trace = slot_trace.astype(jnp.bfloat16).reshape(tile_count, capacity, model_width)
+    returned = send_back(slot_trace)
+    grad_trace = jnp.einsum("tjr,tje->re", picker, returned, preferred_element_type=jnp.float32)
     return (grad_grid, grad_trace, grad_query, grad_key, grad_value, grad_output)
 
 

time: 384 us -> 362 us (0.943)
  waiting for transfers between devices: 168 us -> 159 us
  matrix products: 119 us -> 114 us
  starting transfers between devices: 21.6 us -> 16.8 us
  other arithmetic: 27.3 us -> 22.6 us
    psum x1, waiting for transfers between devices: 143 us -> 130 us  [on_device(): lax.psum((part_query, part_key, part_value, part_output), ('inline', 'cro...]
    all_to_all x1 -> x0, starting transfers between devices: 11.5 us -> none  [send_slots(): lax.all_to_all(counts, ('inline', 'crosslin'), split_axis=0, concat_axis=...]
    all_to_all x1, waiting for transfers between devices: 9.57 us -> 18.7 us  [send_slots(): lax.all_to_all(outgoing, ('inline', 'crosslin'), split_axis=0, concat_axi...]
    while x16 -> x32, local copies, waits for them, and re-layouts: 0.03 us -> 6.83 us
    all_to_all x1, starting transfers between devices: 5.41 us -> 11.9 us  [send_slots(): lax.all_to_all(outgoing, ('inline', 'crosslin'), split_axis=0, concat_axi...]
    dot_general x8, matrix products: 15.6 us -> 10.6 us  [one_head(): jnp.dot(prob_half.T, grad_head, preferred_element_type=jnp.float32)]
    all_to_all x1 -> x0, waiting for transfers between devices: 4.36 us -> none  [send_slots(): lax.all_to_all(counts, ('inline', 'crosslin'), split_axis=0, concat_axis=...]
    unnamed x18 -> x24, local copies, waits for them, and re-layouts: 9.65 us -> 7.94 us
  transfers between devices with their start and end apart: 4 -> 3, of which waited for: 4 -> 3; matrix products, arithmetic and copies ran while one was open for 8% -> 4% of each run, Pallas kernels for 0% -> 0%
where the time goes in v1:
time: 362 us; the launch traced here: 360 us
  waiting for transfers between devices  159 us (44%)
  matrix products  114 us (31%)
  local copies, waits for them, and re-layouts  28.8 us (8%)
  other arithmetic  22.6 us (6%)
  starting transfers between devices  16.8 us (5%)
  between operations  14.2 us (4%)
  loops' own time  5.71 us (2%)
    psum x1, waiting for transfers between devices, on_device(): lax.psum((part_query, part_key, part_value, part_output), ('inline', 'cro...  130 us
    dot_general x8, matrix products, one_head(): jnp.dot(score_grad.T, query_head, preferred_element_type=jnp.float32)  21 us
    all_to_all x1, waiting for transfers between devices, send_slots(): lax.all_to_all(outgoing, ('inline', 'crosslin'), split_axis=0, concat_axi...  18.7 us
    dot_general x8, matrix products, one_head(): jnp.dot(prob_half, value_head, preferred_element_type=jnp.float32)  15.4 us
    dot_general x8, matrix products, one_head(): jnp.dot(query_head, key_head.T, preferred_element_type=jnp.float32) * factor  14.8 us
    convert_element_type x8, other arithmetic, one_head(): (attention * (prob_grad - correction) * factor).astype(jnp.bfloat16)  13.3 us
    all_to_all x1, starting transfers between devices, send_slots(): lax.all_to_all(outgoing, ('inline', 'crosslin'), split_axis=0, concat_axi...  11.9 us
    dot_general x8, matrix products, one_head(): jnp.dot(grad_head, value_head.T, preferred_element_type=jnp.float32)  11.7 us
  transfers between devices with their start and end apart: 3, of which 3 were waited for; matrix products, arithmetic and copies ran while one was open for 4% of the time, Pallas kernels for 0%

profile of v1, /device:TPU:1, one launch (start us, length us, event | category | flops | bytes accessed | tf_op | source)
XLA Modules:
  0.0 360.5 jit_solution(8484255130443011278)
XLA Ops:
  12.6 2.5 copy.29
  15.1 11.9 %all-to-all-start = ((bf16[128,4,1664]{2,1,0:T(4,128)(2,1)}), bf16[128,4,1664]{2,1,0:T(4,128)(2,1)}, u32[]{:S(2)}, u32[]{:S(2)}) async-start(bf16[128,4,1664]{2,1,0:T(4,128)(2,1)} %copy.29), calls=%async_computation | async-start | bytes 3407872 | tf_op jit(solution)/shard_map/all_to_all | solution.py:75
  27.1 4.2 %convolution_convert_fusion.5 = bf16[2048,512]{1,0:T(8,128)(2,1)} fusion(bf16[2048,512]{1,0:T(8,128)(2,1)} %param.11, bf16[512,512]{1,0:T(8,128)(2,1)S(1)} %copy-done.9), kind=kOutput, calls=%fused_computation.38 | convolution fusion | flops 1074790400 | bytes 4718592 | tf_op jit(solution)/shard_map/dot_general | solution.py:26
  31.4 2.6 convolution_convert_fusion.6
  34.0 18.7 %all-to-all-done = bf16[128,4,1664]{2,1,0:T(4,128)(2,1)} async-done(((bf16[128,4,1664]{2,1,0:T(4,128)(2,1)}), bf16[128,4,1664]{2,1,0:T(4,128)(2,1)}, u32[]{:S(2)}, u32[]{:S(2)}) %all-to-all-start) | async-done | bytes 1703968 | tf_op jit(solution)/shard_map/all_to_all | solution.py:75
  52.7 3.8 %reshape.41 = bf16[512,1664]{1,0:T(8,128)(2,1)} reshape(bf16[128,4,1664]{2,1,0:T(4,128)(2,1)} %all-to-all-done) | data formatting | bytes 3407872 | tf_op jit(solution)/shard_map/reshape | solution.py:116
  56.5 2.1 fusion.52
  59.7 121.5 %while.16 = (s32[]{:T(128)}, bf16[8,2048,64]{1,2,0:T(8,128)(2,1)}, bf16[8,2048,64]{1,2,0:T(8,128)(2,1)}, bf16[8,512,64]{1,2,0:T(8,128)(2,1)}, bf16[8,512,64]{1,2...) while((s32[]{:T(128)}, bf16[8,2048,64]{1,2,0:T(8,128)(2,1)}, ...), condition=%wide.region_6.7_spmd, body=%wide.region_2.6_spmd.sunk | while | flops 838133760 | bytes 53721872 | solution.py:62
  60.9 1.9 fusion.99
  66.0 1.7 multiply_convert_fusion.2
  70.3 2.6 fusion.103
  72.9 1.9 fusion.101
  76.1 1.9 fusion.99
  81.2 1.7 multiply_convert_fusion.2
  85.5 2.6 fusion.103
  88.2 1.9 fusion.101
  91.3 1.9 fusion.99
  100.7 2.6 fusion.103
  103.4 1.9 fusion.101
  106.5 1.8 fusion.99
  111.6 1.7 multiply_convert_fusion.2
  115.9 2.6 fusion.103
  118.5 1.9 fusion.101
  121.7 1.9 fusion.99
  126.8 1.7 multiply_convert_fusion.2
  131.1 2.6 fusion.103
  133.7 1.9 fusion.101
  136.9 1.8 fusion.99
  142.0 1.7 multiply_convert_fusion.2
  146.3 2.6 fusion.103
  148.9 1.9 fusion.101
  152.1 1.8 fusion.99
  157.2 1.7 multiply_convert_fusion.2
  161.5 2.6 fusion.103
  164.1 1.9 fusion.101
  167.3 1.8 fusion.99
  176.7 2.6 fusion.103
  179.3 1.9 fusion.101
  181.2 2.6 fusion.33
  183.9 2.5 fusion.35
  186.4 2.2 convolution_bitcast_fusion
  188.6 3.8 %fusion.54 = f32[512,512]{1,0:T(8,128)} fusion(bf16[2048,512]{0,1:T(8,128)(2,1)} %bitcast.20, bf16[2048,512]{1,0:T(8,128)(2,1)S(1)} %copy-done.7), kind=kOutput, calls=%fused_computation.72 | convolution fusion | flops 1073741824 | bytes 5242880 | tf_op jit(solution)/shard_map/dot_general | solution.py:66
  196.5 4.9 %all-to-all-start.1 = ((bf16[128,4,512]{2,1,0:T(4,128)(2,1)}), bf16[128,4,512]{2,1,0:T(4,128)(2,1)S(1)}, u32[]{:S(2)}, u32[]{:S(2)}) async-start(bf16[128,4,512]{2,1,0:T(4,128)(2,1)} %reshape.45), calls=%async_computation.1 | async-start | bytes 1048576 | tf_op jit(solution)/shard_map/all_to_all | solution.py:82
  201.4 4.4 %convolution_convert_fusion.4 = bf16[2048,512]{1,0:T(8,128)(2,1)} fusion(bf16[2048,512]{0,1:T(8,128)(2,1)} %bitcast.81, bf16[512,512]{1,0:T(8,128)(2,1)} %param.14), kind=kOutput, calls=%fused_computation.37 | convolution fusion | flops 1074790400 | bytes 4718592 | tf_op jit(solution)/shard_map/dot_general | solution.py:67
  205.7 10.1 %all-to-all-done.1 = bf16[128,4,512]{2,1,0:T(4,128)(2,1)S(1)} async-done(((bf16[128,4,512]{2,1,0:T(4,128)(2,1)}), bf16[128,4,512]{2,1,0:T(4,128)(2,1)S(1)}, u32[]{:S(2)}, u32[]{:S(2)}) %all-to-all-start.1) | async-done | bytes 524320 | tf_op jit(solution)/shard_map/all_to_all | solution.py:82
  216.8 129.9 %all-reduce.3.cloned.1.call-done = (f32[512,512]{0,1:T(8,128)}, f32[512,512]{1,0:T(8,128)}, f32[512,512]{1,0:T(8,128)}, f32[512,512]{1,0:T(8,128)}) async-done(((f32[512,512]{0,1:T(8,128)}, f32[512,512]{1,0:T(8,128)}, f32[512,512]{1,0:T(8,128)}, f32[512,512]{1,0:T(8,128)}), (f32[512,512]{0,1:T(8,128)}, f32[512,512]{1,0:T(8,128)}, f32[512,512]{1,0:T(8,128)}, ...) | async-done | bytes 4194320 | tf_op jit(solution)/shard_map/psum | solution.py:126
  346.7 2.5 copy.31
  349.3 2.4 copy.58
  (117 shorter events, 68.2 us)
Async XLA Ops:
  7.2 24.2 %copy-start = (bf16[2048,512]{1,0:T(8,128)(2,1)S(1)}, bf16[2048,512]{1,0:T(8,128)(2,1)}, u32[]{:S(2)}) copy-start(bf16[2048,512]{1,0:T(8,128)(2,1)} %param.10) | copy-start | bytes 6291460
  15.1 12.0 %copy-start.9 = (bf16[512,512]{1,0:T(8,128)(2,1)S(1)}, bf16[512,512]{1,0:T(8,128)(2,1)}, u32[]{:S(2)}) copy-start(bf16[512,512]{1,0:T(8,128)(2,1)} %param.17) | copy-start | bytes 1572868
  15.1 37.6 %all-to-all-start = ((bf16[128,4,1664]{2,1,0:T(4,128)(2,1)}), bf16[128,4,1664]{2,1,0:T(4,128)(2,1)}, u32[]{:S(2)}, u32[]{:S(2)}) async-start(bf16[128,4,1664]{2,1,0:T(4,128)(2,1)} %copy.29), calls=%async_computation | async-start | bytes 3407872 | tf_op jit(solution)/shard_map/all_to_all | solution.py:75
  27.0 319.7 %all-reduce.3.cloned.1.call-start = ((), (), s32[]{:S(2)}) async-start(), calls=%async_computation.2 | async-start | bytes 8388608 | tf_op jit(solution)/shard_map/psum | solution.py:126
  27.1 4.3 %copy-start.10 = (bf16[512,512]{1,0:T(8,128)(2,1)S(1)}, bf16[512,512]{1,0:T(8,128)(2,1)}, u32[]{:S(2)}) copy-start(bf16[512,512]{1,0:T(8,128)(2,1)} %param.14) | copy-start | bytes 1572868
  62.8 1.0 copy-start.6
  62.8 1.8 copy-start.11
  78.0 1.0 copy-start.6
  78.0 1.8 copy-start.11
  93.2 1.0 copy-start.6
  93.2 1.8 copy-start.11
  108.4 1.0 copy-start.6
  108.4 1.8 copy-start.11
  123.6 1.0 copy-start.6
  123.6 1.8 copy-start.11
  138.7 1.0 copy-start.6
  138.8 1.8 copy-start.11
  153.9 1.0 copy-start.6
  153.9 1.8 copy-start.11
  169.1 1.0 copy-start.6
  169.1 1.8 copy-start.11
  181.2 2.7 copy-start.3
  181.2 5.2 %copy-start.8 = (bf16[8,2048,64]{1,2,0:T(8,128)(2,1)S(1)}, bf16[8,2048,64]{1,2,0:T(8,128)(2,1)}, u32[]{:S(2)}) copy-start(bf16[8,2048,64]{1,2,0:T(8,128)(2,1)} %get-tuple-element.66) | copy-start | bytes 6291460
  186.4 2.2 copy-start.7
  192.4 1.0 copy-start.2
  193.4 1.6 copy-start.1
  196.5 19.3 %all-to-all-start.1 = ((bf16[128,4,512]{2,1,0:T(4,128)(2,1)}), bf16[128,4,512]{2,1,0:T(4,128)(2,1)S(1)}, u32[]{:S(2)}, u32[]{:S(2)}) async-start(bf16[128,4,512]{2,1,0:T(4,128)(2,1)} %reshape.45), calls=%async_computation.1 | async-start | bytes 1048576 | tf_op jit(solution)/shard_map/all_to_all | solution.py:82
  349.3 2.4 copy-start.5
  349.3 3.4 copy-start.4
Sparse Core Ops, SparseCore 0:
  192.5 154.1 all-reduce.2

commit v2 on v1

--- a/solution.py
+++ b/solution.py
@@ -1,6 +1,8 @@
 import jax
 import jax.numpy as jnp
 from jax import lax
+from jax.experimental import pallas as pl
+from jax.experimental.pallas import tpu as pltpu
 from jax.sharding import PartitionSpec as P
 
 HEADS = 8
@@ -16,53 +18,78 @@
     return (chosen, jnp.sum(named.astype(jnp.int32), axis=0))
 
 
+def attention_kernel(q_ref, g_ref, k_ref, v_ref, live_ref, o_ref, dq_ref, dk_ref, dv_ref, dk_acc, dv_acc):
+    step = pl.program_id(0)
+    width = q_ref.shape[1]
+    head_size = width // HEADS
+    factor = head_size ** (-0.5)
+
+    @pl.when(step == 0)
+    def _():
+        dk_acc[...] = jnp.zeros_like(dk_acc)
+        dv_acc[...] = jnp.zeros_like(dv_acc)
+
+    live = live_ref[...] > 0.5
+    for h in range(HEADS):
+        cols = slice(h * head_size, (h + 1) * head_size)
+        q_h = q_ref[:, cols]
+        g_h = g_ref[:, cols]
+        k_h = k_ref[:, cols]
+        v_h = v_ref[:, cols]
+        nt = (((1,), (1,)), ((), ()))
+        tn = (((0,), (0,)), ((), ()))
+        scores = lax.dot_general(q_h, k_h, nt, preferred_element_type=jnp.float32) * factor
+        scores = jnp.where(live, scores, -1e30)
+        peak = jnp.max(scores, axis=1, keepdims=True)
+        raised = jnp.exp(scores - peak)
+        attention = raised / jnp.sum(raised, axis=1, keepdims=True)
+        prob_half = attention.astype(jnp.bfloat16)
+        o_ref[:, cols] = jnp.dot(prob_half, v_h, preferred_element_type=jnp.float32).astype(o_ref.dtype)
+        prob_grad = lax.dot_general(g_h, v_h, nt, preferred_element_type=jnp.float32)
+        correction = jnp.sum(attention * prob_grad, axis=1, keepdims=True)
+        score_grad = (attention * (prob_grad - correction) * factor).astype(jnp.bfloat16)
+        dq_ref[:, cols] = jnp.dot(score_grad, k_h, preferred_element_type=jnp.float32).astype(dq_ref.dtype)
+        dk_acc[:, cols] += lax.dot_general(score_grad, q_h, tn, preferred_element_type=jnp.float32)
+        dv_acc[:, cols] += lax.dot_general(prob_half, g_h, tn, preferred_element_type=jnp.float32)
+
+    @pl.when(step == pl.num_programs(0) - 1)
+    def _():
+        dk_ref[...] = dk_acc[...].astype(dk_ref.dtype)
+        dv_ref[...] = dv_acc[...].astype(dv_ref.dtype)
+
+
+def fused_attention(queries, out_grad, key_tile, value_tile, live, block=256):
+    rows, width = queries.shape
+    slots = key_tile.shape[0]
+    row_block = pl.BlockSpec((block, width), lambda i: (i, 0))
+    slot_block = pl.BlockSpec((slots, width), lambda i: (0, 0))
+    live_block = pl.BlockSpec((1, slots), lambda i: (0, 0))
+    return pl.pallas_call(
+        attention_kernel,
+        grid=(rows // block,),
+        in_specs=[row_block, row_block, slot_block, slot_block, live_block],
+        out_specs=[row_block, row_block, slot_block, slot_block],
+        out_shape=[
+            jax.ShapeDtypeStruct((rows, width), jnp.bfloat16),
+            jax.ShapeDtypeStruct((rows, width), jnp.bfloat16),
+            jax.ShapeDtypeStruct((slots, width), jnp.bfloat16),
+            jax.ShapeDtypeStruct((slots, width), jnp.bfloat16),
+        ],
+        scratch_shapes=[pltpu.VMEM((slots, width), jnp.float32), pltpu.VMEM((slots, width), jnp.float32)],
+        compiler_params=pltpu.CompilerParams(dimension_semantics=("arbitrary",)),
+    )(queries, out_grad, key_tile, value_tile, live.astype(jnp.float32).reshape(1, slots))
+
+
 def tile_grad(grid_rows, upstream, query_weight, output_weight, key_tile, value_tile, live_slots):
-    model_width = grid_rows.shape[1]
-    head_size = model_width // HEADS
-    factor = head_size ** (-0.5)
     queries = jnp.dot(grid_rows, query_weight, preferred_element_type=jnp.float32).astype(
         jnp.bfloat16
     )
     out_grad = jnp.dot(upstream, output_weight.T, preferred_element_type=jnp.float32).astype(
         jnp.bfloat16
     )
-
-    def one_head(head_index):
-        offset = head_index * head_size
-        query_head = lax.dynamic_slice_in_dim(queries, offset, head_size, 1)
-        key_head = lax.dynamic_slice_in_dim(key_tile, offset, head_size, 1)
-        value_head = lax.dynamic_slice_in_dim(value_tile, offset, head_size, 1)
-        grad_head = lax.dynamic_slice_in_dim(out_grad, offset, head_size, 1)
-        scores = jnp.dot(query_head, key_head.T, preferred_element_type=jnp.float32) * factor
-        scores = jnp.where(live_slots[None, :], scores, -1e30)
-        row_peak = jnp.max(scores, axis=1, keepdims=True)
-        raised = jnp.exp(scores - row_peak)
-        attention = raised / jnp.sum(raised, axis=1, keepdims=True)
-        prob_half = attention.astype(jnp.bfloat16)
-        head_out = jnp.dot(prob_half, value_head, preferred_element_type=jnp.float32).astype(
-            jnp.bfloat16
-        )
-        prob_grad = jnp.dot(grad_head, value_head.T, preferred_element_type=jnp.float32)
-        correction = jnp.sum(attention * prob_grad, axis=1, keepdims=True)
-        score_grad = (attention * (prob_grad - correction) * factor).astype(jnp.bfloat16)
-        query_grad = jnp.dot(score_grad, key_head, preferred_element_type=jnp.float32).astype(
-            jnp.bfloat16
-        )
-        key_grad = jnp.dot(score_grad.T, query_head, preferred_element_type=jnp.float32).astype(
-            jnp.bfloat16
-        )
-        value_grad = jnp.dot(prob_half.T, grad_head, preferred_element_type=jnp.float32).astype(
-            jnp.bfloat16
-        )
-        return (head_out, query_grad, key_grad, value_grad)
-
-    def join_heads(stacked):
-        return jnp.transpose(stacked, (1, 0, 2)).reshape(stacked.shape[1], model_width)
-
-    stacked = lax.map(one_head, jnp.arange(HEADS, dtype=jnp.int32))
-    attn_out, query_grad, key_grad, value_grad = [
-        join_heads(stacked_part) for stacked_part in stacked
-    ]
+    attn_out, query_grad, key_grad, value_grad = fused_attention(
+        queries, out_grad, key_tile, value_tile, live_slots
+    )
     part_output = jnp.dot(attn_out.T, upstream, preferred_element_type=jnp.float32)
     grad_grid = jnp.dot(query_grad, query_weight.T, preferred_element_type=jnp.float32).astype(
         jnp.bfloat16

time: 362 us -> 306 us (0.85)
  matrix products: 114 us -> 25.9 us
  Pallas kernels: 0 us -> 67.5 us
  other arithmetic: 22.6 us -> 2.72 us
  local copies, waits for them, and re-layouts: 28.8 us -> 17.5 us
  loops' own time: 5.71 us -> 0 us
    dot_general x48 -> x0, matrix products: 83.9 us -> none  [the longest x8 21 us: one_head(): jnp.dot(score_grad.T, query_head, preferred_element_type=jnp.float32)]
    pallas_call x0 -> x1, Pallas kernels: none -> 67.5 us  [fused_attention(): pl.pallas_call(attention_kernel, grid=(rows // block,), in_specs=[row_blo...]
    convert_element_type x8 -> x1, other arithmetic: 13.3 us -> 1.6 us  [fused_attention(): live.astype(jnp.float32).reshape(1, slots)]
    reduce_sum x8 -> x0, other arithmetic: 7.17 us -> none  [one_head(): attention = raised / jnp.sum(raised, axis=1, keepdims=True)]
    while x32 -> x0, local copies, waits for them, and re-layouts: 6.83 us -> none
    another operation x1 -> x0, loops' own time: 5.71 us -> none  [tile_grad(): stacked = lax.map(one_head, jnp.arange(HEADS, dtype=jnp.int32))]
    dynamic_slice x8 -> x0, local copies, waits for them, and re-layouts: 4.66 us -> none  [tile_grad(): stacked = lax.map(one_head, jnp.arange(HEADS, dtype=jnp.int32))]
    unnamed x24 -> x30, local copies, waits for them, and re-layouts: 7.94 us -> 7.98 us
where the time goes in v2:
time: 306 us; the launch traced here: 305 us
  waiting for transfers between devices  161 us (53%)
  Pallas kernels  67.5 us (22%)
  matrix products  25.9 us (8%)
  local copies, waits for them, and re-layouts  17.5 us (6%)
  starting transfers between devices  16.6 us (5%)
  between operations  14.2 us (5%)
    psum x1, waiting for transfers between devices, on_device(): lax.psum((part_query, part_key, part_value, part_output), ('inline', 'cro...  130 us
    pallas_call x1, Pallas kernels, fused_attention(): pl.pallas_call(attention_kernel, grid=(rows // block,), in_specs=[row_blo...  67.5 us
    all_to_all x1, waiting for transfers between devices, send_slots(): lax.all_to_all(outgoing, ('inline', 'crosslin'), split_axis=0, concat_axi...  20.4 us
    all_to_all x1, starting transfers between devices, send_slots(): lax.all_to_all(outgoing, ('inline', 'crosslin'), split_axis=0, concat_axi...  11.9 us
    all_to_all x1, waiting for transfers between devices, send_back(): lax.all_to_all(returned, ('inline', 'crosslin'), split_axis=0, concat_axi...  10.1 us
    unnamed x30, local copies, waits for them, and re-layouts  7.98 us
  transfers between devices with their start and end apart: 3, of which 3 were waited for; matrix products, arithmetic and copies ran while one was open for 4% of the time, Pallas kernels for 0%

profile of v2, /device:TPU:1, one launch (start us, length us, event | category | flops | bytes accessed | tf_op | source)
XLA Modules:
  0.0 305.1 jit_solution(8983289925479053288)
XLA Ops:
  7.2 0.0 copy-start
  7.2 0.9 fusion.17
  8.1 0.2 reduce_window_sum.11
  8.3 1.3 convolution_convert_fusion.5
  9.7 1.3 convolution_convert_fusion.4
  11.0 1.6 convolution_convert_fusion.1
  12.6 2.6 copy.30
  15.2 11.9 %all-to-all-start = ((bf16[128,4,1664]{2,1,0:T(4,128)(2,1)}), bf16[128,4,1664]{2,1,0:T(4,128)(2,1)}, u32[]{:S(2)}, u32[]{:S(2)}) async-start(bf16[128,4,1664]{2,1,0:T(4,128)(2,1)} %copy.30), calls=%async_computation | async-start | bytes 3407872 | tf_op jit(solution)/shard_map/all_to_all | solution.py:102
  27.1 0.0 copy-start.12
  27.1 0.0 all-reduce.3.cloned.1.call-start
  27.1 0.0 copy-done
  27.1 0.0 copy-done.11
  27.2 0.0 copy-start.8
  27.2 2.6 convolution_convert_fusion.2.g_ref
  29.8 0.0 copy-done.12
  29.8 0.0 copy-done.8
  29.8 2.6 convolution_convert_fusion.3.q_ref
  32.3 20.4 %all-to-all-done = bf16[128,4,1664]{2,1,0:T(4,128)(2,1)} async-done(((bf16[128,4,1664]{2,1,0:T(4,128)(2,1)}), bf16[128,4,1664]{2,1,0:T(4,128)(2,1)}, u32[]{:S(2)}, u32[]{:S(2)}) %all-to-all-start) | async-done | bytes 1703968 | tf_op jit(solution)/shard_map/all_to_all | solution.py:102
  52.7 3.8 %reshape.39 = bf16[512,1664]{1,0:T(8,128)(2,1)} reshape(bf16[128,4,1664]{2,1,0:T(4,128)(2,1)} %all-to-all-done) | data formatting | bytes 3407872 | tf_op jit(solution)/shard_map/reshape | solution.py:143
  56.6 1.6 convert_reduce_fusion
  58.2 2.2 fusion.21
  60.4 67.5 %shard_map.127 = (bf16[2048,512]{1,0:T(8,128)(2,1)}, bf16[2048,512]{1,0:T(8,128)(2,1)}, bf16[512,512]{1,0:T(8,128)(2,1)}, bf16[512,512]{1,0:T(8,128)(2,1)}) custom-call(bf16[2048,512]{1,0:T(8,128)(2,1)} %convolution_convert_fusion.3.q_ref, bf16[2048,512]{1,0:T(8,128)(2,1)} %convolution_convert_fusion.2.g_ref, bf16[512,512]{1,0:T(8,128)(2,1)} %get-tuple-element.43.k_ref, ...), custom_call_target="tpu_custom_call" | custom-call | tf_op jit(solution)/shard_map/pallas_call | solution.py:67
  127.8 0.0 copy-start.9
  127.9 0.0 copy-start.10
  127.9 4.0 %fusion.23 = f32[512,512]{1,0:T(8,128)} fusion(bf16[2048,512]{1,0:T(8,128)(2,1)} %get-tuple-element.13, bf16[2048,512]{1,0:T(8,128)(2,1)S(1)} %copy-done), kind=kOutput, calls=%fused_computation.35 | convolution fusion | flops 1073741824 | bytes 5242880 | tf_op jit(solution)/shard_map/dot_general | solution.py:93
  131.8 0.0 copy-done.9
  131.9 0.0 copy-done.10
  131.9 2.2 convolution_bitcast_fusion
  134.1 0.0 copy-done.1
  134.1 0.0 copy-done.5
  134.1 1.4 fusion.4
  135.5 0.0 copy-done.3
  135.5 1.4 fusion.2
  137.0 0.0 all-reduce.3.cloned.1.call-update
  137.0 1.0 copy-done.4
  138.0 1.6 fusion.22
  139.6 0.0 copy-done.2
  139.6 0.5 fusion
  140.1 0.9 reshape.40
  141.0 4.7 %all-to-all-start.1 = ((bf16[128,4,512]{2,1,0:T(4,128)(2,1)}), bf16[128,4,512]{2,1,0:T(4,128)(2,1)S(1)}, u32[]{:S(2)}, u32[]{:S(2)}) async-start(bf16[128,4,512]{2,1,0:T(4,128)(2,1)} %reshape.40), calls=%async_computation.1 | async-start | bytes 1048576 | tf_op jit(solution)/shard_map/all_to_all | solution.py:109
  145.7 4.3 %convolution_convert_fusion = bf16[2048,512]{1,0:T(8,128)(2,1)} fusion(bf16[2048,512]{1,0:T(8,128)(2,1)} %get-tuple-element.10, bf16[512,512]{1,0:T(8,128)(2,1)} %param.12), kind=kOutput, calls=%fused_computation | convolution fusion | flops 1074790400 | bytes 4718592 | tf_op jit(solution)/shard_map/dot_general | solution.py:94
  150.0 10.1 %all-to-all-done.1 = bf16[128,4,512]{2,1,0:T(4,128)(2,1)S(1)} async-done(((bf16[128,4,512]{2,1,0:T(4,128)(2,1)}), bf16[128,4,512]{2,1,0:T(4,128)(2,1)S(1)}, u32[]{:S(2)}, u32[]{:S(2)}) %all-to-all-start.1) | async-done | bytes 524320 | tf_op jit(solution)/shard_map/all_to_all | solution.py:109
  160.1 1.0 convolution_bitcast_fusion.1
  161.1 130.2 %all-reduce.3.cloned.1.call-done = (f32[512,512]{0,1:T(8,128)}, f32[512,512]{1,0:T(8,128)}, f32[512,512]{1,0:T(8,128)}, f32[512,512]{1,0:T(8,128)}) async-done(((f32[512,512]{0,1:T(8,128)}, f32[512,512]{1,0:T(8,128)}, f32[512,512]{1,0:T(8,128)}, f32[512,512]{1,0:T(8,128)}), (f32[512,512]{0,1:T(8,128)}, f32[512,512]{1,0:T(8,128)}, f32[512,512]{1,0:T(8,128)}, ...) | async-done | bytes 4194320 | tf_op jit(solution)/shard_map/psum | solution.py:153
  291.3 2.6 copy.32
  293.9 2.4 copy.40
  296.3 1.0 copy.41
  297.2 1.0 copy.42
  (14 shorter events, 0.0 us)
Async XLA Ops:
  7.2 20.0 %copy-start = (bf16[2048,512]{1,0:T(8,128)(2,1)S(1)}, bf16[2048,512]{1,0:T(8,128)(2,1)}, u32[]{:S(2)}) copy-start(bf16[2048,512]{1,0:T(8,128)(2,1)} %param.9) | copy-start | bytes 6291460
  15.2 12.0 %copy-start.11 = (bf16[512,512]{1,0:T(8,128)(2,1)S(1)}, bf16[512,512]{1,0:T(8,128)(2,1)}, u32[]{:S(2)}) copy-start(bf16[512,512]{1,0:T(8,128)(2,1)} %param.15) | copy-start | bytes 1572868
  15.2 37.6 %all-to-all-start = ((bf16[128,4,1664]{2,1,0:T(4,128)(2,1)}), bf16[128,4,1664]{2,1,0:T(4,128)(2,1)}, u32[]{:S(2)}, u32[]{:S(2)}) async-start(bf16[128,4,1664]{2,1,0:T(4,128)(2,1)} %copy.30), calls=%async_computation | async-start | bytes 3407872 | tf_op jit(solution)/shard_map/all_to_all | solution.py:102
  27.1 2.7 copy-start.12
  27.1 264.2 %all-reduce.3.cloned.1.call-start = ((), (), s32[]{:S(2)}) async-start(), calls=%async_computation.2 | async-start | bytes 8388608 | tf_op jit(solution)/shard_map/psum | solution.py:153
  27.2 2.6 copy-start.8
  127.8 4.0 %copy-start.9 = (bf16[2048,512]{1,0:T(8,128)(2,1)S(1)}, bf16[2048,512]{1,0:T(8,128)(2,1)}, u32[]{:S(2)}) copy-start(bf16[2048,512]{1,0:T(8,128)(2,1)} %param.8) | copy-start | bytes 6291460
  127.9 4.0 %copy-start.10 = (bf16[2048,512]{1,0:T(8,128)(2,1)S(1)}, bf16[2048,512]{1,0:T(8,128)(2,1)}, u32[]{:S(2)}) copy-start(bf16[2048,512]{1,0:T(8,128)(2,1)} %get-tuple-element.10) | copy-start | bytes 6291460
  131.9 2.3 copy-start.1
  131.9 2.3 copy-start.5
  134.1 1.4 copy-start.3
  137.0 1.0 copy-start.4
  138.0 1.6 copy-start.2
  141.0 19.1 %all-to-all-start.1 = ((bf16[128,4,512]{2,1,0:T(4,128)(2,1)}), bf16[128,4,512]{2,1,0:T(4,128)(2,1)S(1)}, u32[]{:S(2)}, u32[]{:S(2)}) async-start(bf16[128,4,512]{2,1,0:T(4,128)(2,1)} %reshape.40), calls=%async_computation.1 | async-start | bytes 1048576 | tf_op jit(solution)/shard_map/all_to_all | solution.py:109
  291.3 5.0 %copy-start.7 = (f32[512,512]{1,0:T(8,128)S(1)}, f32[512,512]{1,0:T(8,128)}, u32[]{:S(2)}) copy-start(f32[512,512]{1,0:T(8,128)} %get-tuple-element.48) | copy-start | bytes 3145732
  293.9 3.3 %copy-start.6 = (f32[512,512]{1,0:T(8,128)S(1)}, f32[512,512]{1,0:T(8,128)}, u32[]{:S(2)}) copy-start(f32[512,512]{1,0:T(8,128)} %get-tuple-element.49) | copy-start | bytes 3145732
Sparse Core Ops, SparseCore 0:
  137.1 154.1 all-reduce.2

commit v3 on v2

--- a/solution.py
+++ b/solution.py
@@ -58,7 +58,7 @@
         dv_ref[...] = dv_acc[...].astype(dv_ref.dtype)
 
 
-def fused_attention(queries, out_grad, key_tile, value_tile, live, block=256):
+def fused_attention(queries, out_grad, key_tile, value_tile, live, block=512):
     rows, width = queries.shape
     slots = key_tile.shape[0]
     row_block = pl.BlockSpec((block, width), lambda i: (i, 0))
@@ -135,16 +135,16 @@
         jnp.bfloat16
     )
     flag = jnp.ones((trace_rows, 128), jnp.bfloat16)
-    packed = jnp.concatenate([key_rows, value_rows, trace_feat, flag], axis=1)
-    outgoing = jnp.einsum(
-        "tjr,rd->tjd", picker, packed, preferred_element_type=jnp.float32
-    ).astype(jnp.bfloat16)
+    picker = picker.reshape(tile_count * capacity, trace_rows)
+    packed = jnp.concatenate([key_rows, value_rows, flag], axis=1)
+    outgoing = jnp.dot(picker, packed, preferred_element_type=jnp.float32).astype(jnp.bfloat16)
+    feat_out = jnp.dot(picker, trace_feat, preferred_element_type=jnp.float32).astype(jnp.bfloat16)
     arrived = send_slots(outgoing)
-    arrived = arrived.reshape(tile_count * capacity, packed.shape[1])
+    arrived, feat_out = lax.optimization_barrier((arrived, feat_out))
+    feat_tile = send_slots(feat_out)
     key_tile = arrived[:, :model_width]
     value_tile = arrived[:, model_width : 2 * model_width]
-    feat_tile = arrived[:, 2 * model_width : 3 * model_width]
-    live_slots = arrived[:, 3 * model_width] > 0.5
+    live_slots = arrived[:, 2 * model_width] > 0.5
     grad_grid, key_grad, value_grad, part_output, part_query = tile_grad(
         grid_feat, cotangent, query_weight, output_weight, key_tile, value_tile, live_slots
     )
@@ -157,9 +157,8 @@
     slot_trace = slot_trace + jnp.dot(
         value_grad, value_weight.T, preferred_element_type=jnp.float32
     )
-    slot_trace = slot_trace.astype(jnp.bfloat16).reshape(tile_count, capacity, model_width)
-    returned = send_back(slot_trace)
-    grad_trace = jnp.einsum("tjr,tje->re", picker, returned, preferred_element_type=jnp.float32)
+    returned = send_back(slot_trace.astype(jnp.bfloat16))
+    grad_trace = jnp.dot(picker.T, returned, preferred_element_type=jnp.float32)
     return (grad_grid, grad_trace, grad_query, grad_key, grad_value, grad_output)
 
 

time: 306 us -> 287 us (0.938)
  Pallas kernels: 67.5 us -> 43.9 us
  starting transfers between devices: 16.6 us -> 27.3 us
  waiting for transfers between devices: 161 us -> 154 us
    pallas_call x1, Pallas kernels: 67.5 us -> 43.9 us  [fused_attention(): pl.pallas_call(attention_kernel, grid=(rows // block,), in_specs=[row_blo...]
    all_to_all x1 -> x2, waiting for transfers between devices: 20.4 us -> 12.8 us  [send_slots(): lax.all_to_all(outgoing, ('inline', 'crosslin'), split_axis=0, concat_axi...]
    all_to_all x0 -> x5, local copies, waits for them, and re-layouts: none -> 5.45 us  [the longest x4 4.52 us: send_slots(): lax.all_to_all(outgoing, ('inline', 'crosslin'), split_axis=0, concat_axi...]
    all_to_all x1 -> x2, starting transfers between devices: 11.9 us -> 17.2 us  [send_slots(): lax.all_to_all(outgoing, ('inline', 'crosslin'), split_axis=0, concat_axi...]
    all_to_all x1, starting transfers between devices: 4.67 us -> 9.89 us  [send_back(): lax.all_to_all(returned, ('inline', 'crosslin'), split_axis=0, concat_axi...]
    reshape x2 -> x0, local copies, waits for them, and re-layouts: 4.74 us -> none  [the longest x1 3.82 us: on_device(): arrived = arrived.reshape(tile_count * capacity, packed.shape[1])]
  transfers between devices with their start and end apart: 3 -> 4, of which waited for: 3 -> 3; matrix products, arithmetic and copies ran while one was open for 4% -> 7% of each run, Pallas kernels for 0% -> 15%
where the time goes in v3:
time: 287 us; the launch traced here: 286 us
  waiting for transfers between devices  154 us (54%)
  Pallas kernels  43.9 us (15%)
  matrix products  28 us (10%)
  starting transfers between devices  27.3 us (10%)
  local copies, waits for them, and re-layouts  16.1 us (6%)
  between operations  14.3 us (5%)
  other arithmetic  3.03 us (1%)
    psum x1, waiting for transfers between devices, on_device(): lax.psum((part_query, part_key, part_value, part_output), ('inline', 'cro...  131 us
    pallas_call x1, Pallas kernels, fused_attention(): pl.pallas_call(attention_kernel, grid=(rows // block,), in_specs=[row_blo...  43.9 us
    all_to_all x2, starting transfers between devices, send_slots(): lax.all_to_all(outgoing, ('inline', 'crosslin'), split_axis=0, concat_axi...  17.2 us
    all_to_all x2, waiting for transfers between devices, send_slots(): lax.all_to_all(outgoing, ('inline', 'crosslin'), split_axis=0, concat_axi...  12.8 us
    all_to_all x1, waiting for transfers between devices, send_back(): lax.all_to_all(returned, ('inline', 'crosslin'), split_axis=0, concat_axi...  10.1 us
    all_to_all x1, starting transfers between devices, send_back(): lax.all_to_all(returned, ('inline', 'crosslin'), split_axis=0, concat_axi...  9.89 us
    unnamed x30, local copies, waits for them, and re-layouts  7.98 us
  transfers between devices with their start and end apart: 4, of which 3 were waited for; matrix products, arithmetic and copies ran while one was open for 7% of the time, Pallas kernels for 15%

profile of v3, /device:TPU:1, one launch (start us, length us, event | category | flops | bytes accessed | tf_op | source)
XLA Modules:
  0.0 286.4 jit_solution(8627522568504023718)
XLA Ops:
  7.2 0.0 copy-start
  7.2 0.9 fusion.9
  8.1 0.1 copy.29
  8.3 0.2 reduce_window_sum.11
  8.4 0.1 copy.30
  8.6 0.1 eq.43
  8.7 1.3 convolution_convert_fusion.6
  10.0 1.3 convolution_convert_fusion.5
  11.4 0.1 and.13
  11.5 0.1 compare_and_fusion
  11.7 0.5 convolution_convert_fusion.3
  12.1 0.0 copy-start.5
  12.1 1.2 all_to_all.22
  13.3 11.5 %all-to-all-start = ((bf16[128,4,1152]{2,1,0:T(4,128)(2,1)}), bf16[128,4,1152]{2,1,0:T(4,128)(2,1)S(1)}, u32[]{:S(2)}, u32[]{:S(2)}) async-start(bf16[128,4,1152]{2,1,0:T(4,128)(2,1)} %all_to_all.22), calls=%async_computation | async-start | bytes 2359296 | tf_op jit(solution)/shard_map/all_to_all | solution.py:102
  24.9 1.1 convolution_convert_fusion.4
  25.9 3.8 %convolution_convert_fusion.1.g_ref = bf16[2048,512]{1,0:T(8,128)(2,1)} fusion(bf16[2048,512]{1,0:T(8,128)(2,1)S(1)} %copy-done, bf16[512,512]{1,0:T(8,128)(2,1)} %param.15), kind=kOutput, calls=%fused_computation.1 | convolution fusion | flops 1074790400 | bytes 4718592 | tf_op jit(solution)/shard_map/dot_general | solution.py:87
  29.8 2.6 convolution_convert_fusion.2.q_ref
  32.3 12.8 %all-to-all-done = bf16[128,4,1152]{2,1,0:T(4,128)(2,1)S(1)} async-done(((bf16[128,4,1152]{2,1,0:T(4,128)(2,1)}), bf16[128,4,1152]{2,1,0:T(4,128)(2,1)S(1)}, u32[]{:S(2)}, u32[]{:S(2)}) %all-to-all-start) | async-done | bytes 1179680 | tf_op jit(solution)/shard_map/all_to_all | solution.py:102
  45.1 1.2 all_to_all.24
  46.3 1.7 convert_reduce_fusion
  48.0 2.2 fusion.11
  50.2 0.9 all_to_all.27
  51.1 5.7 %all-to-all-start.2 = ((bf16[128,4,512]{2,1,0:T(4,128)(2,1)}), bf16[128,4,512]{2,1,0:T(4,128)(2,1)}, u32[]{:S(2)}, u32[]{:S(2)}) async-start(bf16[128,4,512]{2,1,0:T(4,128)(2,1)} %all_to_all.27), calls=%async_computation.2 | async-start | bytes 1048576 | tf_op jit(solution)/shard_map/all_to_all | solution.py:102
  56.9 0.2 all-reduce.3.cloned.1.call-start
  57.1 43.9 %shard_map.127 = (bf16[2048,512]{1,0:T(8,128)(2,1)}, bf16[2048,512]{1,0:T(8,128)(2,1)}, bf16[512,512]{1,0:T(8,128)(2,1)}, bf16[512,512]{1,0:T(8,128)(2,1)}) custom-call(bf16[2048,512]{1,0:T(8,128)(2,1)} %convolution_convert_fusion.2.q_ref, bf16[2048,512]{1,0:T(8,128)(2,1)} %convolution_convert_fusion.1.g_ref, bf16[512,512]{1,0:T(8,128)(2,1)} %get-tuple-element.47.k_ref, ...), custom_call_target="tpu_custom_call" | custom-call | tf_op jit(solution)/shard_map/pallas_call | solution.py:67
  101.0 0.0 copy-start.9
  101.0 4.0 %fusion.15 = f32[512,512]{1,0:T(8,128)} fusion(bf16[2048,512]{1,0:T(8,128)(2,1)} %get-tuple-element.17, bf16[2048,512]{1,0:T(8,128)(2,1)S(1)} %copy-done), kind=kOutput, calls=%fused_computation.30 | convolution fusion | flops 1073741824 | bytes 5242880 | tf_op jit(solution)/shard_map/dot_general | solution.py:93
  105.0 2.2 convolution_bitcast_fusion
  107.2 0.0 all-to-all-done.2
  107.2 1.2 all_to_all.29
  108.4 2.5 fusion.13
  110.9 1.4 fusion.14
  112.4 0.0 all-reduce.3.cloned.1.call-update
  112.4 1.0 copy-done.4
  113.4 1.6 fusion.12
  115.0 0.5 fusion
  115.5 0.0 copy-start.12
  115.5 0.9 all_to_all.25
  116.4 9.9 %all-to-all-start.1 = ((bf16[128,4,512]{2,1,0:T(4,128)(2,1)}), bf16[128,4,512]{2,1,0:T(4,128)(2,1)S(1)}, u32[]{:S(2)}, u32[]{:S(2)}) async-start(bf16[128,4,512]{2,1,0:T(4,128)(2,1)} %all_to_all.25), calls=%async_computation.1 | async-start | bytes 1048576 | tf_op jit(solution)/shard_map/all_to_all | solution.py:109
  126.3 0.1 fusion.6
  126.4 4.3 %convolution_convert_fusion = bf16[2048,512]{1,0:T(8,128)(2,1)} fusion(bf16[2048,512]{1,0:T(8,128)(2,1)} %get-tuple-element.13, bf16[512,512]{1,0:T(8,128)(2,1)S(1)} %copy-done.12), kind=kOutput, calls=%fused_computation | convolution fusion | flops 1074790400 | bytes 4718592 | tf_op jit(solution)/shard_map/dot_general | solution.py:94
  130.7 10.1 %all-to-all-done.1 = bf16[128,4,512]{2,1,0:T(4,128)(2,1)S(1)} async-done(((bf16[128,4,512]{2,1,0:T(4,128)(2,1)}), bf16[128,4,512]{2,1,0:T(4,128)(2,1)S(1)}, u32[]{:S(2)}, u32[]{:S(2)}) %all-to-all-start.1) | async-done | bytes 524320 | tf_op jit(solution)/shard_map/all_to_all | solution.py:109
  140.8 1.0 convolution_bitcast_fusion.1
  141.8 130.9 %all-reduce.3.cloned.1.call-done = (f32[512,512]{0,1:T(8,128)}, f32[512,512]{1,0:T(8,128)}, f32[512,512]{1,0:T(8,128)}, f32[512,512]{1,0:T(8,128)}) async-done(((f32[512,512]{0,1:T(8,128)}, f32[512,512]{1,0:T(8,128)}, f32[512,512]{1,0:T(8,128)}, f32[512,512]{1,0:T(8,128)}), (f32[512,512]{0,1:T(8,128)}, f32[512,512]{1,0:T(8,128)}, f32[512,512]{1,0:T(8,128)}, ...) | async-done | bytes 4194320 | tf_op jit(solution)/shard_map/psum | solution.py:153
  272.7 2.6 copy.33
  275.3 2.4 copy.45
  277.6 1.0 copy.46
  278.6 1.0 copy.47
  (27 shorter events, 0.1 us)
Async XLA Ops:
  7.2 18.8 %copy-start = (bf16[2048,512]{1,0:T(8,128)(2,1)S(1)}, bf16[2048,512]{1,0:T(8,128)(2,1)}, u32[]{:S(2)}) copy-start(bf16[2048,512]{1,0:T(8,128)(2,1)} %param.9) | copy-start | bytes 6291460
  12.1 12.7 %copy-start.5 = (bf16[128,512]{1,0:T(8,128)(2,1)S(1)}, bf16[128,512]{1,0:T(8,128)(2,1)}, u32[]{:S(2)}) copy-start(bf16[128,512]{1,0:T(8,128)(2,1)} %param.10) | copy-start | bytes 393220
  13.3 31.8 %all-to-all-start = ((bf16[128,4,1152]{2,1,0:T(4,128)(2,1)}), bf16[128,4,1152]{2,1,0:T(4,128)(2,1)S(1)}, u32[]{:S(2)}, u32[]{:S(2)}) async-start(bf16[128,4,1152]{2,1,0:T(4,128)(2,1)} %all_to_all.22), calls=%async_computation | async-start | bytes 2359296 | tf_op jit(solution)/shard_map/all_to_all | solution.py:102
  25.9 3.8 %copy-start.8 = (bf16[2048,512]{1,0:T(8,128)(2,1)S(1)}, bf16[2048,512]{1,0:T(8,128)(2,1)}, u32[]{:S(2)}) copy-start(bf16[2048,512]{1,0:T(8,128)(2,1)} %param.8) | copy-start | bytes 6291460
  25.9 3.8 %copy-start.11 = (bf16[512,512]{1,0:T(8,128)(2,1)S(1)}, bf16[512,512]{1,0:T(8,128)(2,1)}, u32[]{:S(2)}) copy-start(bf16[512,512]{1,0:T(8,128)(2,1)} %param.12) | copy-start | bytes 1572868
  46.3 3.9 %copy-start.3 = (bf16[512,512]{1,0:T(8,128)(2,1)S(1)}, bf16[512,512]{1,0:T(8,128)(2,1)}, u32[]{:S(2)}) copy-start(bf16[512,512]{1,0:T(8,128)(2,1)} %convolution_convert_fusion.4) | copy-start | bytes 1572868
  51.1 56.1 %all-to-all-start.2 = ((bf16[128,4,512]{2,1,0:T(4,128)(2,1)}), bf16[128,4,512]{2,1,0:T(4,128)(2,1)}, u32[]{:S(2)}, u32[]{:S(2)}) async-start(bf16[128,4,512]{2,1,0:T(4,128)(2,1)} %all_to_all.27), calls=%async_computation.2 | async-start | bytes 1048576 | tf_op jit(solution)/shard_map/all_to_all | solution.py:102
  56.9 215.8 %all-reduce.3.cloned.1.call-start = ((), (), s32[]{:S(2)}) async-start(), calls=%async_computation.3 | async-start | bytes 8388608 | tf_op jit(solution)/shard_map/psum | solution.py:153
  101.0 4.0 %copy-start.9 = (bf16[2048,512]{1,0:T(8,128)(2,1)S(1)}, bf16[2048,512]{1,0:T(8,128)(2,1)}, u32[]{:S(2)}) copy-start(bf16[2048,512]{1,0:T(8,128)(2,1)} %param.8) | copy-start | bytes 6291460
  101.0 4.0 %copy-start.10 = (bf16[2048,512]{1,0:T(8,128)(2,1)S(1)}, bf16[2048,512]{1,0:T(8,128)(2,1)}, u32[]{:S(2)}) copy-start(bf16[2048,512]{1,0:T(8,128)(2,1)} %get-tuple-element.13) | copy-start | bytes 6291460
  107.2 3.7 %copy-start.2 = (bf16[512,512]{1,0:T(8,128)(2,1)S(1)}, bf16[512,512]{1,0:T(8,128)(2,1)}, u32[]{:S(2)}) copy-start(bf16[512,512]{1,0:T(8,128)(2,1)} %get-tuple-element.15) | copy-start | bytes 1572868
  112.4 1.0 copy-start.4
  113.4 1.6 copy-start.1
  115.5 11.0 %copy-start.12 = (bf16[512,512]{1,0:T(8,128)(2,1)S(1)}, bf16[512,512]{1,0:T(8,128)(2,1)}, u32[]{:S(2)}) copy-start(bf16[512,512]{1,0:T(8,128)(2,1)} %param.12) | copy-start | bytes 1572868
  116.4 24.4 %all-to-all-start.1 = ((bf16[128,4,512]{2,1,0:T(4,128)(2,1)}), bf16[128,4,512]{2,1,0:T(4,128)(2,1)S(1)}, u32[]{:S(2)}, u32[]{:S(2)}) async-start(bf16[128,4,512]{2,1,0:T(4,128)(2,1)} %all_to_all.25), calls=%async_computation.1 | async-start | bytes 1048576 | tf_op jit(solution)/shard_map/all_to_all | solution.py:109
  272.7 5.0 %copy-start.7 = (f32[512,512]{1,0:T(8,128)S(1)}, f32[512,512]{1,0:T(8,128)}, u32[]{:S(2)}) copy-start(f32[512,512]{1,0:T(8,128)} %get-tuple-element.52) | copy-start | bytes 3145732
  275.3 3.3 %copy-start.6 = (f32[512,512]{1,0:T(8,128)S(1)}, f32[512,512]{1,0:T(8,128)}, u32[]{:S(2)}) copy-start(f32[512,512]{1,0:T(8,128)} %get-tuple-element.53) | copy-start | bytes 3145732
Sparse Core Ops, SparseCore 0:
  112.5 160.1 all-reduce.2

commit v4 on v3

--- a/solution.py
+++ b/solution.py
@@ -112,6 +112,15 @@
     return result_rows
 
 
+def sum_over_devices(parts):
+    count = lax.axis_size("inline") * lax.axis_size("crosslin")
+    stacked = jnp.stack(parts)
+    pieces = stacked.reshape(count, stacked.size // (count * stacked.shape[-1]), stacked.shape[-1])
+    mine = send_slots(pieces).sum(axis=0, keepdims=True)
+    gathered = send_slots(jnp.broadcast_to(mine, pieces.shape)).reshape(stacked.shape)
+    return tuple(gathered[i] for i in range(len(parts)))
+
+
 def on_device(
     grid_feat,
     cotangent,
@@ -150,8 +159,8 @@
     )
     part_key = jnp.dot(feat_tile.T, key_grad, preferred_element_type=jnp.float32)
     part_value = jnp.dot(feat_tile.T, value_grad, preferred_element_type=jnp.float32)
-    grad_query, grad_key, grad_value, grad_output = lax.psum(
-        (part_query, part_key, part_value, part_output), ("inline", "crosslin")
+    grad_query, grad_key, grad_value, grad_output = sum_over_devices(
+        (part_query, part_key, part_value, part_output)
     )
     slot_trace = jnp.dot(key_grad, key_weight.T, preferred_element_type=jnp.float32)
     slot_trace = slot_trace + jnp.dot(

time: 287 us -> 254 us (0.89)
  waiting for transfers between devices: 154 us -> 121 us
  between operations: 14.3 us -> 0.94 us
  starting transfers between devices: 27.3 us -> 37.6 us
  other arithmetic: 3.03 us -> 7.9 us
    psum x1 -> x0, waiting for transfers between devices: 131 us -> none  [on_device(): lax.psum((part_query, part_key, part_value, part_output), ('inline', 'cro...]
    all_to_all x2 -> x4, waiting for transfers between devices: 12.8 us -> 110 us  [send_slots(): lax.all_to_all(outgoing, ('inline', 'crosslin'), split_axis=0, concat_axi...]
    all_to_all x2 -> x4, starting transfers between devices: 17.2 us -> 33.3 us  [send_slots(): lax.all_to_all(outgoing, ('inline', 'crosslin'), split_axis=0, concat_axi...]
    unnamed x30 -> x26, local copies, waits for them, and re-layouts: 7.98 us -> 0.07 us
    all_to_all x1, starting transfers between devices: 9.89 us -> 4.25 us  [send_back(): lax.all_to_all(returned, ('inline', 'crosslin'), split_axis=0, concat_axi...]
    slice x0 -> x1, local copies, waits for them, and re-layouts: none -> 4.52 us  [sum_over_devices(): return tuple((gathered[i] for i in range(len(parts))))]
  transfers between devices with their start and end apart: 4 -> 5, of which waited for: 3 -> 4; matrix products, arithmetic and copies ran while one was open for 7% -> 9% of each run, Pallas kernels for 15% -> 17%
where the time goes in v4:
time: 254 us; the launch traced here: 253 us
  waiting for transfers between devices  121 us (48%)
  Pallas kernels  43.9 us (17%)
  starting transfers between devices  37.6 us (15%)
  matrix products  26.2 us (10%)
  local copies, waits for them, and re-layouts  15.2 us (6%)
  other arithmetic  7.9 us (3%)
    all_to_all x4, waiting for transfers between devices, send_slots(): lax.all_to_all(outgoing, ('inline', 'crosslin'), split_axis=0, concat_axi...  110 us
    pallas_call x1, Pallas kernels, fused_attention(): pl.pallas_call(attention_kernel, grid=(rows // block,), in_specs=[row_blo...  43.9 us
    all_to_all x4, starting transfers between devices, send_slots(): lax.all_to_all(outgoing, ('inline', 'crosslin'), split_axis=0, concat_axi...  33.3 us
    all_to_all x1, waiting for transfers between devices, send_back(): lax.all_to_all(returned, ('inline', 'crosslin'), split_axis=0, concat_axi...  11.2 us
  transfers between devices with their start and end apart: 5, of which 4 were waited for; matrix products, arithmetic and copies ran while one was open for 9% of the time, Pallas kernels for 17%

profile of v4, /device:TPU:1, one launch (start us, length us, event | category | flops | bytes accessed | tf_op | source)
XLA Modules:
  0.0 253.1 jit_solution(17532132483653643782)
XLA Ops:
  0.6 0.0 copy-start
  0.6 0.9 fusion.9
  1.6 0.1 copy.26
  1.7 0.2 reduce_window_sum.11
  1.9 0.1 copy.27
  2.0 0.1 eq.43
  2.1 1.3 convolution_convert_fusion.6
  3.5 1.3 convolution_convert_fusion.5
  4.9 0.1 and.13
  5.0 0.1 compare_and_fusion
  5.1 0.5 convolution_convert_fusion.3
  5.6 0.0 copy-start.5
  5.6 1.2 all_to_all.28
  6.8 11.5 %all-to-all-start = ((bf16[128,4,1152]{2,1,0:T(4,128)(2,1)}), bf16[128,4,1152]{2,1,0:T(4,128)(2,1)S(1)}, u32[]{:S(2)}, u32[]{:S(2)}) async-start(bf16[128,4,1152]{2,1,0:T(4,128)(2,1)} %all_to_all.28), calls=%async_computation | async-start | bytes 2359296 | tf_op jit(solution)/shard_map/all_to_all | solution.py:102
  18.3 1.1 convolution_convert_fusion.4
  19.4 3.8 %convolution_convert_fusion.1.g_ref = bf16[2048,512]{1,0:T(8,128)(2,1)} fusion(bf16[2048,512]{1,0:T(8,128)(2,1)S(1)} %copy-done, bf16[512,512]{1,0:T(8,128)(2,1)} %param.15), kind=kOutput, calls=%fused_computation.2 | convolution fusion | flops 1074790400 | bytes 4718592 | tf_op jit(solution)/shard_map/dot_general | solution.py:87
  23.2 2.6 %convolution_convert_fusion.2.q_ref = bf16[2048,512]{1,0:T(8,128)(2,1)} fusion(bf16[2048,512]{1,0:T(8,128)(2,1)S(1)} %copy-done.8, bf16[512,512]{1,0:T(8,128)(2,1)S(1)} %copy-done.11), kind=kOutput, calls=%fused_computation.3 | convolution fusion | flops 1074790400 | bytes 4718592 | tf_op jit(solution)/shard_map/dot_general | solution.py:84
  25.8 12.8 %all-to-all-done = bf16[128,4,1152]{2,1,0:T(4,128)(2,1)S(1)} async-done(((bf16[128,4,1152]{2,1,0:T(4,128)(2,1)}), bf16[128,4,1152]{2,1,0:T(4,128)(2,1)S(1)}, u32[]{:S(2)}, u32[]{:S(2)}) %all-to-all-start) | async-done | bytes 1179680 | tf_op jit(solution)/shard_map/all_to_all | solution.py:102
  38.6 1.2 all_to_all.30
  39.8 1.7 convert_reduce_fusion
  41.4 2.2 fusion.12
  43.6 0.9 all_to_all.33
  44.6 5.7 %all-to-all-start.2 = ((bf16[128,4,512]{2,1,0:T(4,128)(2,1)}), bf16[128,4,512]{2,1,0:T(4,128)(2,1)}, u32[]{:S(2)}, u32[]{:S(2)}) async-start(bf16[128,4,512]{2,1,0:T(4,128)(2,1)} %all_to_all.33), calls=%async_computation.2 | async-start | bytes 1048576 | tf_op jit(solution)/shard_map/all_to_all | solution.py:102
  50.3 43.9 %shard_map.127 = (bf16[2048,512]{1,0:T(8,128)(2,1)}, bf16[2048,512]{1,0:T(8,128)(2,1)}, bf16[512,512]{1,0:T(8,128)(2,1)}, bf16[512,512]{1,0:T(8,128)(2,1)}) custom-call(bf16[2048,512]{1,0:T(8,128)(2,1)} %convolution_convert_fusion.2.q_ref, bf16[2048,512]{1,0:T(8,128)(2,1)} %convolution_convert_fusion.1.g_ref, bf16[512,512]{1,0:T(8,128)(2,1)} %get-tuple-element.23.k_ref, ...), custom_call_target="tpu_custom_call" | custom-call | tf_op jit(solution)/shard_map/pallas_call | solution.py:67
  94.2 4.0 %convolution_bitcast_fusion = f32[1,512,512]{2,1,0:T(8,128)} fusion(bf16[2048,512]{1,0:T(8,128)(2,1)} %get-tuple-element.17, bf16[2048,512]{1,0:T(8,128)(2,1)S(1)} %copy-done), kind=kOutput, calls=%fused_computation.5 | convolution fusion | flops 1073741824 | bytes 5242880 | tf_op jit(solution)/shard_map/dot_general | solution.py:93
  98.2 2.3 convolution_bitcast_fusion.3
  100.4 1.2 all_to_all.35
  101.7 0.0 copy-start.6
  101.7 0.0 copy-start.7
  101.7 1.7 convolution_bitcast_fusion.2
  103.4 0.5 convolution_bitcast_fusion.1
  103.8 2.4 pad_maximum_fusion
  106.3 10.4 %all-to-all-start.3 = ((f32[128,16,512]{2,1,0:T(8,128)}), f32[128,16,512]{2,1,0:T(8,128)}, u32[]{:S(2)}, u32[]{:S(2)}) async-start(f32[128,16,512]{2,1,0:T(8,128)} %bitcast.48), calls=%async_computation.3 | async-start | bytes 8388608 | tf_op jit(solution)/shard_map/all_to_all | solution.py:102
  116.6 0.0 copy-start.1
  116.6 1.6 fusion.13
  118.2 0.5 fusion
  118.7 0.9 all_to_all.31
  119.6 49.8 %all-to-all-done.3 = f32[128,16,512]{2,1,0:T(8,128)} async-done(((f32[128,16,512]{2,1,0:T(8,128)}), f32[128,16,512]{2,1,0:T(8,128)}, u32[]{:S(2)}, u32[]{:S(2)}) %all-to-all-start.3) | async-done | bytes 4194336 | tf_op jit(solution)/shard_map/all_to_all | solution.py:102
  169.4 4.2 %all-to-all-start.1 = ((bf16[128,4,512]{2,1,0:T(4,128)(2,1)}), bf16[128,4,512]{2,1,0:T(4,128)(2,1)S(1)}, u32[]{:S(2)}, u32[]{:S(2)}) async-start(bf16[128,4,512]{2,1,0:T(4,128)(2,1)} %all_to_all.31), calls=%async_computation.1 | async-start | bytes 1048576 | tf_op jit(solution)/shard_map/all_to_all | solution.py:109
  173.7 2.5 reduce_sum.9
  176.2 11.2 %all-to-all-done.1 = bf16[128,4,512]{2,1,0:T(4,128)(2,1)S(1)} async-done(((bf16[128,4,512]{2,1,0:T(4,128)(2,1)}), bf16[128,4,512]{2,1,0:T(4,128)(2,1)S(1)}, u32[]{:S(2)}, u32[]{:S(2)}) %all-to-all-start.1) | async-done | bytes 524320 | tf_op jit(solution)/shard_map/all_to_all | solution.py:109
  187.3 2.5 broadcast_in_dim.5
  189.8 5.8 %all-to-all-start.4 = ((f32[128,16,512]{2,1,0:T(8,128)}), f32[128,16,512]{2,1,0:T(8,128)}, u32[]{:S(2)}, u32[]{:S(2)}) async-start(f32[128,16,512]{2,1,0:T(8,128)} %broadcast_in_dim.5), calls=%async_computation.4 | async-start | bytes 8388608 | tf_op jit(solution)/shard_map/all_to_all | solution.py:102
  195.6 0.1 fusion.6
  195.7 4.2 %convolution_convert_fusion = bf16[2048,512]{1,0:T(8,128)(2,1)} fusion(bf16[2048,512]{1,0:T(8,128)(2,1)} %get-tuple-element.13, bf16[512,512]{1,0:T(8,128)(2,1)S(1)} %copy-done.12), kind=kOutput, calls=%fused_computation.1 | convolution fusion | flops 1074790400 | bytes 4718592 | tf_op jit(solution)/shard_map/dot_general | solution.py:94
  199.9 1.0 convolution_bitcast_fusion.4
  200.9 47.6 %all-to-all-done.4 = f32[128,16,512]{2,1,0:T(8,128)} async-done(((f32[128,16,512]{2,1,0:T(8,128)}), f32[128,16,512]{2,1,0:T(8,128)}, u32[]{:S(2)}, u32[]{:S(2)}) %all-to-all-start.4) | async-done | bytes 4194336 | tf_op jit(solution)/shard_map/all_to_all | solution.py:102
  248.6 4.5 %fusion.11 = (f32[32,16,512]{2,1,0:T(8,128)}, f32[32,16,512]{2,1,0:T(8,128)}, f32[32,16,512]{2,1,0:T(8,128)}, f32[32,16,512]{2,1,0:T(8,128)}) fusion(f32[128,16,512]{2,1,0:T(8,128)} %all-to-all-done.4), kind=kLoop, calls=%fused_computation.30 | loop fusion | bytes 8388608 | tf_op jit(solution)/shard_map/slice | solution.py:121
  (28 shorter events, 0.1 us)
Async XLA Ops:
  0.6 18.8 %copy-start = (bf16[2048,512]{1,0:T(8,128)(2,1)S(1)}, bf16[2048,512]{1,0:T(8,128)(2,1)}, u32[]{:S(2)}) copy-start(bf16[2048,512]{1,0:T(8,128)(2,1)} %param.9) | copy-start | bytes 6291460
  5.6 12.7 %copy-start.5 = (bf16[128,512]{1,0:T(8,128)(2,1)S(1)}, bf16[128,512]{1,0:T(8,128)(2,1)}, u32[]{:S(2)}) copy-start(bf16[128,512]{1,0:T(8,128)(2,1)} %param.10) | copy-start | bytes 393220
  6.8 31.8 %all-to-all-start = ((bf16[128,4,1152]{2,1,0:T(4,128)(2,1)}), bf16[128,4,1152]{2,1,0:T(4,128)(2,1)S(1)}, u32[]{:S(2)}, u32[]{:S(2)}) async-start(bf16[128,4,1152]{2,1,0:T(4,128)(2,1)} %all_to_all.28), calls=%async_computation | async-start | bytes 2359296 | tf_op jit(solution)/shard_map/all_to_all | solution.py:102
  19.4 3.8 %copy-start.8 = (bf16[2048,512]{1,0:T(8,128)(2,1)S(1)}, bf16[2048,512]{1,0:T(8,128)(2,1)}, u32[]{:S(2)}) copy-start(bf16[2048,512]{1,0:T(8,128)(2,1)} %param.8) | copy-start | bytes 6291460
  19.4 3.8 %copy-start.11 = (bf16[512,512]{1,0:T(8,128)(2,1)S(1)}, bf16[512,512]{1,0:T(8,128)(2,1)}, u32[]{:S(2)}) copy-start(bf16[512,512]{1,0:T(8,128)(2,1)} %param.12) | copy-start | bytes 1572868
  39.7 3.9 %copy-start.3 = (bf16[512,512]{1,0:T(8,128)(2,1)S(1)}, bf16[512,512]{1,0:T(8,128)(2,1)}, u32[]{:S(2)}) copy-start(bf16[512,512]{1,0:T(8,128)(2,1)} %convolution_convert_fusion.4) | copy-start | bytes 1572868
  44.6 55.9 %all-to-all-start.2 = ((bf16[128,4,512]{2,1,0:T(4,128)(2,1)}), bf16[128,4,512]{2,1,0:T(4,128)(2,1)}, u32[]{:S(2)}, u32[]{:S(2)}) async-start(bf16[128,4,512]{2,1,0:T(4,128)(2,1)} %all_to_all.33), calls=%async_computation.2 | async-start | bytes 1048576 | tf_op jit(solution)/shard_map/all_to_all | solution.py:102
  94.2 4.0 %copy-start.9 = (bf16[2048,512]{1,0:T(8,128)(2,1)S(1)}, bf16[2048,512]{1,0:T(8,128)(2,1)}, u32[]{:S(2)}) copy-start(bf16[2048,512]{1,0:T(8,128)(2,1)} %param.8) | copy-start | bytes 6291460
  94.2 4.0 %copy-start.10 = (bf16[2048,512]{1,0:T(8,128)(2,1)S(1)}, bf16[2048,512]{1,0:T(8,128)(2,1)}, u32[]{:S(2)}) copy-start(bf16[2048,512]{1,0:T(8,128)(2,1)} %get-tuple-element.13) | copy-start | bytes 6291460
  100.4 2.9 %copy-start.2 = (bf16[512,512]{1,0:T(8,128)(2,1)S(1)}, bf16[512,512]{1,0:T(8,128)(2,1)}, u32[]{:S(2)}) copy-start(bf16[512,512]{1,0:T(8,128)(2,1)} %get-tuple-element.15) | copy-start | bytes 1572868
  101.7 2.2 copy-start.6
  101.7 2.2 copy-start.7
  106.3 10.4 %copy-start.4 = (bf16[512,512]{1,0:T(8,128)(2,1)S(1)}, bf16[512,512]{1,0:T(8,128)(2,1)}, u32[]{:S(2)}) copy-start(bf16[512,512]{1,0:T(8,128)(2,1)} %param.13) | copy-start | bytes 1572868
  106.3 63.2 %all-to-all-start.3 = ((f32[128,16,512]{2,1,0:T(8,128)}), f32[128,16,512]{2,1,0:T(8,128)}, u32[]{:S(2)}, u32[]{:S(2)}) async-start(f32[128,16,512]{2,1,0:T(8,128)} %bitcast.48), calls=%async_computation.3 | async-start | bytes 8388608 | tf_op jit(solution)/shard_map/all_to_all | solution.py:102
  116.6 1.6 copy-start.1
  169.4 17.9 %all-to-all-start.1 = ((bf16[128,4,512]{2,1,0:T(4,128)(2,1)}), bf16[128,4,512]{2,1,0:T(4,128)(2,1)S(1)}, u32[]{:S(2)}, u32[]{:S(2)}) async-start(bf16[128,4,512]{2,1,0:T(4,128)(2,1)} %all_to_all.31), calls=%async_computation.1 | async-start | bytes 1048576 | tf_op jit(solution)/shard_map/all_to_all | solution.py:109
  189.8 5.9 %copy-start.12 = (bf16[512,512]{1,0:T(8,128)(2,1)S(1)}, bf16[512,512]{1,0:T(8,128)(2,1)}, u32[]{:S(2)}) copy-start(bf16[512,512]{1,0:T(8,128)(2,1)} %param.12) | copy-start | bytes 1572868
  189.8 58.7 %all-to-all-start.4 = ((f32[128,16,512]{2,1,0:T(8,128)}), f32[128,16,512]{2,1,0:T(8,128)}, u32[]{:S(2)}, u32[]{:S(2)}) async-start(f32[128,16,512]{2,1,0:T(8,128)} %broadcast_in_dim.5), calls=%async_computation.4 | async-start | bytes 8388608 | tf_op jit(solution)/shard_map/all_to_all | solution.py:102

commit v5 on v4

--- a/solution.py
+++ b/solution.py
@@ -80,24 +80,6 @@
     )(queries, out_grad, key_tile, value_tile, live.astype(jnp.float32).reshape(1, slots))
 
 
-def tile_grad(grid_rows, upstream, query_weight, output_weight, key_tile, value_tile, live_slots):
-    queries = jnp.dot(grid_rows, query_weight, preferred_element_type=jnp.float32).astype(
-        jnp.bfloat16
-    )
-    out_grad = jnp.dot(upstream, output_weight.T, preferred_element_type=jnp.float32).astype(
-        jnp.bfloat16
-    )
-    attn_out, query_grad, key_grad, value_grad = fused_attention(
-        queries, out_grad, key_tile, value_tile, live_slots
-    )
-    part_output = jnp.dot(attn_out.T, upstream, preferred_element_type=jnp.float32)
-    grad_grid = jnp.dot(query_grad, query_weight.T, preferred_element_type=jnp.float32).astype(
-        jnp.bfloat16
-    )
-    part_query = jnp.dot(grid_rows.T, query_grad, preferred_element_type=jnp.float32)
-    return (grad_grid, key_grad, value_grad, part_output, part_query)
-
-
 def send_slots(outgoing):
     arrived = lax.all_to_all(
         outgoing, ("inline", "crosslin"), split_axis=0, concat_axis=0, tiled=True
@@ -136,37 +118,44 @@
     model_width = trace_feat.shape[1]
     capacity = 2 * trace_rows * TOP // tile_count
     chosen, counts = slot_table(trace_dest, tile_count, capacity)
-    picker = chosen.astype(jnp.bfloat16)
-    key_rows = jnp.dot(trace_feat, key_weight, preferred_element_type=jnp.float32).astype(
+    picker = chosen.astype(jnp.bfloat16).reshape(tile_count * capacity, trace_rows)
+    flag = jnp.ones((trace_rows, 128), jnp.bfloat16)
+    packed = jnp.concatenate([trace_feat, flag], axis=1)
+    outgoing = jnp.dot(picker, packed, preferred_element_type=jnp.float32).astype(jnp.bfloat16)
+    arrived = send_slots(outgoing)
+    feat_tile = arrived[:, :model_width]
+    live_slots = arrived[:, model_width] > 0.5
+    key_tile = jnp.dot(feat_tile, key_weight, preferred_element_type=jnp.float32).astype(
         jnp.bfloat16
     )
-    value_rows = jnp.dot(trace_feat, value_weight, preferred_element_type=jnp.float32).astype(
+    value_tile = jnp.dot(feat_tile, value_weight, preferred_element_type=jnp.float32).astype(
         jnp.bfloat16
     )
-    flag = jnp.ones((trace_rows, 128), jnp.bfloat16)
-    picker = picker.reshape(tile_count * capacity, trace_rows)
-    packed = jnp.concatenate([key_rows, value_rows, flag], axis=1)
-    outgoing = jnp.dot(picker, packed, preferred_element_type=jnp.float32).astype(jnp.bfloat16)
-    feat_out = jnp.dot(picker, trace_feat, preferred_element_type=jnp.float32).astype(jnp.bfloat16)
-    arrived = send_slots(outgoing)
-    arrived, feat_out = lax.optimization_barrier((arrived, feat_out))
-    feat_tile = send_slots(feat_out)
-    key_tile = arrived[:, :model_width]
-    value_tile = arrived[:, model_width : 2 * model_width]
-    live_slots = arrived[:, 2 * model_width] > 0.5
-    grad_grid, key_grad, value_grad, part_output, part_query = tile_grad(
-        grid_feat, cotangent, query_weight, output_weight, key_tile, value_tile, live_slots
+    queries = jnp.dot(grid_feat, query_weight, preferred_element_type=jnp.float32).astype(
+        jnp.bfloat16
     )
-    part_key = jnp.dot(feat_tile.T, key_grad, preferred_element_type=jnp.float32)
-    part_value = jnp.dot(feat_tile.T, value_grad, preferred_element_type=jnp.float32)
-    grad_query, grad_key, grad_value, grad_output = sum_over_devices(
-        (part_query, part_key, part_value, part_output)
+    out_grad = jnp.dot(cotangent, output_weight.T, preferred_element_type=jnp.float32).astype(
+        jnp.bfloat16
+    )
+    attn_out, query_grad, key_grad, value_grad = fused_attention(
+        queries, out_grad, key_tile, value_tile, live_slots
     )
     slot_trace = jnp.dot(key_grad, key_weight.T, preferred_element_type=jnp.float32)
     slot_trace = slot_trace + jnp.dot(
         value_grad, value_weight.T, preferred_element_type=jnp.float32
     )
     returned = send_back(slot_trace.astype(jnp.bfloat16))
+    part_output = jnp.dot(attn_out.T, cotangent, preferred_element_type=jnp.float32)
+    part_query = jnp.dot(grid_feat.T, query_grad, preferred_element_type=jnp.float32)
+    part_key = jnp.dot(feat_tile.T, key_grad, preferred_element_type=jnp.float32)
+    part_value = jnp.dot(feat_tile.T, value_grad, preferred_element_type=jnp.float32)
+    returned, parts = lax.optimization_barrier(
+        (returned, (part_query, part_key, part_value, part_output))
+    )
+    grad_query, grad_key, grad_value, grad_output = sum_over_devices(parts)
+    grad_grid = jnp.dot(query_grad, query_weight.T, preferred_element_type=jnp.float32).astype(
+        jnp.bfloat16
+    )
     grad_trace = jnp.dot(picker.T, returned, preferred_element_type=jnp.float32)
     return (grad_grid, grad_trace, grad_query, grad_key, grad_value, grad_output)
 

time: 254 us -> 252 us (level)
  blocking collectives: 0 us -> 58.8 us
  waiting for transfers between devices: 121 us -> 62.8 us
  starting transfers between devices: 37.6 us -> 22.7 us
  local copies, waits for them, and re-layouts: 15.2 us -> 23.3 us
  matrix products: 26.2 us -> 29.7 us
    all_to_all x0 -> x1, blocking collectives: none -> 58.8 us  [send_slots(): lax.all_to_all(outgoing, ('inline', 'crosslin'), split_axis=0, concat_axi...]
    all_to_all x4 -> x2, waiting for transfers between devices: 110 us -> 56.1 us  [send_slots(): lax.all_to_all(outgoing, ('inline', 'crosslin'), split_axis=0, concat_axi...]
    all_to_all x4 -> x2, starting transfers between devices: 33.3 us -> 17 us  [send_slots(): lax.all_to_all(outgoing, ('inline', 'crosslin'), split_axis=0, concat_axi...]
    optimization_barrier x0 -> x3, local copies, waits for them, and re-layouts: none -> 6.46 us  [on_device(): lax.optimization_barrier((returned, (part_query, part_key, part_value, pa...]
    another operation x0 -> x1, local copies, waits for them, and re-layouts: none -> 5.24 us  [sum_over_devices(): stacked = jnp.stack(parts)]
    all_to_all x1, waiting for transfers between devices: 11.2 us -> 6.73 us  [send_back(): lax.all_to_all(returned, ('inline', 'crosslin'), split_axis=0, concat_axi...]
    all_to_all x4 -> x2, local copies, waits for them, and re-layouts: 4.48 us -> 1.14 us  [send_slots(): lax.all_to_all(outgoing, ('inline', 'crosslin'), split_axis=0, concat_axi...]
    dot_general x8 -> x7, matrix products: 20.6 us -> 21.3 us  [the longest x1 4.25 us: on_device(): jnp.dot(query_grad, query_weight.T, preferred_element_type=jnp.float32)]
  transfers between devices with their start and end apart: 5 -> 3, of which waited for: 4 -> 3; matrix products, arithmetic and copies ran while one was open for 9% -> 7% of each run, Pallas kernels for 17% -> 0%
where the time goes in v5:
time: 252 us; the launch traced here: 251 us
  waiting for transfers between devices  62.8 us (25%)
  blocking collectives  58.8 us (23%)
  Pallas kernels  43.8 us (17%)
  matrix products  29.7 us (12%)
  local copies, waits for them, and re-layouts  23.3 us (9%)
  starting transfers between devices  22.7 us (9%)
  other arithmetic  8.79 us (3%)
    all_to_all x1, blocking collectives, send_slots(): lax.all_to_all(outgoing, ('inline', 'crosslin'), split_axis=0, concat_axi...  58.8 us
    all_to_all x2, waiting for transfers between devices, send_slots(): lax.all_to_all(outgoing, ('inline', 'crosslin'), split_axis=0, concat_axi...  56.1 us
    pallas_call x1, Pallas kernels, fused_attention(): pl.pallas_call(attention_kernel, grid=(rows // block,), in_specs=[row_blo...  43.8 us
    all_to_all x2, starting transfers between devices, send_slots(): lax.all_to_all(outgoing, ('inline', 'crosslin'), split_axis=0, concat_axi...  17 us
    all_to_all x1, waiting for transfers between devices, send_back(): lax.all_to_all(returned, ('inline', 'crosslin'), split_axis=0, concat_axi...  6.73 us
    optimization_barrier x3, local copies, waits for them, and re-layouts, on_device(): lax.optimization_barrier((returned, (part_query, part_key, part_value, pa...  6.46 us
    all_to_all x1, starting transfers between devices, send_back(): lax.all_to_all(returned, ('inline', 'crosslin'), split_axis=0, concat_axi...  5.64 us
    another operation x1, local copies, waits for them, and re-layouts, sum_over_devices(): stacked = jnp.stack(parts)  5.24 us
  transfers between devices with their start and end apart: 3, of which 3 were waited for; matrix products, arithmetic and copies ran while one was open for 7% of the time, Pallas kernels for 0%

profile of v5, /device:TPU:1, one launch (start us, length us, event | category | flops | bytes accessed | tf_op | source)
XLA Modules:
  0.0 250.7 jit_solution(17544195004972316893)
XLA Ops:
  0.6 0.0 copy-start
  0.6 0.9 fusion.8
  1.6 0.1 copy.35
  1.7 0.2 reduce_window_sum.11
  1.9 0.1 copy.36
  2.0 0.1 eq.39
  2.1 0.1 and.11
  2.3 0.1 compare_and_fusion
  2.4 1.2 convolution_convert_fusion.3
  3.6 1.0 all_to_all.22
  4.6 11.5 %all-to-all-start = ((bf16[128,4,640]{2,1,0:T(4,128)(2,1)}), bf16[128,4,640]{2,1,0:T(4,128)(2,1)S(1)}, u32[]{:S(2)}, u32[]{:S(2)}) async-start(bf16[128,4,640]{2,1,0:T(4,128)(2,1)} %all_to_all.22), calls=%async_computation | async-start | bytes 1310720 | tf_op jit(solution)/shard_map/all_to_all | solution.py:84
  16.1 0.0 copy-start.8
  16.1 0.0 copy-start.11
  16.2 3.8 %convolution_convert_fusion.1.g_ref = bf16[2048,512]{1,0:T(8,128)(2,1)} fusion(bf16[2048,512]{1,0:T(8,128)(2,1)S(1)} %copy-done, bf16[512,512]{1,0:T(8,128)(2,1)} %param.15), kind=kOutput, calls=%fused_computation.2 | convolution fusion | flops 1074790400 | bytes 4718592 | tf_op jit(solution)/shard_map/dot_general | solution.py:137
  20.0 2.6 %convolution_convert_fusion.2.q_ref = bf16[2048,512]{1,0:T(8,128)(2,1)} fusion(bf16[2048,512]{1,0:T(8,128)(2,1)S(1)} %copy-done.8, bf16[512,512]{1,0:T(8,128)(2,1)S(1)} %copy-done.11), kind=kOutput, calls=%fused_computation.3 | convolution fusion | flops 1074790400 | bytes 4718592 | tf_op jit(solution)/shard_map/dot_general | solution.py:134
  22.6 8.4 %all-to-all-done = bf16[128,4,640]{2,1,0:T(4,128)(2,1)S(1)} async-done(((bf16[128,4,640]{2,1,0:T(4,128)(2,1)}), bf16[128,4,640]{2,1,0:T(4,128)(2,1)S(1)}, u32[]{:S(2)}, u32[]{:S(2)}) %all-to-all-start) | async-done | bytes 655392 | tf_op jit(solution)/shard_map/all_to_all | solution.py:84
  30.9 0.1 all_to_all.24
  31.1 0.7 convert_reduce_fusion
  31.8 2.3 convolution_convert_fusion.4.v_ref
  34.0 2.3 convolution_convert_fusion.5.k_ref
  36.3 43.8 %shard_map.127 = (bf16[2048,512]{1,0:T(8,128)(2,1)}, bf16[2048,512]{1,0:T(8,128)(2,1)}, bf16[512,512]{1,0:T(8,128)(2,1)}, bf16[512,512]{1,0:T(8,128)(2,1)}) custom-call(bf16[2048,512]{1,0:T(8,128)(2,1)} %convolution_convert_fusion.2.q_ref, bf16[2048,512]{1,0:T(8,128)(2,1)} %convolution_convert_fusion.1.g_ref, ...), custom_call_target="tpu_custom_call" | custom-call | tf_op jit(solution)/shard_map/pallas_call | solution.py:67
  80.2 0.0 copy-start.5
  80.2 0.0 copy-start.7
  80.2 2.6 %fusion.3 = f32[512,512]{1,0:T(8,128)} fusion(bf16[512,512]{1,0:T(8,128)(2,1)} %get-tuple-element.16, bf16[512,640]{1,0:T(8,128)(2,1)S(1)} %all_to_all.24), kind=kOutput, calls=%fused_computation.12 | convolution fusion | flops 268435456 | bytes 2097152 | tf_op jit(solution)/shard_map/dot_general | solution.py:150
  82.8 0.5 fusion.11
  83.3 0.0 copy-start.6
  83.3 2.2 fusion.12
  85.6 0.5 fusion
  86.1 0.9 all_to_all.25
  87.0 5.6 %all-to-all-start.1 = ((bf16[128,4,512]{2,1,0:T(4,128)(2,1)}), bf16[128,4,512]{2,1,0:T(4,128)(2,1)}, u32[]{:S(2)}, u32[]{:S(2)}) async-start(bf16[128,4,512]{2,1,0:T(4,128)(2,1)} %all_to_all.25), calls=%async_computation.1 | async-start | bytes 1048576 | tf_op jit(solution)/shard_map/all_to_all | solution.py:91
  92.6 0.0 copy-start.9
  92.6 2.6 %fusion.1 = f32[512,512]{1,0:T(8,128)} fusion(bf16[512,512]{1,0:T(8,128)(2,1)} %get-tuple-element.17, bf16[512,640]{1,0:T(8,128)(2,1)S(1)} %all_to_all.24), kind=kOutput, calls=%fused_computation.10 | convolution fusion | flops 268435456 | bytes 2097152 | tf_op jit(solution)/shard_map/dot_general | solution.py:151
  95.3 3.9 %convolution_bitcast_fusion = f32[512,512]{0,1:T(8,128)} fusion(bf16[2048,512]{1,0:T(8,128)(2,1)} %get-tuple-element.15, bf16[2048,512]{1,0:T(8,128)(2,1)S(1)} %copy-done.9), kind=kOutput, calls=%fused_computation.4 | convolution fusion | flops 1073741824 | bytes 5242880 | tf_op jit(solution)/shard_map/dot_general | solution.py:149
  99.2 6.7 %all-to-all-done.1 = bf16[128,4,512]{2,1,0:T(4,128)(2,1)} async-done(((bf16[128,4,512]{2,1,0:T(4,128)(2,1)}), bf16[128,4,512]{2,1,0:T(4,128)(2,1)}, u32[]{:S(2)}, u32[]{:S(2)}) %all-to-all-start.1) | async-done | bytes 524320 | tf_op jit(solution)/shard_map/all_to_all | solution.py:91
  105.9 2.0 all_to_all.27
  107.9 1.3 copy.37
  109.2 2.6 %copy.38 = f32[512,512]{0,1:T(8,128)} copy(f32[512,512]{1,0:T(8,128)} %fusion.1) | data formatting | bytes 2097152 | tf_op jit(solution)/shard_map/optimization_barrier | solution.py:152
  111.8 2.5 %copy.39 = f32[512,512]{0,1:T(8,128)} copy(f32[512,512]{1,0:T(8,128)} %fusion.12) | data formatting | bytes 2097152 | tf_op jit(solution)/shard_map/optimization_barrier | solution.py:152
  114.4 4.4 %pad_maximum_fusion = f32[4,512,512]{1,2,0:T(8,128)} fusion(f32[1,512,512]{1,2,0:T(8,128)} %bitcast.41, f32[1,512,512]{1,2,0:T(8,128)} %bitcast.40, f32[1,512,512]{1,2,0:T(8,128)S(1)} %bitcast.39, f32[1,512,512]{1,2,0:T(8,128)} %bitcast.47), kind=kLoop, calls=%fused_computation | loop fusion | flops 3145728 | bytes 8388608 | tf_op jit(solution)/shard_map/stack | solution.py:99
  118.7 5.2 %copy.40 = f32[4,512,512]{2,1,0:T(8,128)} copy(f32[4,512,512]{1,2,0:T(8,128)} %pad_maximum_fusion) | data formatting | bytes 8388608 | tf_op jit(solution)/shard_map/stack | solution.py:99
  124.0 58.8 %all_to_all.34 = f32[128,16,512]{2,1,0:T(8,128)} all-to-all(f32[128,16,512]{2,1,0:T(8,128)} %bitcast.38), channel_id=1, replica_groups=mesh['inline'=16,'crosslin'=8] {'inline','crosslin'}, dimensions={0} | all-to-all | bytes 8388608 | tf_op jit(solution)/shard_map/all_to_all | solution.py:84
  182.8 2.5 reduce_sum.9
  185.2 2.5 broadcast_in_dim.2
  187.8 5.5 %all-to-all-start.3 = ((f32[128,16,512]{2,1,0:T(8,128)}), f32[128,16,512]{2,1,0:T(8,128)}, u32[]{:S(2)}, u32[]{:S(2)}) async-start(f32[128,16,512]{2,1,0:T(8,128)} %broadcast_in_dim.2), calls=%async_computation.3 | async-start | bytes 8388608 | tf_op jit(solution)/shard_map/all_to_all | solution.py:84
  193.3 4.3 %convolution_convert_fusion = bf16[2048,512]{1,0:T(8,128)(2,1)} fusion(bf16[2048,512]{1,0:T(8,128)(2,1)} %get-tuple-element.15, bf16[512,512]{1,0:T(8,128)(2,1)S(1)} %copy-done.12), kind=kOutput, calls=%fused_computation.1 | convolution fusion | flops 1074790400 | bytes 4718592 | tf_op jit(solution)/shard_map/dot_general | solution.py:156
  197.6 1.0 fusion.13
  198.5 47.7 %all-to-all-done.3 = f32[128,16,512]{2,1,0:T(8,128)} async-done(((f32[128,16,512]{2,1,0:T(8,128)}), f32[128,16,512]{2,1,0:T(8,128)}, u32[]{:S(2)}, u32[]{:S(2)}) %all-to-all-start.3) | async-done | bytes 4194336 | tf_op jit(solution)/shard_map/all_to_all | solution.py:84
  246.2 4.5 %fusion.10 = (f32[32,16,512]{2,1,0:T(8,128)}, f32[32,16,512]{2,1,0:T(8,128)}, f32[32,16,512]{2,1,0:T(8,128)}, f32[32,16,512]{2,1,0:T(8,128)}) fusion(f32[128,16,512]{2,1,0:T(8,128)} %all-to-all-done.3), kind=kLoop, calls=%fused_computation.23 | loop fusion | bytes 8388608 | tf_op jit(solution)/shard_map/slice | solution.py:103
  (23 shorter events, 0.1 us)
Async XLA Ops:
  0.6 15.5 %copy-start = (bf16[2048,512]{1,0:T(8,128)(2,1)S(1)}, bf16[2048,512]{1,0:T(8,128)(2,1)}, u32[]{:S(2)}) copy-start(bf16[2048,512]{1,0:T(8,128)(2,1)} %param.9) | copy-start | bytes 6291460
  4.6 26.3 %all-to-all-start = ((bf16[128,4,640]{2,1,0:T(4,128)(2,1)}), bf16[128,4,640]{2,1,0:T(4,128)(2,1)S(1)}, u32[]{:S(2)}, u32[]{:S(2)}) async-start(bf16[128,4,640]{2,1,0:T(4,128)(2,1)} %all_to_all.22), calls=%async_computation | async-start | bytes 1310720 | tf_op jit(solution)/shard_map/all_to_all | solution.py:84
  16.1 3.8 %copy-start.8 = (bf16[2048,512]{1,0:T(8,128)(2,1)S(1)}, bf16[2048,512]{1,0:T(8,128)(2,1)}, u32[]{:S(2)}) copy-start(bf16[2048,512]{1,0:T(8,128)(2,1)} %param.8) | copy-start | bytes 6291460
  16.1 3.8 %copy-start.11 = (bf16[512,512]{1,0:T(8,128)(2,1)S(1)}, bf16[512,512]{1,0:T(8,128)(2,1)}, u32[]{:S(2)}) copy-start(bf16[512,512]{1,0:T(8,128)(2,1)} %param.12) | copy-start | bytes 1572868
  80.2 2.7 %copy-start.5 = (bf16[512,512]{1,0:T(8,128)(2,1)S(1)}, bf16[512,512]{1,0:T(8,128)(2,1)}, u32[]{:S(2)}) copy-start(bf16[512,512]{1,0:T(8,128)(2,1)} %get-tuple-element.16) | copy-start | bytes 1572868
  80.2 2.7 %copy-start.7 = (bf16[512,512]{1,0:T(8,128)(2,1)S(1)}, bf16[512,512]{1,0:T(8,128)(2,1)}, u32[]{:S(2)}) copy-start(bf16[512,512]{1,0:T(8,128)(2,1)} %param.13) | copy-start | bytes 1572868
  80.2 3.1 %copy-start.10 = (bf16[2048,512]{1,0:T(8,128)(2,1)S(1)}, bf16[2048,512]{1,0:T(8,128)(2,1)}, u32[]{:S(2)}) copy-start(bf16[2048,512]{1,0:T(8,128)(2,1)} %get-tuple-element.18) | copy-start | bytes 6291460
  83.3 2.3 copy-start.4
  83.3 2.3 copy-start.6
  87.0 18.9 %all-to-all-start.1 = ((bf16[128,4,512]{2,1,0:T(4,128)(2,1)}), bf16[128,4,512]{2,1,0:T(4,128)(2,1)}, u32[]{:S(2)}, u32[]{:S(2)}) async-start(bf16[128,4,512]{2,1,0:T(4,128)(2,1)} %all_to_all.25), calls=%async_computation.1 | async-start | bytes 1048576 | tf_op jit(solution)/shard_map/all_to_all | solution.py:91
  92.6 2.6 %copy-start.9 = (bf16[2048,512]{1,0:T(8,128)(2,1)S(1)}, bf16[2048,512]{1,0:T(8,128)(2,1)}, u32[]{:S(2)}) copy-start(bf16[2048,512]{1,0:T(8,128)(2,1)} %param.8) | copy-start | bytes 6291460
  95.3 12.6 %copy-start.1 = (f32[512,512]{1,0:T(8,128)S(1)}, f32[512,512]{1,0:T(8,128)}, u32[]{:S(2)}) copy-start(f32[512,512]{1,0:T(8,128)} %fusion.3) | copy-start | bytes 3145732
  109.2 5.2 %copy-start.2 = (f32[512,512]{0,1:T(8,128)S(1)}, f32[512,512]{0,1:T(8,128)}, u32[]{:S(2)}) copy-start(f32[512,512]{0,1:T(8,128)} %copy.37) | copy-start | bytes 3145732
  187.8 5.5 %copy-start.12 = (bf16[512,512]{1,0:T(8,128)(2,1)S(1)}, bf16[512,512]{1,0:T(8,128)(2,1)}, u32[]{:S(2)}) copy-start(bf16[512,512]{1,0:T(8,128)(2,1)} %param.12) | copy-start | bytes 1572868
  187.8 58.5 %all-to-all-start.3 = ((f32[128,16,512]{2,1,0:T(8,128)}), f32[128,16,512]{2,1,0:T(8,128)}, u32[]{:S(2)}, u32[]{:S(2)}) async-start(f32[128,16,512]{2,1,0:T(8,128)} %broadcast_in_dim.2), calls=%async_computation.3 | async-start | bytes 8388608 | tf_op jit(solution)/shard_map/all_to_all | solution.py:84
  193.3 4.3 %copy-start.3 = (bf16[512,512]{1,0:T(8,128)(2,1)S(1)}, bf16[512,512]{1,0:T(8,128)(2,1)}, u32[]{:S(2)}) copy-start(bf16[512,512]{1,0:T(8,128)(2,1)} %all_to_all.27) | copy-start | bytes 1572868

commit v6 on v5

--- a/solution.py
+++ b/solution.py
@@ -94,13 +94,26 @@
     return result_rows
 
 
+def as_tiles(part):
+    rows, cols = part.shape
+    return part.reshape(rows // 8, 8, cols // 128, 128).transpose(0, 2, 1, 3)
+
+
+def from_tiles(tiles, shape):
+    return tiles.reshape(shape[0] // 8, shape[1] // 128, 8, 128).transpose(0, 2, 1, 3).reshape(shape)
+
+
 def sum_over_devices(parts):
     count = lax.axis_size("inline") * lax.axis_size("crosslin")
-    stacked = jnp.stack(parts)
-    pieces = stacked.reshape(count, stacked.size // (count * stacked.shape[-1]), stacked.shape[-1])
+    tiled = [as_tiles(part).reshape(count, -1, 128) for part in parts]
+    depth = tiled[0].shape[1]
+    pieces = jnp.concatenate(tiled, axis=1)
     mine = send_slots(pieces).sum(axis=0, keepdims=True)
-    gathered = send_slots(jnp.broadcast_to(mine, pieces.shape)).reshape(stacked.shape)
-    return tuple(gathered[i] for i in range(len(parts)))
+    gathered = send_slots(jnp.broadcast_to(mine, pieces.shape))
+    return tuple(
+        from_tiles(gathered[:, i * depth : (i + 1) * depth], part.shape)
+        for i, part in enumerate(parts)
+    )
 
 
 def on_device(

time: 252 us -> 239 us (0.948)
  local copies, waits for them, and re-layouts: 23.3 us -> 13.9 us
    another operation x1 -> x0, local copies, waits for them, and re-layouts: 5.24 us -> none  [sum_over_devices(): stacked = jnp.stack(parts)]
    another operation x1 -> x0, other arithmetic: 4.38 us -> none  [sum_over_devices(): stacked = jnp.stack(parts)]
    optimization_barrier x3 -> x1, local copies, waits for them, and re-layouts: 6.46 us -> 2.53 us  [on_device(): lax.optimization_barrier((returned, (part_query, part_key, part_value, pa...]
    concatenate x0 -> x1, other arithmetic: none -> 2.52 us  [sum_over_devices(): pieces = jnp.concatenate(tiled, axis=1)]
  transfers between devices with their start and end apart: 3 -> 3, of which waited for: 3 -> 3; matrix products, arithmetic and copies ran while one was open for 7% -> 8% of each run, Pallas kernels for 0% -> 0%
where the time goes in v6:
time: 239 us
  waiting for transfers between devices  62.9 us (26%)
  blocking collectives  57.8 us (24%)
  Pallas kernels  43.9 us (18%)
  matrix products  29.6 us (12%)
  starting transfers between devices  22.7 us (9%)
  local copies, waits for them, and re-layouts  13.9 us (6%)
  other arithmetic  6.94 us (3%)
    all_to_all x1, blocking collectives, send_slots(): lax.all_to_all(outgoing, ('inline', 'crosslin'), split_axis=0, concat_axi...  57.8 us
    all_to_all x2, waiting for transfers between devices, send_slots(): lax.all_to_all(outgoing, ('inline', 'crosslin'), split_axis=0, concat_axi...  56.1 us
    pallas_call x1, Pallas kernels, fused_attention(): pl.pallas_call(attention_kernel, grid=(rows // block,), in_specs=[row_blo...  43.9 us
    all_to_all x2, starting transfers between devices, send_slots(): lax.all_to_all(outgoing, ('inline', 'crosslin'), split_axis=0, concat_axi...  17 us
    all_to_all x1, waiting for transfers between devices, send_back(): lax.all_to_all(returned, ('inline', 'crosslin'), split_axis=0, concat_axi...  6.82 us
    all_to_all x1, starting transfers between devices, send_back(): lax.all_to_all(returned, ('inline', 'crosslin'), split_axis=0, concat_axi...  5.64 us
  transfers between devices with their start and end apart: 3, of which 3 were waited for; matrix products, arithmetic and copies ran while one was open for 8% of the time, Pallas kernels for 0%

profile of v6, /device:TPU:1, one launch (start us, length us, event | category | flops | bytes accessed | tf_op | source)
XLA Modules:
  0.0 238.6 jit_solution(8555726370311600078)
XLA Ops:
  0.6 0.0 copy-start
  0.6 0.9 fusion.8
  1.6 0.1 copy.26
  1.7 0.2 reduce_window_sum.11
  1.9 0.1 copy.27
  2.0 0.1 eq.39
  2.1 0.1 and.11
  2.3 0.1 compare_and_fusion
  2.4 1.2 convolution_convert_fusion.3
  3.6 1.0 all_to_all.22
  4.6 11.5 %all-to-all-start = ((bf16[128,4,640]{2,1,0:T(4,128)(2,1)}), bf16[128,4,640]{2,1,0:T(4,128)(2,1)S(1)}, u32[]{:S(2)}, u32[]{:S(2)}) async-start(bf16[128,4,640]{2,1,0:T(4,128)(2,1)} %all_to_all.22), calls=%async_computation | async-start | bytes 1310720 | tf_op jit(solution)/shard_map/all_to_all | solution.py:84
  16.1 0.0 copy-done
  16.1 0.0 copy-start.7
  16.1 0.0 copy-start.10
  16.2 3.8 %convolution_convert_fusion.1.g_ref = bf16[2048,512]{1,0:T(8,128)(2,1)} fusion(bf16[2048,512]{1,0:T(8,128)(2,1)S(1)} %copy-done, bf16[512,512]{1,0:T(8,128)(2,1)} %param.15), kind=kOutput, calls=%fused_computation.2 | convolution fusion | flops 1074790400 | bytes 4718592 | tf_op jit(solution)/shard_map/dot_general | solution.py:150
  20.0 2.6 %convolution_convert_fusion.2.q_ref = bf16[2048,512]{1,0:T(8,128)(2,1)} fusion(bf16[2048,512]{1,0:T(8,128)(2,1)S(1)} %copy-done.7, bf16[512,512]{1,0:T(8,128)(2,1)S(1)} %copy-done.10), kind=kOutput, calls=%fused_computation.3 | convolution fusion | flops 1074790400 | bytes 4718592 | tf_op jit(solution)/shard_map/dot_general | solution.py:147
  22.6 8.4 %all-to-all-done = bf16[128,4,640]{2,1,0:T(4,128)(2,1)S(1)} async-done(((bf16[128,4,640]{2,1,0:T(4,128)(2,1)}), bf16[128,4,640]{2,1,0:T(4,128)(2,1)S(1)}, u32[]{:S(2)}, u32[]{:S(2)}) %all-to-all-start) | async-done | bytes 655392 | tf_op jit(solution)/shard_map/all_to_all | solution.py:84
  30.9 0.1 all_to_all.24
  31.1 0.7 convert_reduce_fusion
  31.8 2.3 convolution_convert_fusion.4.v_ref
  34.0 2.3 convolution_convert_fusion.5.k_ref
  36.3 43.9 %shard_map.127 = (bf16[2048,512]{1,0:T(8,128)(2,1)}, bf16[2048,512]{1,0:T(8,128)(2,1)}, bf16[512,512]{1,0:T(8,128)(2,1)}, bf16[512,512]{1,0:T(8,128)(2,1)}) custom-call(bf16[2048,512]{1,0:T(8,128)(2,1)} %convolution_convert_fusion.2.q_ref, bf16[2048,512]{1,0:T(8,128)(2,1)} %convolution_convert_fusion.1.g_ref, ...), custom_call_target="tpu_custom_call" | custom-call | tf_op jit(solution)/shard_map/pallas_call | solution.py:67
  80.2 0.0 copy-start.4
  80.2 0.0 copy-start.6
  80.2 0.0 copy-start.9
  80.2 2.6 %fusion.3 = f32[512,512]{1,0:T(8,128)} fusion(bf16[512,512]{1,0:T(8,128)(2,1)} %get-tuple-element.16, bf16[512,640]{1,0:T(8,128)(2,1)S(1)} %all_to_all.24), kind=kOutput, calls=%fused_computation.12 | convolution fusion | flops 268435456 | bytes 2097152 | tf_op jit(solution)/shard_map/dot_general | solution.py:163
  82.8 0.0 copy-done.4
  82.8 0.5 fusion.11
  83.3 0.0 copy-start.5
  83.3 2.2 fusion.12
  85.6 0.5 fusion
  86.1 0.9 all_to_all.25
  87.0 5.6 %all-to-all-start.1 = ((bf16[128,4,512]{2,1,0:T(4,128)(2,1)}), bf16[128,4,512]{2,1,0:T(4,128)(2,1)}, u32[]{:S(2)}, u32[]{:S(2)}) async-start(bf16[128,4,512]{2,1,0:T(4,128)(2,1)} %all_to_all.25), calls=%async_computation.1 | async-start | bytes 1048576 | tf_op jit(solution)/shard_map/all_to_all | solution.py:91
  92.6 0.0 copy-start.8
  92.6 2.6 %fusion.1 = f32[512,512]{1,0:T(8,128)} fusion(bf16[512,512]{1,0:T(8,128)(2,1)} %get-tuple-element.17, bf16[512,640]{1,0:T(8,128)(2,1)S(1)} %all_to_all.24), kind=kOutput, calls=%fused_computation.10 | convolution fusion | flops 268435456 | bytes 2097152 | tf_op jit(solution)/shard_map/dot_general | solution.py:164
  95.3 3.8 %convolution_bitcast_fusion = f32[512,512]{0,1:T(8,128)} fusion(bf16[2048,512]{1,0:T(8,128)(2,1)} %get-tuple-element.15, bf16[2048,512]{1,0:T(8,128)(2,1)S(1)} %copy-done.8), kind=kOutput, calls=%fused_computation.4 | convolution fusion | flops 1073741824 | bytes 5242880 | tf_op jit(solution)/shard_map/dot_general | solution.py:162
  99.1 6.8 %all-to-all-done.1 = bf16[128,4,512]{2,1,0:T(4,128)(2,1)} async-done(((bf16[128,4,512]{2,1,0:T(4,128)(2,1)}), bf16[128,4,512]{2,1,0:T(4,128)(2,1)}, u32[]{:S(2)}, u32[]{:S(2)}) %all-to-all-start.1) | async-done | bytes 524320 | tf_op jit(solution)/shard_map/all_to_all | solution.py:91
  105.9 2.0 all_to_all.27
  107.9 2.5 %copy.28 = f32[512,512]{1,0:T(8,128)} copy(f32[512,512]{0,1:T(8,128)} %convolution_bitcast_fusion) | data formatting | bytes 2097152 | tf_op jit(solution)/shard_map/optimization_barrier | solution.py:165
  110.4 2.5 %pad_maximum_fusion = f32[128,64,128]{2,1,0:T(8,128)S(1)} fusion(f32[128,16,128]{2,1,0:T(8,128)} %bitcast.73, f32[128,16,128]{2,1,0:T(8,128)} %bitcast.70, f32[128,16,128]{2,1,0:T(8,128)S(1)} %bitcast.69, f32[128,16,128]{2,1,0:T(8,128)} %bitcast.71), kind=kLoop, calls=%fused_computation | loop fusion | flops 3145728 | bytes 8388608 | tf_op jit(solution)/shard_map/concatenate | solution.py:110
  113.0 57.8 %all_to_all.34 = f32[128,64,128]{2,1,0:T(8,128)} all-to-all(f32[128,64,128]{2,1,0:T(8,128)S(1)} %pad_maximum_fusion), channel_id=1, replica_groups=mesh['inline'=16,'crosslin'=8] {'inline','crosslin'}, dimensions={0} | all-to-all | bytes 8388608 | tf_op jit(solution)/shard_map/all_to_all | solution.py:84
  170.8 2.5 %reduce_sum.9 = f32[64,128]{1,0:T(8,128)S(1)} reduce(f32[128,64,128]{2,1,0:T(8,128)} %all_to_all.34, f32[]{:T(128)} %constant.14.clone.1), dimensions={0}, to_apply=%region_2.3 | reduce | flops 1040384 | bytes 4227076 | tf_op jit(solution)/shard_map/reduce_sum | solution.py:111
  173.3 2.5 %broadcast_in_dim.2 = f32[128,64,128]{2,1,0:T(8,128)} broadcast(f32[64,128]{1,0:T(8,128)S(1)} %reduce_sum.9), dimensions={1,2} | broadcast | bytes 4227072 | tf_op jit(solution)/shard_map/broadcast_in_dim | solution.py:112
  175.8 5.5 %all-to-all-start.3 = ((f32[128,64,128]{2,1,0:T(8,128)}), f32[128,64,128]{2,1,0:T(8,128)}, u32[]{:S(2)}, u32[]{:S(2)}) async-start(f32[128,64,128]{2,1,0:T(8,128)} %broadcast_in_dim.2), calls=%async_computation.3 | async-start | bytes 8388608 | tf_op jit(solution)/shard_map/all_to_all | solution.py:84
  181.3 4.3 %convolution_convert_fusion = bf16[2048,512]{1,0:T(8,128)(2,1)} fusion(bf16[2048,512]{1,0:T(8,128)(2,1)} %get-tuple-element.15, bf16[512,512]{1,0:T(8,128)(2,1)S(1)} %copy-done.11), kind=kOutput, calls=%fused_computation.1 | convolution fusion | flops 1074790400 | bytes 4718592 | tf_op jit(solution)/shard_map/dot_general | solution.py:169
  185.6 1.0 fusion.13
  186.6 47.7 %all-to-all-done.3 = f32[128,64,128]{2,1,0:T(8,128)} async-done(((f32[128,64,128]{2,1,0:T(8,128)}), f32[128,64,128]{2,1,0:T(8,128)}, u32[]{:S(2)}, u32[]{:S(2)}) %all-to-all-start.3) | async-done | bytes 4194336 | tf_op jit(solution)/shard_map/all_to_all | solution.py:84
  234.3 4.3 %fusion.10 = (f32[128,16,128]{2,1,0:T(8,128)}, f32[128,16,128]{2,1,0:T(8,128)}, f32[128,16,128]{2,1,0:T(8,128)}, f32[128,16,128]{2,1,0:T(8,128)}) fusion(f32[128,64,128]{2,1,0:T(8,128)} %all-to-all-done.3), kind=kLoop, calls=%fused_computation.23 | loop fusion | bytes 8388608 | tf_op jit(solution)/shard_map/slice | solution.py:114
  (18 shorter events, 0.1 us)
Async XLA Ops:
  0.6 15.5 %copy-start = (bf16[2048,512]{1,0:T(8,128)(2,1)S(1)}, bf16[2048,512]{1,0:T(8,128)(2,1)}, u32[]{:S(2)}) copy-start(bf16[2048,512]{1,0:T(8,128)(2,1)} %param.9) | copy-start | bytes 6291460
  4.6 26.3 %all-to-all-start = ((bf16[128,4,640]{2,1,0:T(4,128)(2,1)}), bf16[128,4,640]{2,1,0:T(4,128)(2,1)S(1)}, u32[]{:S(2)}, u32[]{:S(2)}) async-start(bf16[128,4,640]{2,1,0:T(4,128)(2,1)} %all_to_all.22), calls=%async_computation | async-start | bytes 1310720 | tf_op jit(solution)/shard_map/all_to_all | solution.py:84
  16.1 3.9 %copy-start.7 = (bf16[2048,512]{1,0:T(8,128)(2,1)S(1)}, bf16[2048,512]{1,0:T(8,128)(2,1)}, u32[]{:S(2)}) copy-start(bf16[2048,512]{1,0:T(8,128)(2,1)} %param.8) | copy-start | bytes 6291460
  16.1 3.8 %copy-start.10 = (bf16[512,512]{1,0:T(8,128)(2,1)S(1)}, bf16[512,512]{1,0:T(8,128)(2,1)}, u32[]{:S(2)}) copy-start(bf16[512,512]{1,0:T(8,128)(2,1)} %param.12) | copy-start | bytes 1572868
  80.2 2.7 %copy-start.4 = (bf16[512,512]{1,0:T(8,128)(2,1)S(1)}, bf16[512,512]{1,0:T(8,128)(2,1)}, u32[]{:S(2)}) copy-start(bf16[512,512]{1,0:T(8,128)(2,1)} %get-tuple-element.16) | copy-start | bytes 1572868
  80.2 2.7 %copy-start.6 = (bf16[512,512]{1,0:T(8,128)(2,1)S(1)}, bf16[512,512]{1,0:T(8,128)(2,1)}, u32[]{:S(2)}) copy-start(bf16[512,512]{1,0:T(8,128)(2,1)} %param.13) | copy-start | bytes 1572868
  80.2 3.1 %copy-start.9 = (bf16[2048,512]{1,0:T(8,128)(2,1)S(1)}, bf16[2048,512]{1,0:T(8,128)(2,1)}, u32[]{:S(2)}) copy-start(bf16[2048,512]{1,0:T(8,128)(2,1)} %get-tuple-element.18) | copy-start | bytes 6291460
  83.3 2.3 copy-start.3
  83.3 2.3 copy-start.5
  87.0 18.9 %all-to-all-start.1 = ((bf16[128,4,512]{2,1,0:T(4,128)(2,1)}), bf16[128,4,512]{2,1,0:T(4,128)(2,1)}, u32[]{:S(2)}, u32[]{:S(2)}) async-start(bf16[128,4,512]{2,1,0:T(4,128)(2,1)} %all_to_all.25), calls=%async_computation.1 | async-start | bytes 1048576 | tf_op jit(solution)/shard_map/all_to_all | solution.py:91
  92.6 2.6 %copy-start.8 = (bf16[2048,512]{1,0:T(8,128)(2,1)S(1)}, bf16[2048,512]{1,0:T(8,128)(2,1)}, u32[]{:S(2)}) copy-start(bf16[2048,512]{1,0:T(8,128)(2,1)} %param.8) | copy-start | bytes 6291460
  99.1 11.3 %copy-start.1 = (f32[512,512]{1,0:T(8,128)S(1)}, f32[512,512]{1,0:T(8,128)}, u32[]{:S(2)}) copy-start(f32[512,512]{1,0:T(8,128)} %fusion.3) | copy-start | bytes 3145732
  175.8 5.5 %copy-start.11 = (bf16[512,512]{1,0:T(8,128)(2,1)S(1)}, bf16[512,512]{1,0:T(8,128)(2,1)}, u32[]{:S(2)}) copy-start(bf16[512,512]{1,0:T(8,128)(2,1)} %param.12) | copy-start | bytes 1572868
  175.8 58.5 %all-to-all-start.3 = ((f32[128,64,128]{2,1,0:T(8,128)}), f32[128,64,128]{2,1,0:T(8,128)}, u32[]{:S(2)}, u32[]{:S(2)}) async-start(f32[128,64,128]{2,1,0:T(8,128)} %broadcast_in_dim.2), calls=%async_computation.3 | async-start | bytes 8388608 | tf_op jit(solution)/shard_map/all_to_all | solution.py:84
  181.3 4.3 %copy-start.2 = (bf16[512,512]{1,0:T(8,128)(2,1)S(1)}, bf16[512,512]{1,0:T(8,128)(2,1)}, u32[]{:S(2)}) copy-start(bf16[512,512]{1,0:T(8,128)(2,1)} %all_to_all.27) | copy-start | bytes 1572868

commit v7 on v6

--- a/solution.py
+++ b/solution.py
@@ -108,8 +108,8 @@
     tiled = [as_tiles(part).reshape(count, -1, 128) for part in parts]
     depth = tiled[0].shape[1]
     pieces = jnp.concatenate(tiled, axis=1)
-    mine = send_slots(pieces).sum(axis=0, keepdims=True)
-    gathered = send_slots(jnp.broadcast_to(mine, pieces.shape))
+    mine = send_slots(pieces).sum(axis=0, keepdims=True).astype(jnp.bfloat16)
+    gathered = send_slots(jnp.broadcast_to(mine, pieces.shape)).astype(jnp.float32)
     return tuple(
         from_tiles(gathered[:, i * depth : (i + 1) * depth], part.shape)
         for i, part in enumerate(parts)

time: 239 us -> 215 us (0.90)
  waiting for transfers between devices: 62.9 us -> 40.2 us
    all_to_all x2, waiting for transfers between devices: 56.1 us -> 33.4 us  [send_slots(): lax.all_to_all(outgoing, ('inline', 'crosslin'), split_axis=0, concat_axi...]
where the time goes in v7:
time: 215 us
  blocking collectives  57.8 us (27%)
  Pallas kernels  43.8 us (20%)
  waiting for transfers between devices  40.2 us (19%)
  matrix products  29.7 us (14%)
  starting transfers between devices  22.6 us (11%)
  local copies, waits for them, and re-layouts  12.5 us (6%)
  other arithmetic  6.94 us (3%)
    all_to_all x1, blocking collectives, send_slots(): lax.all_to_all(outgoing, ('inline', 'crosslin'), split_axis=0, concat_axi...  57.8 us
    pallas_call x1, Pallas kernels, fused_attention(): pl.pallas_call(attention_kernel, grid=(rows // block,), in_specs=[row_blo...  43.8 us
    all_to_all x2, waiting for transfers between devices, send_slots(): lax.all_to_all(outgoing, ('inline', 'crosslin'), split_axis=0, concat_axi...  33.4 us
    all_to_all x2, starting transfers between devices, send_slots(): lax.all_to_all(outgoing, ('inline', 'crosslin'), split_axis=0, concat_axi...  17 us
    all_to_all x1, waiting for transfers between devices, send_back(): lax.all_to_all(returned, ('inline', 'crosslin'), split_axis=0, concat_axi...  6.81 us
    all_to_all x1, starting transfers between devices, send_back(): lax.all_to_all(returned, ('inline', 'crosslin'), split_axis=0, concat_axi...  5.65 us
  transfers between devices with their start and end apart: 3, of which 3 were waited for; matrix products, arithmetic and copies ran while one was open for 8% of the time, Pallas kernels for 0%

profile of v7, /device:TPU:1, one launch (start us, length us, event | category | flops | bytes accessed | tf_op | source)
XLA Modules:
  0.0 214.5 jit_solution(17232728388455165911)
XLA Ops:
  0.6 0.0 copy-start
  0.6 0.9 fusion.8
  1.6 0.1 copy.26
  1.7 0.2 reduce_window_sum.11
  1.9 0.1 copy.27
  2.0 0.1 eq.39
  2.1 0.1 and.11
  2.3 0.1 compare_and_fusion
  2.4 1.2 convolution_convert_fusion.3
  3.6 1.0 all_to_all.22
  4.6 11.5 %all-to-all-start = ((bf16[128,4,640]{2,1,0:T(4,128)(2,1)}), bf16[128,4,640]{2,1,0:T(4,128)(2,1)S(1)}, u32[]{:S(2)}, u32[]{:S(2)}) async-start(bf16[128,4,640]{2,1,0:T(4,128)(2,1)} %all_to_all.22), calls=%async_computation | async-start | bytes 1310720 | tf_op jit(solution)/shard_map/all_to_all | solution.py:84
  16.1 0.0 copy-done
  16.1 0.0 copy-start.7
  16.1 0.0 copy-start.10
  16.2 3.8 %convolution_convert_fusion.1.g_ref = bf16[2048,512]{1,0:T(8,128)(2,1)} fusion(bf16[2048,512]{1,0:T(8,128)(2,1)S(1)} %copy-done, bf16[512,512]{1,0:T(8,128)(2,1)} %param.15), kind=kOutput, calls=%fused_computation.2 | convolution fusion | flops 1074790400 | bytes 4718592 | tf_op jit(solution)/shard_map/dot_general | solution.py:150
  20.0 2.6 %convolution_convert_fusion.2.q_ref = bf16[2048,512]{1,0:T(8,128)(2,1)} fusion(bf16[2048,512]{1,0:T(8,128)(2,1)S(1)} %copy-done.7, bf16[512,512]{1,0:T(8,128)(2,1)S(1)} %copy-done.10), kind=kOutput, calls=%fused_computation.3 | convolution fusion | flops 1074790400 | bytes 4718592 | tf_op jit(solution)/shard_map/dot_general | solution.py:147
  22.6 8.4 %all-to-all-done = bf16[128,4,640]{2,1,0:T(4,128)(2,1)S(1)} async-done(((bf16[128,4,640]{2,1,0:T(4,128)(2,1)}), bf16[128,4,640]{2,1,0:T(4,128)(2,1)S(1)}, u32[]{:S(2)}, u32[]{:S(2)}) %all-to-all-start) | async-done | bytes 655392 | tf_op jit(solution)/shard_map/all_to_all | solution.py:84
  30.9 0.1 all_to_all.24
  31.1 0.7 convert_reduce_fusion
  31.8 2.3 %convolution_convert_fusion.4.v_ref = bf16[512,512]{1,0:T(8,128)(2,1)} fusion(bf16[512,512]{1,0:T(8,128)(2,1)} %param.14, bf16[512,640]{1,0:T(8,128)(2,1)S(1)} %all_to_all.24), kind=kOutput, calls=%fused_computation.7 | convolution fusion | flops 268697600 | bytes 1572864 | tf_op jit(solution)/shard_map/dot_general | solution.py:144
  34.0 2.3 %convolution_convert_fusion.5.k_ref = bf16[512,512]{1,0:T(8,128)(2,1)} fusion(bf16[512,512]{1,0:T(8,128)(2,1)} %param.13, bf16[512,640]{1,0:T(8,128)(2,1)S(1)} %all_to_all.24), kind=kOutput, calls=%fused_computation.8 | convolution fusion | flops 268697600 | bytes 1572864 | tf_op jit(solution)/shard_map/dot_general | solution.py:141
  36.3 43.8 %shard_map.127 = (bf16[2048,512]{1,0:T(8,128)(2,1)}, bf16[2048,512]{1,0:T(8,128)(2,1)}, bf16[512,512]{1,0:T(8,128)(2,1)}, bf16[512,512]{1,0:T(8,128)(2,1)}) custom-call(bf16[2048,512]{1,0:T(8,128)(2,1)} %convolution_convert_fusion.2.q_ref, bf16[2048,512]{1,0:T(8,128)(2,1)} %convolution_convert_fusion.1.g_ref, ...), custom_call_target="tpu_custom_call" | custom-call | tf_op jit(solution)/shard_map/pallas_call | solution.py:67
  80.2 0.0 copy-start.4
  80.2 0.0 copy-start.6
  80.2 0.0 copy-start.9
  80.2 2.6 %fusion.3 = f32[512,512]{1,0:T(8,128)} fusion(bf16[512,512]{1,0:T(8,128)(2,1)} %get-tuple-element.16, bf16[512,640]{1,0:T(8,128)(2,1)S(1)} %all_to_all.24), kind=kOutput, calls=%fused_computation.12 | convolution fusion | flops 268435456 | bytes 2097152 | tf_op jit(solution)/shard_map/dot_general | solution.py:163
  82.8 0.5 fusion.11
  83.3 0.0 copy-start.5
  83.3 2.2 %fusion.12 = f32[512,512]{1,0:T(8,128)} fusion(bf16[2048,512]{1,0:T(8,128)(2,1)S(1)} %copy-done.9, bf16[2048,512]{1,0:T(8,128)(2,1)S(1)} %copy-done), kind=kOutput, calls=%fused_computation.25 | convolution fusion | flops 1073741824 | bytes 5242880 | tf_op jit(solution)/shard_map/dot_general | solution.py:161
  85.6 0.5 fusion
  86.1 0.9 all_to_all.25
  87.0 5.6 %all-to-all-start.1 = ((bf16[128,4,512]{2,1,0:T(4,128)(2,1)}), bf16[128,4,512]{2,1,0:T(4,128)(2,1)}, u32[]{:S(2)}, u32[]{:S(2)}) async-start(bf16[128,4,512]{2,1,0:T(4,128)(2,1)} %all_to_all.25), calls=%async_computation.1 | async-start | bytes 1048576 | tf_op jit(solution)/shard_map/all_to_all | solution.py:91
  92.6 0.0 copy-start.8
  92.6 2.6 %fusion.1 = f32[512,512]{1,0:T(8,128)} fusion(bf16[512,512]{1,0:T(8,128)(2,1)} %get-tuple-element.17, bf16[512,640]{1,0:T(8,128)(2,1)S(1)} %all_to_all.24), kind=kOutput, calls=%fused_computation.10 | convolution fusion | flops 268435456 | bytes 2097152 | tf_op jit(solution)/shard_map/dot_general | solution.py:164
  95.3 3.8 %convolution_bitcast_fusion = f32[512,512]{0,1:T(8,128)} fusion(bf16[2048,512]{1,0:T(8,128)(2,1)} %get-tuple-element.15, bf16[2048,512]{1,0:T(8,128)(2,1)S(1)} %copy-done.8), kind=kOutput, calls=%fused_computation.4 | convolution fusion | flops 1073741824 | bytes 5242880 | tf_op jit(solution)/shard_map/dot_general | solution.py:162
  99.1 6.8 %all-to-all-done.1 = bf16[128,4,512]{2,1,0:T(4,128)(2,1)} async-done(((bf16[128,4,512]{2,1,0:T(4,128)(2,1)}), bf16[128,4,512]{2,1,0:T(4,128)(2,1)}, u32[]{:S(2)}, u32[]{:S(2)}) %all-to-all-start.1) | async-done | bytes 524320 | tf_op jit(solution)/shard_map/all_to_all | solution.py:91
  105.9 2.0 all_to_all.27
  107.9 2.5 %copy.28 = f32[512,512]{1,0:T(8,128)} copy(f32[512,512]{0,1:T(8,128)} %convolution_bitcast_fusion) | data formatting | bytes 2097152 | tf_op jit(solution)/shard_map/optimization_barrier | solution.py:165
  110.4 0.0 copy-done.1
  110.4 2.5 %pad_maximum_fusion = f32[128,64,128]{2,1,0:T(8,128)S(1)} fusion(f32[128,16,128]{2,1,0:T(8,128)} %bitcast.73, f32[128,16,128]{2,1,0:T(8,128)} %bitcast.70, f32[128,16,128]{2,1,0:T(8,128)S(1)} %bitcast.69, f32[128,16,128]{2,1,0:T(8,128)} %bitcast.71), kind=kLoop, calls=%fused_computation | loop fusion | flops 3145728 | bytes 8388608 | tf_op jit(solution)/shard_map/concatenate | solution.py:110
  113.0 57.8 %all_to_all.34 = f32[128,64,128]{2,1,0:T(8,128)} all-to-all(f32[128,64,128]{2,1,0:T(8,128)S(1)} %pad_maximum_fusion), channel_id=1, replica_groups=mesh['inline'=16,'crosslin'=8] {'inline','crosslin'}, dimensions={0} | all-to-all | bytes 8388608 | tf_op jit(solution)/shard_map/all_to_all | solution.py:84
  170.8 2.5 %reduce_sum.9 = bf16[64,128]{1,0:T(8,128)(2,1)S(1)} reduce(f32[128,64,128]{2,1,0:T(8,128)} %all_to_all.34, f32[]{:T(128)} %constant.14.clone.1), dimensions={0}, to_apply=%region_2.3 | reduce | flops 1040384 | bytes 4210692 | tf_op jit(solution)/shard_map/reduce_sum | solution.py:111
  173.3 1.8 broadcast_in_dim.2
  175.1 5.5 %all-to-all-start.3 = ((bf16[128,64,128]{2,1,0:T(8,128)(2,1)}), bf16[128,64,128]{2,1,0:T(8,128)(2,1)}, u32[]{:S(2)}, u32[]{:S(2)}) async-start(bf16[128,64,128]{2,1,0:T(8,128)(2,1)} %broadcast_in_dim.2), calls=%async_computation.3 | async-start | bytes 4194304 | tf_op jit(solution)/shard_map/all_to_all | solution.py:84
  180.6 4.3 %convolution_convert_fusion = bf16[2048,512]{1,0:T(8,128)(2,1)} fusion(bf16[2048,512]{1,0:T(8,128)(2,1)} %get-tuple-element.15, bf16[512,512]{1,0:T(8,128)(2,1)S(1)} %copy-done.11), kind=kOutput, calls=%fused_computation.1 | convolution fusion | flops 1074790400 | bytes 4718592 | tf_op jit(solution)/shard_map/dot_general | solution.py:169
  184.8 1.0 fusion.13
  185.8 25.0 %all-to-all-done.3 = bf16[128,64,128]{2,1,0:T(8,128)(2,1)} async-done(((bf16[128,64,128]{2,1,0:T(8,128)(2,1)}), bf16[128,64,128]{2,1,0:T(8,128)(2,1)}, u32[]{:S(2)}, u32[]{:S(2)}) %all-to-all-start.3) | async-done | bytes 2097184 | tf_op jit(solution)/shard_map/all_to_all | solution.py:84
  210.9 3.6 %fusion.10 = (f32[128,16,128]{2,1,0:T(8,128)}, f32[128,16,128]{2,1,0:T(8,128)}, f32[128,16,128]{2,1,0:T(8,128)}, f32[128,16,128]{2,1,0:T(8,128)}) fusion(bf16[128,64,128]{2,1,0:T(8,128)(2,1)} %all-to-all-done.3), kind=kLoop, calls=%fused_computation.23 | loop fusion | bytes 8388608 | tf_op jit(solution)/shard_map/slice | solution.py:114
  (18 shorter events, 0.1 us)
Async XLA Ops:
  0.6 15.5 %copy-start = (bf16[2048,512]{1,0:T(8,128)(2,1)S(1)}, bf16[2048,512]{1,0:T(8,128)(2,1)}, u32[]{:S(2)}) copy-start(bf16[2048,512]{1,0:T(8,128)(2,1)} %param.9) | copy-start | bytes 6291460
  4.6 26.3 %all-to-all-start = ((bf16[128,4,640]{2,1,0:T(4,128)(2,1)}), bf16[128,4,640]{2,1,0:T(4,128)(2,1)S(1)}, u32[]{:S(2)}, u32[]{:S(2)}) async-start(bf16[128,4,640]{2,1,0:T(4,128)(2,1)} %all_to_all.22), calls=%async_computation | async-start | bytes 1310720 | tf_op jit(solution)/shard_map/all_to_all | solution.py:84
  16.1 3.9 %copy-start.7 = (bf16[2048,512]{1,0:T(8,128)(2,1)S(1)}, bf16[2048,512]{1,0:T(8,128)(2,1)}, u32[]{:S(2)}) copy-start(bf16[2048,512]{1,0:T(8,128)(2,1)} %param.8) | copy-start | bytes 6291460
  16.1 3.8 %copy-start.10 = (bf16[512,512]{1,0:T(8,128)(2,1)S(1)}, bf16[512,512]{1,0:T(8,128)(2,1)}, u32[]{:S(2)}) copy-start(bf16[512,512]{1,0:T(8,128)(2,1)} %param.12) | copy-start | bytes 1572868
  80.2 2.7 %copy-start.4 = (bf16[512,512]{1,0:T(8,128)(2,1)S(1)}, bf16[512,512]{1,0:T(8,128)(2,1)}, u32[]{:S(2)}) copy-start(bf16[512,512]{1,0:T(8,128)(2,1)} %get-tuple-element.16) | copy-start | bytes 1572868
  80.2 2.7 %copy-start.6 = (bf16[512,512]{1,0:T(8,128)(2,1)S(1)}, bf16[512,512]{1,0:T(8,128)(2,1)}, u32[]{:S(2)}) copy-start(bf16[512,512]{1,0:T(8,128)(2,1)} %param.13) | copy-start | bytes 1572868
  80.2 3.1 %copy-start.9 = (bf16[2048,512]{1,0:T(8,128)(2,1)S(1)}, bf16[2048,512]{1,0:T(8,128)(2,1)}, u32[]{:S(2)}) copy-start(bf16[2048,512]{1,0:T(8,128)(2,1)} %get-tuple-element.18) | copy-start | bytes 6291460
  83.3 2.3 %copy-start.3 = (bf16[512,512]{1,0:T(8,128)(2,1)S(1)}, bf16[512,512]{1,0:T(8,128)(2,1)}, u32[]{:S(2)}) copy-start(bf16[512,512]{1,0:T(8,128)(2,1)} %get-tuple-element.17) | copy-start | bytes 1572868
  83.3 2.3 %copy-start.5 = (bf16[512,512]{1,0:T(8,128)(2,1)S(1)}, bf16[512,512]{1,0:T(8,128)(2,1)}, u32[]{:S(2)}) copy-start(bf16[512,512]{1,0:T(8,128)(2,1)} %param.14) | copy-start | bytes 1572868
  87.0 18.9 %all-to-all-start.1 = ((bf16[128,4,512]{2,1,0:T(4,128)(2,1)}), bf16[128,4,512]{2,1,0:T(4,128)(2,1)}, u32[]{:S(2)}, u32[]{:S(2)}) async-start(bf16[128,4,512]{2,1,0:T(4,128)(2,1)} %all_to_all.25), calls=%async_computation.1 | async-start | bytes 1048576 | tf_op jit(solution)/shard_map/all_to_all | solution.py:91
  92.6 2.6 %copy-start.8 = (bf16[2048,512]{1,0:T(8,128)(2,1)S(1)}, bf16[2048,512]{1,0:T(8,128)(2,1)}, u32[]{:S(2)}) copy-start(bf16[2048,512]{1,0:T(8,128)(2,1)} %param.8) | copy-start | bytes 6291460
  99.1 11.3 %copy-start.1 = (f32[512,512]{1,0:T(8,128)S(1)}, f32[512,512]{1,0:T(8,128)}, u32[]{:S(2)}) copy-start(f32[512,512]{1,0:T(8,128)} %fusion.3) | copy-start | bytes 3145732
  175.1 5.5 %copy-start.11 = (bf16[512,512]{1,0:T(8,128)(2,1)S(1)}, bf16[512,512]{1,0:T(8,128)(2,1)}, u32[]{:S(2)}) copy-start(bf16[512,512]{1,0:T(8,128)(2,1)} %param.12) | copy-start | bytes 1572868
  175.1 35.8 %all-to-all-start.3 = ((bf16[128,64,128]{2,1,0:T(8,128)(2,1)}), bf16[128,64,128]{2,1,0:T(8,128)(2,1)}, u32[]{:S(2)}, u32[]{:S(2)}) async-start(bf16[128,64,128]{2,1,0:T(8,128)(2,1)} %broadcast_in_dim.2), calls=%async_computation.3 | async-start | bytes 4194304 | tf_op jit(solution)/shard_map/all_to_all | solution.py:84
  180.6 4.3 %copy-start.2 = (bf16[512,512]{1,0:T(8,128)(2,1)S(1)}, bf16[512,512]{1,0:T(8,128)(2,1)}, u32[]{:S(2)}) copy-start(bf16[512,512]{1,0:T(8,128)(2,1)} %all_to_all.27) | copy-start | bytes 1572868

commit v8 on v7

--- a/solution.py
+++ b/solution.py
@@ -87,13 +87,6 @@
     return arrived
 
 
-def send_back(returned):
-    result_rows = lax.all_to_all(
-        returned, ("inline", "crosslin"), split_axis=0, concat_axis=0, tiled=True
-    )
-    return result_rows
-
-
 def as_tiles(part):
     rows, cols = part.shape
     return part.reshape(rows // 8, 8, cols // 128, 128).transpose(0, 2, 1, 3)
@@ -103,17 +96,23 @@
     return tiles.reshape(shape[0] // 8, shape[1] // 128, 8, 128).transpose(0, 2, 1, 3).reshape(shape)
 
 
-def sum_over_devices(parts):
+def sum_over_devices(parts, rider):
     count = lax.axis_size("inline") * lax.axis_size("crosslin")
     tiled = [as_tiles(part).reshape(count, -1, 128) for part in parts]
     depth = tiled[0].shape[1]
     pieces = jnp.concatenate(tiled, axis=1)
     mine = send_slots(pieces).sum(axis=0, keepdims=True).astype(jnp.bfloat16)
-    gathered = send_slots(jnp.broadcast_to(mine, pieces.shape)).astype(jnp.float32)
-    return tuple(
+    rider_rows = rider.size // (count * 128)
+    payload = jnp.concatenate(
+        [jnp.broadcast_to(mine, pieces.shape), rider.reshape(count, rider_rows, 128)], axis=1
+    )
+    arrived = send_slots(payload)
+    gathered = arrived[:, : pieces.shape[1]].astype(jnp.float32)
+    sums = tuple(
         from_tiles(gathered[:, i * depth : (i + 1) * depth], part.shape)
         for i, part in enumerate(parts)
     )
+    return sums, arrived[:, pieces.shape[1] :].reshape(rider.shape)
 
 
 def on_device(
@@ -157,15 +156,13 @@
     slot_trace = slot_trace + jnp.dot(
         value_grad, value_weight.T, preferred_element_type=jnp.float32
     )
-    returned = send_back(slot_trace.astype(jnp.bfloat16))
     part_output = jnp.dot(attn_out.T, cotangent, preferred_element_type=jnp.float32)
     part_query = jnp.dot(grid_feat.T, query_grad, preferred_element_type=jnp.float32)
     part_key = jnp.dot(feat_tile.T, key_grad, preferred_element_type=jnp.float32)
     part_value = jnp.dot(feat_tile.T, value_grad, preferred_element_type=jnp.float32)
-    returned, parts = lax.optimization_barrier(
-        (returned, (part_query, part_key, part_value, part_output))
+    (grad_query, grad_key, grad_value, grad_output), returned = sum_over_devices(
+        (part_query, part_key, part_value, part_output), slot_trace.astype(jnp.bfloat16)
     )
-    grad_query, grad_key, grad_value, grad_output = sum_over_devices(parts)
     grad_grid = jnp.dot(query_grad, query_weight.T, preferred_element_type=jnp.float32).astype(
         jnp.bfloat16
     )

time: 215 us -> 205 us (0.953)
  blocking collectives: 57.8 us -> 0 us
  waiting for transfers between devices: 40.2 us -> 90.9 us
  matrix products: 29.7 us -> 25.5 us
  other arithmetic: 6.94 us -> 10.8 us
  local copies, waits for them, and re-layouts: 12.5 us -> 10.1 us
    all_to_all x1 -> x0, blocking collectives: 57.8 us -> none  [send_slots(): lax.all_to_all(outgoing, ('inline', 'crosslin'), split_axis=0, concat_axi...]
    all_to_all x2 -> x3, waiting for transfers between devices: 33.4 us -> 90.9 us  [send_slots(): lax.all_to_all(outgoing, ('inline', 'crosslin'), split_axis=0, concat_axi...]
    all_to_all x1 -> x0, waiting for transfers between devices: 6.81 us -> none  [send_back(): lax.all_to_all(returned, ('inline', 'crosslin'), split_axis=0, concat_axi...]
    all_to_all x2 -> x3, starting transfers between devices: 17 us -> 22.8 us  [send_slots(): lax.all_to_all(outgoing, ('inline', 'crosslin'), split_axis=0, concat_axi...]
    all_to_all x1 -> x0, starting transfers between devices: 5.65 us -> none  [send_back(): lax.all_to_all(returned, ('inline', 'crosslin'), split_axis=0, concat_axi...]
    all_to_all x2 -> x0, local copies, waits for them, and re-layouts: 2.89 us -> none  [send_back(): lax.all_to_all(returned, ('inline', 'crosslin'), split_axis=0, concat_axi...]
    dot_general x0 -> x1, local copies, waits for them, and re-layouts: none -> 2.59 us  [on_device(): jnp.dot(grid_feat.T, query_grad, preferred_element_type=jnp.float32)]
    optimization_barrier x1 -> x0, local copies, waits for them, and re-layouts: 2.53 us -> none  [on_device(): lax.optimization_barrier((returned, (part_query, part_key, part_value, pa...]
  transfers between devices with their start and end apart: 3 -> 3, of which waited for: 3 -> 3; matrix products, arithmetic and copies ran while one was open for 8% -> 6% of each run, Pallas kernels for 0% -> 0%
where the time goes in v8:
time: 205 us
  waiting for transfers between devices  90.9 us (44%)
  Pallas kernels  43.9 us (21%)
  matrix products  25.5 us (12%)
  starting transfers between devices  22.8 us (11%)
  other arithmetic  10.8 us (5%)
  local copies, waits for them, and re-layouts  10.1 us (5%)
    all_to_all x3, waiting for transfers between devices, send_slots(): lax.all_to_all(outgoing, ('inline', 'crosslin'), split_axis=0, concat_axi...  90.9 us
    pallas_call x1, Pallas kernels, fused_attention(): pl.pallas_call(attention_kernel, grid=(rows // block,), in_specs=[row_blo...  43.9 us
    all_to_all x3, starting transfers between devices, send_slots(): lax.all_to_all(outgoing, ('inline', 'crosslin'), split_axis=0, concat_axi...  22.8 us
    dot_general x1, matrix products, on_device(): jnp.dot(query_grad, query_weight.T, preferred_element_type=jnp.float32)  4.2 us
  transfers between devices with their start and end apart: 3, of which 3 were waited for; matrix products, arithmetic and copies ran while one was open for 6% of the time, Pallas kernels for 0%

profile of v8, /device:TPU:1, one launch (start us, length us, event | category | flops | bytes accessed | tf_op | source)
XLA Modules:
  0.0 204.8 jit_solution(3512933047737401303)
XLA Ops:
  0.6 0.0 copy-start
  0.6 0.9 fusion.12
  1.6 0.1 copy.26
  1.7 0.2 reduce_window_sum.11
  1.9 0.1 copy.27
  2.0 0.1 eq.50
  2.1 0.1 and.22
  2.3 1.3 convolution_convert_fusion.3
  3.5 1.0 all_to_all.14
  4.5 11.5 %all-to-all-start = ((bf16[128,4,640]{2,1,0:T(4,128)(2,1)}), bf16[128,4,640]{2,1,0:T(4,128)(2,1)S(1)}, u32[]{:S(2)}, u32[]{:S(2)}) async-start(bf16[128,4,640]{2,1,0:T(4,128)(2,1)} %all_to_all.14), calls=%async_computation | async-start | bytes 1310720 | tf_op jit(solution)/shard_map/all_to_all | solution.py:84
  16.0 0.0 copy-start.9
  16.1 0.0 copy-start.12
  16.1 3.8 %convolution_convert_fusion.1.g_ref = bf16[2048,512]{1,0:T(8,128)(2,1)} fusion(bf16[2048,512]{1,0:T(8,128)(2,1)S(1)} %copy-done, bf16[512,512]{1,0:T(8,128)(2,1)} %param.15), kind=kOutput, calls=%fused_computation.2 | convolution fusion | flops 1074790400 | bytes 4718592 | tf_op jit(solution)/shard_map/dot_general | solution.py:149
  19.9 2.6 %convolution_convert_fusion.2.q_ref = bf16[2048,512]{1,0:T(8,128)(2,1)} fusion(bf16[2048,512]{1,0:T(8,128)(2,1)S(1)} %copy-done.9, bf16[512,512]{1,0:T(8,128)(2,1)S(1)} %copy-done.12), kind=kOutput, calls=%fused_computation.3 | convolution fusion | flops 1074790400 | bytes 4718592 | tf_op jit(solution)/shard_map/dot_general | solution.py:146
  22.5 8.4 %all-to-all-done = bf16[128,4,640]{2,1,0:T(4,128)(2,1)S(1)} async-done(((bf16[128,4,640]{2,1,0:T(4,128)(2,1)}), bf16[128,4,640]{2,1,0:T(4,128)(2,1)S(1)}, u32[]{:S(2)}, u32[]{:S(2)}) %all-to-all-start) | async-done | bytes 655392 | tf_op jit(solution)/shard_map/all_to_all | solution.py:84
  30.8 0.1 all_to_all.16
  31.0 0.7 convert_reduce_fusion
  31.7 2.3 %convolution_convert_fusion.4.v_ref = bf16[512,512]{1,0:T(8,128)(2,1)} fusion(bf16[512,512]{1,0:T(8,128)(2,1)} %param.14, bf16[512,640]{1,0:T(8,128)(2,1)S(1)} %all_to_all.16), kind=kOutput, calls=%fused_computation.9 | convolution fusion | flops 268697600 | bytes 1572864 | tf_op jit(solution)/shard_map/dot_general | solution.py:143
  34.0 2.3 %convolution_convert_fusion.5.k_ref = bf16[512,512]{1,0:T(8,128)(2,1)} fusion(bf16[512,512]{1,0:T(8,128)(2,1)} %param.13, bf16[512,640]{1,0:T(8,128)(2,1)S(1)} %all_to_all.16), kind=kOutput, calls=%fused_computation.10 | convolution fusion | flops 268697600 | bytes 1572864 | tf_op jit(solution)/shard_map/dot_general | solution.py:140
  36.2 43.9 %shard_map.127 = (bf16[2048,512]{1,0:T(8,128)(2,1)}, bf16[2048,512]{1,0:T(8,128)(2,1)}, bf16[512,512]{1,0:T(8,128)(2,1)}, bf16[512,512]{1,0:T(8,128)(2,1)}) custom-call(bf16[2048,512]{1,0:T(8,128)(2,1)} %convolution_convert_fusion.2.q_ref, bf16[2048,512]{1,0:T(8,128)(2,1)} %convolution_convert_fusion.1.g_ref, ...), custom_call_target="tpu_custom_call" | custom-call | tf_op jit(solution)/shard_map/pallas_call | solution.py:67
  80.1 4.0 %fusion.15 = f32[512,512]{1,0:T(8,128)} fusion(bf16[2048,512]{1,0:T(8,128)(2,1)} %get-tuple-element.13, bf16[2048,512]{1,0:T(8,128)(2,1)S(1)} %copy-done), kind=kOutput, calls=%fused_computation.30 | convolution fusion | flops 1073741824 | bytes 5242880 | tf_op jit(solution)/shard_map/dot_general | solution.py:159
  84.1 2.2 %convolution_bitcast_fusion = f32[512,512]{0,1:T(8,128)} fusion(bf16[2048,512]{1,0:T(8,128)(2,1)S(1)} %copy-done.11, bf16[2048,512]{1,0:T(8,128)(2,1)S(1)} %copy-done.10), kind=kOutput, calls=%fused_computation.7 | convolution fusion | flops 1073741824 | bytes 5242880 | tf_op jit(solution)/shard_map/dot_general | solution.py:160
  86.3 2.6 %copy.28 = f32[512,512]{1,0:T(8,128)} copy(f32[512,512]{0,1:T(8,128)} %convolution_bitcast_fusion) | data formatting | bytes 2097152 | tf_op jit(solution)/shard_map/dot_general | solution.py:160
  88.9 0.5 fusion.1
  89.4 0.6 copy-done.4
  90.0 0.5 fusion.3
  90.4 0.2 copy-done.6
  90.6 2.6 %pad_maximum_fusion = f32[128,64,128]{2,1,0:T(8,128)} fusion(f32[128,16,128]{2,1,0:T(8,128)S(1)} %bitcast.77, f32[128,16,128]{2,1,0:T(8,128)S(1)} %bitcast.70, f32[128,16,128]{2,1,0:T(8,128)S(1)} %bitcast.71, f32[128,16,128]{2,1,0:T(8,128)S(1)} %bitcast.69), kind=kLoop, calls=%fused_computation | loop fusion | flops 3145728 | bytes 8388608 | tf_op jit(solution)/shard_map/concatenate | solution.py:103
  93.3 5.9 %all-to-all-start.1 = ((f32[128,64,128]{2,1,0:T(8,128)}), f32[128,64,128]{2,1,0:T(8,128)}, u32[]{:S(2)}, u32[]{:S(2)}) async-start(f32[128,64,128]{2,1,0:T(8,128)} %pad_maximum_fusion), calls=%async_computation.1 | async-start | bytes 8388608 | tf_op jit(solution)/shard_map/all_to_all | solution.py:84
  99.2 0.0 copy-start.7
  99.2 0.5 fusion.16
  99.6 0.6 copy-done.3
  100.2 0.2 copy-done.7
  100.4 0.5 fusion
  100.8 0.3 reshape.138
  101.1 50.9 %all-to-all-done.1 = f32[128,64,128]{2,1,0:T(8,128)} async-done(((f32[128,64,128]{2,1,0:T(8,128)}), f32[128,64,128]{2,1,0:T(8,128)}, u32[]{:S(2)}, u32[]{:S(2)}) %all-to-all-start.1) | async-done | bytes 4194336 | tf_op jit(solution)/shard_map/all_to_all | solution.py:84
  152.1 2.5 %reduce_sum.9 = bf16[64,128]{1,0:T(8,128)(2,1)S(1)} reduce(f32[128,64,128]{2,1,0:T(8,128)} %all-to-all-done.1, f32[]{:T(128)} %constant.14.clone.1), dimensions={0}, to_apply=%region_2.3 | reduce | flops 1040384 | bytes 4210692 | tf_op jit(solution)/shard_map/reduce_sum | solution.py:104
  154.5 0.5 broadcast_in_dim.2
  155.1 1.7 pad_maximum_fusion.1
  156.8 5.4 %all-to-all-start.2 = ((bf16[128,80,128]{2,1,0:T(8,128)(2,1)}), bf16[128,80,128]{2,1,0:T(8,128)(2,1)}, u32[]{:S(2)}, u32[]{:S(2)}) async-start(bf16[128,80,128]{2,1,0:T(8,128)(2,1)} %pad_maximum_fusion.1), calls=%async_computation.2 | async-start | bytes 5242880 | tf_op jit(solution)/shard_map/all_to_all | solution.py:84
  162.2 0.1 fusion.7
  162.4 4.2 %convolution_convert_fusion = bf16[2048,512]{1,0:T(8,128)(2,1)} fusion(bf16[2048,512]{1,0:T(8,128)(2,1)} %get-tuple-element.10, bf16[512,512]{1,0:T(8,128)(2,1)S(1)} %copy-done.13), kind=kOutput, calls=%fused_computation.1 | convolution fusion | flops 1074790400 | bytes 4718592 | tf_op jit(solution)/shard_map/dot_general | solution.py:166
  166.6 31.6 %all-to-all-done.2 = bf16[128,80,128]{2,1,0:T(8,128)(2,1)} async-done(((bf16[128,80,128]{2,1,0:T(8,128)(2,1)}), bf16[128,80,128]{2,1,0:T(8,128)(2,1)}, u32[]{:S(2)}, u32[]{:S(2)}) %all-to-all-start.2) | async-done | bytes 2621472 | tf_op jit(solution)/shard_map/all_to_all | solution.py:84
  198.2 1.1 slice.34
  199.3 0.3 reshape.139
  199.6 2.0 slice_convert_fusion
  201.7 2.1 %fusion.14 = (f32[128,16,128]{2,1,0:T(8,128)}, f32[128,16,128]{2,1,0:T(8,128)}, f32[128,16,128]{2,1,0:T(8,128)}, f32[128,16,128]{2,1,0:T(8,128)}) fusion(f32[128,64,128]{2,1,0:T(8,128)S(1)} %slice_convert_fusion), kind=kLoop, calls=%fused_computation.29 | loop fusion | bytes 8388608 | tf_op jit(solution)/shard_map/slice | solution.py:112
  203.8 1.0 fusion.17
  (24 shorter events, 0.1 us)
Async XLA Ops:
  0.6 15.4 %copy-start = (bf16[2048,512]{1,0:T(8,128)(2,1)S(1)}, bf16[2048,512]{1,0:T(8,128)(2,1)}, u32[]{:S(2)}) copy-start(bf16[2048,512]{1,0:T(8,128)(2,1)} %param.9) | copy-start | bytes 6291460
  4.5 26.3 %all-to-all-start = ((bf16[128,4,640]{2,1,0:T(4,128)(2,1)}), bf16[128,4,640]{2,1,0:T(4,128)(2,1)S(1)}, u32[]{:S(2)}, u32[]{:S(2)}) async-start(bf16[128,4,640]{2,1,0:T(4,128)(2,1)} %all_to_all.14), calls=%async_computation | async-start | bytes 1310720 | tf_op jit(solution)/shard_map/all_to_all | solution.py:84
  16.0 3.8 %copy-start.9 = (bf16[2048,512]{1,0:T(8,128)(2,1)S(1)}, bf16[2048,512]{1,0:T(8,128)(2,1)}, u32[]{:S(2)}) copy-start(bf16[2048,512]{1,0:T(8,128)(2,1)} %param.8) | copy-start | bytes 6291460
  16.1 3.8 %copy-start.12 = (bf16[512,512]{1,0:T(8,128)(2,1)S(1)}, bf16[512,512]{1,0:T(8,128)(2,1)}, u32[]{:S(2)}) copy-start(bf16[512,512]{1,0:T(8,128)(2,1)} %param.12) | copy-start | bytes 1572868
  80.1 4.0 %copy-start.10 = (bf16[2048,512]{1,0:T(8,128)(2,1)S(1)}, bf16[2048,512]{1,0:T(8,128)(2,1)}, u32[]{:S(2)}) copy-start(bf16[2048,512]{1,0:T(8,128)(2,1)} %param.8) | copy-start | bytes 6291460
  80.1 4.0 %copy-start.11 = (bf16[2048,512]{1,0:T(8,128)(2,1)S(1)}, bf16[2048,512]{1,0:T(8,128)(2,1)}, u32[]{:S(2)}) copy-start(bf16[2048,512]{1,0:T(8,128)(2,1)} %get-tuple-element.10) | copy-start | bytes 6291460
  86.3 2.6 %copy-start.2 = (bf16[512,512]{1,0:T(8,128)(2,1)S(1)}, bf16[512,512]{1,0:T(8,128)(2,1)}, u32[]{:S(2)}) copy-start(bf16[512,512]{1,0:T(8,128)(2,1)} %get-tuple-element.12) | copy-start | bytes 1572868
  88.9 1.0 copy-start.4
  88.9 1.5 copy-start.1
  88.9 1.7 copy-start.6
  93.2 5.9 %copy-start.5 = (bf16[512,512]{1,0:T(8,128)(2,1)S(1)}, bf16[512,512]{1,0:T(8,128)(2,1)}, u32[]{:S(2)}) copy-start(bf16[512,512]{1,0:T(8,128)(2,1)} %get-tuple-element.11) | copy-start | bytes 1572868
  93.3 5.9 %copy-start.8 = (bf16[512,512]{1,0:T(8,128)(2,1)S(1)}, bf16[512,512]{1,0:T(8,128)(2,1)}, u32[]{:S(2)}) copy-start(bf16[512,512]{1,0:T(8,128)(2,1)} %param.13) | copy-start | bytes 1572868
  93.3 58.8 %all-to-all-start.1 = ((f32[128,64,128]{2,1,0:T(8,128)}), f32[128,64,128]{2,1,0:T(8,128)}, u32[]{:S(2)}, u32[]{:S(2)}) async-start(f32[128,64,128]{2,1,0:T(8,128)} %pad_maximum_fusion), calls=%async_computation.1 | async-start | bytes 8388608 | tf_op jit(solution)/shard_map/all_to_all | solution.py:84
  99.2 1.0 copy-start.3
  99.2 1.2 copy-start.7
  156.8 5.6 %copy-start.13 = (bf16[512,512]{1,0:T(8,128)(2,1)S(1)}, bf16[512,512]{1,0:T(8,128)(2,1)}, u32[]{:S(2)}) copy-start(bf16[512,512]{1,0:T(8,128)(2,1)} %param.12) | copy-start | bytes 1572868
  156.8 41.4 %all-to-all-start.2 = ((bf16[128,80,128]{2,1,0:T(8,128)(2,1)}), bf16[128,80,128]{2,1,0:T(8,128)(2,1)}, u32[]{:S(2)}, u32[]{:S(2)}) async-start(bf16[128,80,128]{2,1,0:T(8,128)(2,1)} %pad_maximum_fusion.1), calls=%async_computation.2 | async-start | bytes 5242880 | tf_op jit(solution)/shard_map/all_to_all | solution.py:84

commit v9 on v8

--- a/solution.py
+++ b/solution.py
@@ -18,7 +18,10 @@
     return (chosen, jnp.sum(named.astype(jnp.int32), axis=0))
 
 
-def attention_kernel(q_ref, g_ref, k_ref, v_ref, live_ref, o_ref, dq_ref, dk_ref, dv_ref, dk_acc, dv_acc):
+def attention_kernel(
+    q_ref, g_ref, k_ref, v_ref, live_ref, x_ref, c_ref,
+    o_ref, dq_ref, dk_ref, dv_ref, po_ref, pq_ref, dk_acc, dv_acc,
+):
     step = pl.program_id(0)
     width = q_ref.shape[1]
     head_size = width // HEADS
@@ -28,6 +31,8 @@
     def _():
         dk_acc[...] = jnp.zeros_like(dk_acc)
         dv_acc[...] = jnp.zeros_like(dv_acc)
+        po_ref[...] = jnp.zeros_like(po_ref)
+        pq_ref[...] = jnp.zeros_like(pq_ref)
 
     live = live_ref[...] > 0.5
     for h in range(HEADS):
@@ -52,13 +57,17 @@
         dk_acc[:, cols] += lax.dot_general(score_grad, q_h, tn, preferred_element_type=jnp.float32)
         dv_acc[:, cols] += lax.dot_general(prob_half, g_h, tn, preferred_element_type=jnp.float32)
 
+    tn = (((0,), (0,)), ((), ()))
+    po_ref[...] += lax.dot_general(o_ref[...], c_ref[...], tn, preferred_element_type=jnp.float32)
+    pq_ref[...] += lax.dot_general(x_ref[...], dq_ref[...], tn, preferred_element_type=jnp.float32)
+
     @pl.when(step == pl.num_programs(0) - 1)
     def _():
         dk_ref[...] = dk_acc[...].astype(dk_ref.dtype)
         dv_ref[...] = dv_acc[...].astype(dv_ref.dtype)
 
 
-def fused_attention(queries, out_grad, key_tile, value_tile, live, block=512):
+def fused_attention(queries, out_grad, key_tile, value_tile, live, grid_rows, upstream, block=512):
     rows, width = queries.shape
     slots = key_tile.shape[0]
     row_block = pl.BlockSpec((block, width), lambda i: (i, 0))
@@ -67,17 +76,22 @@
     return pl.pallas_call(
         attention_kernel,
         grid=(rows // block,),
-        in_specs=[row_block, row_block, slot_block, slot_block, live_block],
-        out_specs=[row_block, row_block, slot_block, slot_block],
+        in_specs=[row_block, row_block, slot_block, slot_block, live_block, row_block, row_block],
+        out_specs=[row_block, row_block, slot_block, slot_block, slot_block, slot_block],
         out_shape=[
             jax.ShapeDtypeStruct((rows, width), jnp.bfloat16),
             jax.ShapeDtypeStruct((rows, width), jnp.bfloat16),
             jax.ShapeDtypeStruct((slots, width), jnp.bfloat16),
             jax.ShapeDtypeStruct((slots, width), jnp.bfloat16),
+            jax.ShapeDtypeStruct((width, width), jnp.float32),
+            jax.ShapeDtypeStruct((width, width), jnp.float32),
         ],
         scratch_shapes=[pltpu.VMEM((slots, width), jnp.float32), pltpu.VMEM((slots, width), jnp.float32)],
         compiler_params=pltpu.CompilerParams(dimension_semantics=("arbitrary",)),
-    )(queries, out_grad, key_tile, value_tile, live.astype(jnp.float32).reshape(1, slots))
+    )(
+        queries, out_grad, key_tile, value_tile, live.astype(jnp.float32).reshape(1, slots),
+        grid_rows, upstream,
+    )
 
 
 def send_slots(outgoing):
@@ -149,15 +163,13 @@
     out_grad = jnp.dot(cotangent, output_weight.T, preferred_element_type=jnp.float32).astype(
         jnp.bfloat16
     )
-    attn_out, query_grad, key_grad, value_grad = fused_attention(
-        queries, out_grad, key_tile, value_tile, live_slots
+    attn_out, query_grad, key_grad, value_grad, part_output, part_query = fused_attention(
+        queries, out_grad, key_tile, value_tile, live_slots, grid_feat, cotangent
     )
     slot_trace = jnp.dot(key_grad, key_weight.T, preferred_element_type=jnp.float32)
     slot_trace = slot_trace + jnp.dot(
         value_grad, value_weight.T, preferred_element_type=jnp.float32
     )
-    part_output = jnp.dot(attn_out.T, cotangent, preferred_element_type=jnp.float32)
-    part_query = jnp.dot(grid_feat.T, query_grad, preferred_element_type=jnp.float32)
     part_key = jnp.dot(feat_tile.T, key_grad, preferred_element_type=jnp.float32)
     part_value = jnp.dot(feat_tile.T, value_grad, preferred_element_type=jnp.float32)
     (grad_query, grad_key, grad_value, grad_output), returned = sum_over_devices(

time: 205 us -> 198 us (0.966)
  matrix products: 25.5 us -> 20 us
  local copies, waits for them, and re-layouts: 10.1 us -> 7.55 us
  Pallas kernels: 43.9 us -> 46.3 us
    dot_general x2 -> x0, matrix products: 6.22 us -> none  [the longest x1 3.98 us: on_device(): jnp.dot(attn_out.T, cotangent, preferred_element_type=jnp.float32)]
    dot_general x1 -> x0, local copies, waits for them, and re-layouts: 2.59 us -> none  [on_device(): jnp.dot(grid_feat.T, query_grad, preferred_element_type=jnp.float32)]
    pallas_call x1, Pallas kernels: 43.9 us -> 46.3 us  [fused_attention(): pl.pallas_call(attention_kernel, grid=(rows // block,), in_specs=[row_blo...]
where the time goes in v9:
time: 198 us; the launch traced here: 197 us
  waiting for transfers between devices  91.4 us (46%)
  Pallas kernels  46.3 us (23%)
  starting transfers between devices  22 us (11%)
  matrix products  20 us (10%)
  other arithmetic  9.23 us (5%)
  local copies, waits for them, and re-layouts  7.55 us (4%)
    all_to_all x3, waiting for transfers between devices, send_slots(): lax.all_to_all(outgoing, ('inline', 'crosslin'), split_axis=0, concat_axi...  91.4 us
    pallas_call x1, Pallas kernels, fused_attention(): pl.pallas_call(attention_kernel, grid=(rows // block,), in_specs=[row_blo...  46.3 us
    all_to_all x3, starting transfers between devices, send_slots(): lax.all_to_all(outgoing, ('inline', 'crosslin'), split_axis=0, concat_axi...  22 us
    dot_general x1, matrix products, on_device(): jnp.dot(cotangent, output_weight.T, preferred_element_type=jnp.float32)  4.38 us
    dot_general x1, matrix products, on_device(): jnp.dot(query_grad, query_weight.T, preferred_element_type=jnp.float32)  4.2 us
  transfers between devices with their start and end apart: 3, of which 3 were waited for; matrix products, arithmetic and copies ran while one was open for 6% of the time, Pallas kernels for 0%

profile of v9, /device:TPU:1, one launch (start us, length us, event | category | flops | bytes accessed | tf_op | source)
XLA Modules:
  0.0 197.3 jit_solution(1853544497010176196)
XLA Ops:
  0.6 0.0 copy-start
  0.6 0.0 copy-start.9
  0.7 0.9 fusion.12
  1.5 0.1 copy.24
  1.7 0.2 reduce_window_sum.11
  1.9 0.1 copy.25
  2.0 0.1 eq.50
  2.1 0.1 and.22
  2.2 1.3 convolution_convert_fusion.3
  3.5 1.0 all_to_all.14
  4.5 11.5 %all-to-all-start = ((bf16[128,4,640]{2,1,0:T(4,128)(2,1)}), bf16[128,4,640]{2,1,0:T(4,128)(2,1)S(1)}, u32[]{:S(2)}, u32[]{:S(2)}) async-start(bf16[128,4,640]{2,1,0:T(4,128)(2,1)} %all_to_all.14), calls=%async_computation | async-start | bytes 1310720 | tf_op jit(solution)/shard_map/all_to_all | solution.py:98
  16.0 0.0 copy-done.9
  16.0 0.0 copy-start.1
  16.0 4.4 %convolution_convert_fusion.1.g_ref = bf16[2048,512]{1,0:T(8,128)(2,1)} fusion(bf16[2048,512]{1,0:T(8,128)(2,1)} %c_ref.1, bf16[512,512]{1,0:T(8,128)(2,1)S(1)} %copy-done.9), kind=kOutput, calls=%fused_computation.2 | convolution fusion | flops 1074790400 | bytes 4718592 | tf_op jit(solution)/shard_map/dot_general | solution.py:163
  20.4 0.0 copy-done
  20.4 0.0 copy-done.1
  20.4 2.6 %convolution_convert_fusion.2.q_ref = bf16[2048,512]{1,0:T(8,128)(2,1)} fusion(bf16[2048,512]{1,0:T(8,128)(2,1)S(1)} %copy-done.1, bf16[512,512]{1,0:T(8,128)(2,1)S(1)} %copy-done), kind=kOutput, calls=%fused_computation.3 | convolution fusion | flops 1074790400 | bytes 4718592 | tf_op jit(solution)/shard_map/dot_general | solution.py:160
  23.0 7.8 %all-to-all-done = bf16[128,4,640]{2,1,0:T(4,128)(2,1)S(1)} async-done(((bf16[128,4,640]{2,1,0:T(4,128)(2,1)}), bf16[128,4,640]{2,1,0:T(4,128)(2,1)S(1)}, u32[]{:S(2)}, u32[]{:S(2)}) %all-to-all-start) | async-done | bytes 655392 | tf_op jit(solution)/shard_map/all_to_all | solution.py:98
  30.8 0.1 all_to_all.16
  30.9 0.7 convert_reduce_fusion
  31.6 0.0 copy-done.7
  31.6 1.2 convolution_convert_fusion.4.v_ref
  32.9 0.0 copy-done.8
  32.9 1.2 convolution_convert_fusion.5.k_ref
  34.1 46.3 %shard_map.127 = (bf16[2048,512]{1,0:T(8,128)(2,1)}, bf16[2048,512]{1,0:T(8,128)(2,1)}, bf16[512,512]{1,0:T(8,128)(2,1)}, bf16[512,512]{1,0:T(8,128)(2,1)}, f32[512,512]{1,0:T(8,128)}, /*index=5*/f32[512,512]{1,0:T(8,128)}) custom-call(bf16[2048,512]{1,0:T(8,128)(2,1)} %convolution_convert_fusion.2.q_ref, bf16[2048,512]{1,0:T(8,128)(2,1)} %convolution_convert_fusion.1.g_ref, ...), custom_call_target="tpu_custom_call" | custom-call | tf_op jit(solution)/shard_map/pallas_call | solution.py:76
  80.4 0.0 copy-start.5
  80.4 0.0 copy-start.6
  80.5 1.6 fusion.1
  82.1 1.5 fusion.3
  83.6 0.0 copy-done.5
  83.6 2.6 %pad_maximum_fusion = f32[128,64,128]{2,1,0:T(8,128)} fusion(f32[128,16,128]{2,1,0:T(8,128)S(1)} %bitcast.70, f32[128,16,128]{2,1,0:T(8,128)S(1)} %bitcast.63, f32[128,16,128]{2,1,0:T(8,128)S(1)} %bitcast.64, f32[128,16,128]{2,1,0:T(8,128)S(1)} %bitcast.71), kind=kLoop, calls=%fused_computation | loop fusion | flops 3145728 | bytes 8388608 | tf_op jit(solution)/shard_map/concatenate | solution.py:117
  86.3 6.2 %all-to-all-start.1 = ((f32[128,64,128]{2,1,0:T(8,128)}), f32[128,64,128]{2,1,0:T(8,128)}, u32[]{:S(2)}, u32[]{:S(2)}) async-start(f32[128,64,128]{2,1,0:T(8,128)} %pad_maximum_fusion), calls=%async_computation.1 | async-start | bytes 8388608 | tf_op jit(solution)/shard_map/all_to_all | solution.py:98
  92.5 0.5 fusion.15
  92.9 0.5 fusion
  93.4 0.3 reshape.138
  93.7 51.7 %all-to-all-done.1 = f32[128,64,128]{2,1,0:T(8,128)} async-done(((f32[128,64,128]{2,1,0:T(8,128)}), f32[128,64,128]{2,1,0:T(8,128)}, u32[]{:S(2)}, u32[]{:S(2)}) %all-to-all-start.1) | async-done | bytes 4194336 | tf_op jit(solution)/shard_map/all_to_all | solution.py:98
  145.4 2.5 %reduce_sum.9 = bf16[64,128]{1,0:T(8,128)(2,1)S(1)} reduce(f32[128,64,128]{2,1,0:T(8,128)} %all-to-all-done.1, f32[]{:T(128)} %constant.14.clone.1), dimensions={0}, to_apply=%region_2.3 | reduce | flops 1040384 | bytes 4210692 | tf_op jit(solution)/shard_map/reduce_sum | solution.py:118
  147.9 0.5 broadcast_in_dim.2
  148.4 1.7 pad_maximum_fusion.1
  150.1 4.3 %all-to-all-start.2 = ((bf16[128,80,128]{2,1,0:T(8,128)(2,1)}), bf16[128,80,128]{2,1,0:T(8,128)(2,1)S(1)}, u32[]{:S(2)}, u32[]{:S(2)}) async-start(bf16[128,80,128]{2,1,0:T(8,128)(2,1)} %pad_maximum_fusion.1), calls=%async_computation.2 | async-start | bytes 5242880 | tf_op jit(solution)/shard_map/all_to_all | solution.py:98
  154.4 0.1 fusion.7
  154.5 4.2 %convolution_convert_fusion = bf16[2048,512]{1,0:T(8,128)(2,1)} fusion(bf16[2048,512]{1,0:T(8,128)(2,1)} %get-tuple-element.11, bf16[512,512]{1,0:T(8,128)(2,1)S(1)} %copy-done), kind=kOutput, calls=%fused_computation.1 | convolution fusion | flops 1074790400 | bytes 4718592 | tf_op jit(solution)/shard_map/dot_general | solution.py:178
  158.7 31.9 %all-to-all-done.2 = bf16[128,80,128]{2,1,0:T(8,128)(2,1)S(1)} async-done(((bf16[128,80,128]{2,1,0:T(8,128)(2,1)}), bf16[128,80,128]{2,1,0:T(8,128)(2,1)S(1)}, u32[]{:S(2)}, u32[]{:S(2)}) %all-to-all-start.2) | async-done | bytes 2621472 | tf_op jit(solution)/shard_map/all_to_all | solution.py:98
  190.7 0.8 slice.34
  191.5 2.1 %reshape.139 = bf16[512,512]{1,0:T(8,128)(2,1)} reshape(bf16[128,16,128]{2,1,0:T(8,128)(2,1)} %slice.34) | data formatting | bytes 1048576 | tf_op jit(solution)/shard_map/reshape | solution.py:129
  193.6 0.6 slice_convert_fusion
  194.2 2.1 %fusion.14 = (f32[128,16,128]{2,1,0:T(8,128)}, f32[128,16,128]{2,1,0:T(8,128)}, f32[128,16,128]{2,1,0:T(8,128)}, f32[128,16,128]{2,1,0:T(8,128)}) fusion(f32[128,64,128]{2,1,0:T(8,128)S(1)} %slice_convert_fusion), kind=kLoop, calls=%fused_computation.28 | loop fusion | bytes 8388608 | tf_op jit(solution)/shard_map/slice | solution.py:126
  196.4 1.0 fusion.16
  (13 shorter events, 0.1 us)
Async XLA Ops:
  0.6 19.8 %copy-start = (bf16[512,512]{1,0:T(8,128)(2,1)S(1)}, bf16[512,512]{1,0:T(8,128)(2,1)}, u32[]{:S(2)}) copy-start(bf16[512,512]{1,0:T(8,128)(2,1)} %param.12) | copy-start | bytes 1572868
  0.6 15.3 %copy-start.9 = (bf16[512,512]{1,0:T(8,128)(2,1)S(1)}, bf16[512,512]{1,0:T(8,128)(2,1)}, u32[]{:S(2)}) copy-start(bf16[512,512]{1,0:T(8,128)(2,1)} %param.15) | copy-start | bytes 1572868
  4.5 26.3 %all-to-all-start = ((bf16[128,4,640]{2,1,0:T(4,128)(2,1)}), bf16[128,4,640]{2,1,0:T(4,128)(2,1)S(1)}, u32[]{:S(2)}, u32[]{:S(2)}) async-start(bf16[128,4,640]{2,1,0:T(4,128)(2,1)} %all_to_all.14), calls=%async_computation | async-start | bytes 1310720 | tf_op jit(solution)/shard_map/all_to_all | solution.py:98
  16.0 4.4 %copy-start.1 = (bf16[2048,512]{1,0:T(8,128)(2,1)S(1)}, bf16[2048,512]{1,0:T(8,128)(2,1)}, u32[]{:S(2)}) copy-start(bf16[2048,512]{1,0:T(8,128)(2,1)} %x_ref.1) | copy-start | bytes 6291460
  20.4 11.2 %copy-start.7 = (bf16[512,512]{1,0:T(8,128)(2,1)S(1)}, bf16[512,512]{1,0:T(8,128)(2,1)}, u32[]{:S(2)}) copy-start(bf16[512,512]{1,0:T(8,128)(2,1)} %param.14) | copy-start | bytes 1572868
  23.0 9.9 %copy-start.8 = (bf16[512,512]{1,0:T(8,128)(2,1)S(1)}, bf16[512,512]{1,0:T(8,128)(2,1)}, u32[]{:S(2)}) copy-start(bf16[512,512]{1,0:T(8,128)(2,1)} %param.13) | copy-start | bytes 1572868
  80.4 3.2 %copy-start.5 = (f32[512,512]{1,0:T(8,128)S(1)}, f32[512,512]{1,0:T(8,128)}, u32[]{:S(2)}) copy-start(f32[512,512]{1,0:T(8,128)} %get-tuple-element.15) | copy-start | bytes 3145732
  80.4 3.2 %copy-start.6 = (f32[512,512]{1,0:T(8,128)S(1)}, f32[512,512]{1,0:T(8,128)}, u32[]{:S(2)}) copy-start(f32[512,512]{1,0:T(8,128)} %get-tuple-element.12) | copy-start | bytes 3145732
  86.3 6.2 %copy-start.4 = (bf16[512,512]{1,0:T(8,128)(2,1)S(1)}, bf16[512,512]{1,0:T(8,128)(2,1)}, u32[]{:S(2)}) copy-start(bf16[512,512]{1,0:T(8,128)(2,1)} %get-tuple-element.13) | copy-start | bytes 1572868
  86.3 6.7 %copy-start.2 = (bf16[512,512]{1,0:T(8,128)(2,1)S(1)}, bf16[512,512]{1,0:T(8,128)(2,1)}, u32[]{:S(2)}) copy-start(bf16[512,512]{1,0:T(8,128)(2,1)} %get-tuple-element.14) | copy-start | bytes 1572868
  86.3 59.1 %all-to-all-start.1 = ((f32[128,64,128]{2,1,0:T(8,128)}), f32[128,64,128]{2,1,0:T(8,128)}, u32[]{:S(2)}, u32[]{:S(2)}) async-start(f32[128,64,128]{2,1,0:T(8,128)} %pad_maximum_fusion), calls=%async_computation.1 | async-start | bytes 8388608 | tf_op jit(solution)/shard_map/all_to_all | solution.py:98
  150.1 40.6 %all-to-all-start.2 = ((bf16[128,80,128]{2,1,0:T(8,128)(2,1)}), bf16[128,80,128]{2,1,0:T(8,128)(2,1)S(1)}, u32[]{:S(2)}, u32[]{:S(2)}) async-start(bf16[128,80,128]{2,1,0:T(8,128)(2,1)} %pad_maximum_fusion.1), calls=%async_computation.2 | async-start | bytes 5242880 | tf_op jit(solution)/shard_map/all_to_all | solution.py:98
  194.2 2.1 %copy-start.3 = (bf16[512,512]{1,0:T(8,128)(2,1)S(1)}, bf16[512,512]{1,0:T(8,128)(2,1)}, u32[]{:S(2)}) copy-start(bf16[512,512]{1,0:T(8,128)(2,1)} %reshape.139) | copy-start | bytes 1572868

commit v10 on v9

--- a/solution.py
+++ b/solution.py
@@ -19,8 +19,8 @@
 
 
 def attention_kernel(
-    q_ref, g_ref, k_ref, v_ref, live_ref, x_ref, c_ref,
-    o_ref, dq_ref, dk_ref, dv_ref, po_ref, pq_ref, dk_acc, dv_acc,
+    q_ref, g_ref, f_ref, wk_ref, wv_ref, live_ref, x_ref, c_ref,
+    o_ref, dq_ref, dk_ref, dv_ref, po_ref, pq_ref, pk_ref, pv_ref, k_ref, v_ref, dk_acc, dv_acc,
 ):
     step = pl.program_id(0)
     width = q_ref.shape[1]
@@ -33,6 +33,9 @@
         dv_acc[...] = jnp.zeros_like(dv_acc)
         po_ref[...] = jnp.zeros_like(po_ref)
         pq_ref[...] = jnp.zeros_like(pq_ref)
+        feat = f_ref[...]
+        k_ref[...] = jnp.dot(feat, wk_ref[...], preferred_element_type=jnp.float32).astype(k_ref.dtype)
+        v_ref[...] = jnp.dot(feat, wv_ref[...], preferred_element_type=jnp.float32).astype(v_ref.dtype)
 
     live = live_ref[...] > 0.5
     for h in range(HEADS):
@@ -63,21 +66,34 @@
 
     @pl.when(step == pl.num_programs(0) - 1)
     def _():
-        dk_ref[...] = dk_acc[...].astype(dk_ref.dtype)
-        dv_ref[...] = dv_acc[...].astype(dv_ref.dtype)
-
-
-def fused_attention(queries, out_grad, key_tile, value_tile, live, grid_rows, upstream, block=512):
+        key_grad = dk_acc[...].astype(dk_ref.dtype)
+        value_grad = dv_acc[...].astype(dv_ref.dtype)
+        dk_ref[...] = key_grad
+        dv_ref[...] = value_grad
+        pk_ref[...] = lax.dot_general(f_ref[...], key_grad, tn, preferred_element_type=jnp.float32)
+        pv_ref[...] = lax.dot_general(f_ref[...], value_grad, tn, preferred_element_type=jnp.float32)
+
+
+def fused_attention(
+    queries, out_grad, feat_tile, key_weight, value_weight, live, grid_rows, upstream, block=512
+):
     rows, width = queries.shape
-    slots = key_tile.shape[0]
+    slots = feat_tile.shape[0]
     row_block = pl.BlockSpec((block, width), lambda i: (i, 0))
     slot_block = pl.BlockSpec((slots, width), lambda i: (0, 0))
     live_block = pl.BlockSpec((1, slots), lambda i: (0, 0))
+    weight_block = pl.BlockSpec((width, width), lambda i: (0, 0))
     return pl.pallas_call(
         attention_kernel,
         grid=(rows // block,),
-        in_specs=[row_block, row_block, slot_block, slot_block, live_block, row_block, row_block],
-        out_specs=[row_block, row_block, slot_block, slot_block, slot_block, slot_block],
+        in_specs=[
+            row_block, row_block, slot_block, weight_block, weight_block, live_block,
+            row_block, row_block,
+        ],
+        out_specs=[
+            row_block, row_block, slot_block, slot_block,
+            weight_block, weight_block, weight_block, weight_block,
+        ],
         out_shape=[
             jax.ShapeDtypeStruct((rows, width), jnp.bfloat16),
             jax.ShapeDtypeStruct((rows, width), jnp.bfloat16),
@@ -85,12 +101,19 @@
             jax.ShapeDtypeStruct((slots, width), jnp.bfloat16),
             jax.ShapeDtypeStruct((width, width), jnp.float32),
             jax.ShapeDtypeStruct((width, width), jnp.float32),
-        ],
-        scratch_shapes=[pltpu.VMEM((slots, width), jnp.float32), pltpu.VMEM((slots, width), jnp.float32)],
+            jax.ShapeDtypeStruct((width, width), jnp.float32),
+            jax.ShapeDtypeStruct((width, width), jnp.float32),
+        ],
+        scratch_shapes=[
+            pltpu.VMEM((slots, width), jnp.bfloat16),
+            pltpu.VMEM((slots, width), jnp.bfloat16),
+            pltpu.VMEM((slots, width), jnp.float32),
+            pltpu.VMEM((slots, width), jnp.float32),
+        ],
         compiler_params=pltpu.CompilerParams(dimension_semantics=("arbitrary",)),
     )(
-        queries, out_grad, key_tile, value_tile, live.astype(jnp.float32).reshape(1, slots),
-        grid_rows, upstream,
+        queries, out_grad, feat_tile, key_weight, value_weight,
+        live.astype(jnp.float32).reshape(1, slots), grid_rows, upstream,
     )
 
 
@@ -151,27 +174,20 @@
     arrived = send_slots(outgoing)
     feat_tile = arrived[:, :model_width]
     live_slots = arrived[:, model_width] > 0.5
-    key_tile = jnp.dot(feat_tile, key_weight, preferred_element_type=jnp.float32).astype(
-        jnp.bfloat16
-    )
-    value_tile = jnp.dot(feat_tile, value_weight, preferred_element_type=jnp.float32).astype(
-        jnp.bfloat16
-    )
     queries = jnp.dot(grid_feat, query_weight, preferred_element_type=jnp.float32).astype(
         jnp.bfloat16
     )
     out_grad = jnp.dot(cotangent, output_weight.T, preferred_element_type=jnp.float32).astype(
         jnp.bfloat16
     )
-    attn_out, query_grad, key_grad, value_grad, part_output, part_query = fused_attention(
-        queries, out_grad, key_tile, value_tile, live_slots, grid_feat, cotangent
-    )
+    outs = fused_attention(
+        queries, out_grad, feat_tile, key_weight, value_weight, live_slots, grid_feat, cotangent
+    )
+    attn_out, query_grad, key_grad, value_grad, part_output, part_query, part_key, part_value = outs
     slot_trace = jnp.dot(key_grad, key_weight.T, preferred_element_type=jnp.float32)
     slot_trace = slot_trace + jnp.dot(
         value_grad, value_weight.T, preferred_element_type=jnp.float32
     )
-    part_key = jnp.dot(feat_tile.T, key_grad, preferred_element_type=jnp.float32)
-    part_value = jnp.dot(feat_tile.T, value_grad, preferred_element_type=jnp.float32)
     (grad_query, grad_key, grad_value, grad_output), returned = sum_over_devices(
         (part_query, part_key, part_value, part_output), slot_trace.astype(jnp.bfloat16)
     )

time: 198 us -> 197 us (level)
  matrix products: 20 us -> 13.8 us
  other arithmetic: 9.23 us -> 11.4 us
  Pallas kernels: 46.3 us -> 48.4 us
    dot_general x4 -> x0, matrix products: 5.61 us -> none  [the longest x1 1.65 us: on_device(): jnp.dot(feat_tile.T, value_grad, preferred_element_type=jnp.float32)]
    concatenate x1, other arithmetic: 2.62 us -> 4.77 us  [sum_over_devices(): pieces = jnp.concatenate(tiled, axis=1)]
    pallas_call x1, Pallas kernels: 46.3 us -> 48.4 us  [fused_attention(): pl.pallas_call(attention_kernel, grid=(rows // block,), in_specs=[row_blo...]
where the time goes in v10:
time: 197 us; the launch traced here: 196 us
  waiting for transfers between devices  92 us (47%)
  Pallas kernels  48.4 us (25%)
  starting transfers between devices  21.7 us (11%)
  matrix products  13.8 us (7%)
  other arithmetic  11.4 us (6%)
  local copies, waits for them, and re-layouts  8.41 us (4%)
    all_to_all x3, waiting for transfers between devices, send_slots(): lax.all_to_all(outgoing, ('inline', 'crosslin'), split_axis=0, concat_axi...  92 us
    pallas_call x1, Pallas kernels, fused_attention(): pl.pallas_call(attention_kernel, grid=(rows // block,), in_specs=[row_blo...  48.4 us
    all_to_all x3, starting transfers between devices, send_slots(): lax.all_to_all(outgoing, ('inline', 'crosslin'), split_axis=0, concat_axi...  21.7 us
    concatenate x1, other arithmetic, sum_over_devices(): pieces = jnp.concatenate(tiled, axis=1)  4.77 us
    dot_general x1, matrix products, on_device(): jnp.dot(query_grad, query_weight.T, preferred_element_type=jnp.float32)  4.2 us
  transfers between devices with their start and end apart: 3, of which 3 were waited for; matrix products, arithmetic and copies ran while one was open for 6% of the time, Pallas kernels for 0%

profile of v10, /device:TPU:1, one launch (start us, length us, event | category | flops | bytes accessed | tf_op | source)
XLA Modules:
  0.0 196.5 jit_solution(16803956118900501596)
XLA Ops:
  0.6 0.0 copy-start
  0.6 0.0 copy-start.3
  0.7 0.9 fusion.6
  1.6 0.1 copy.20
  1.7 0.2 reduce_window_sum.11
  1.9 0.1 copy.21
  2.0 0.1 eq.50
  2.1 0.1 and.22
  2.3 1.3 convolution_convert_fusion.3
  3.6 1.0 all_to_all.14
  4.5 11.5 %all-to-all-start = ((bf16[128,4,640]{2,1,0:T(4,128)(2,1)}), bf16[128,4,640]{2,1,0:T(4,128)(2,1)S(1)}, u32[]{:S(2)}, u32[]{:S(2)}) async-start(bf16[128,4,640]{2,1,0:T(4,128)(2,1)} %all_to_all.14), calls=%async_computation | async-start | bytes 1310720 | tf_op jit(solution)/shard_map/all_to_all | solution.py:121
  16.0 0.0 copy-done.3
  16.1 0.0 copy-start.2
  16.1 3.8 %convolution_convert_fusion.1.g_ref = bf16[2048,512]{1,0:T(8,128)(2,1)} fusion(bf16[2048,512]{1,0:T(8,128)(2,1)S(1)} %copy-done.3, bf16[512,512]{1,0:T(8,128)(2,1)} %param.15), kind=kOutput, calls=%fused_computation.2 | convolution fusion | flops 1074790400 | bytes 4718592 | tf_op jit(solution)/shard_map/dot_general | solution.py:180
  19.9 0.0 copy-done
  19.9 0.0 copy-done.2
  19.9 2.6 %convolution_convert_fusion.2.q_ref = bf16[2048,512]{1,0:T(8,128)(2,1)} fusion(bf16[2048,512]{1,0:T(8,128)(2,1)S(1)} %copy-done.2, bf16[512,512]{1,0:T(8,128)(2,1)S(1)} %copy-done), kind=kOutput, calls=%fused_computation.3 | convolution fusion | flops 1074790400 | bytes 4718592 | tf_op jit(solution)/shard_map/dot_general | solution.py:177
  22.5 8.4 %all-to-all-done = bf16[128,4,640]{2,1,0:T(4,128)(2,1)S(1)} async-done(((bf16[128,4,640]{2,1,0:T(4,128)(2,1)}), bf16[128,4,640]{2,1,0:T(4,128)(2,1)S(1)}, u32[]{:S(2)}, u32[]{:S(2)}) %all-to-all-start) | async-done | bytes 655392 | tf_op jit(solution)/shard_map/all_to_all | solution.py:121
  30.8 0.1 all_to_all.16
  31.0 0.7 convert_reduce_fusion
  31.7 0.9 slice.32.f_ref
  32.6 48.4 %shard_map.127 = (bf16[2048,512]{1,0:T(8,128)(2,1)}, bf16[2048,512]{1,0:T(8,128)(2,1)}, bf16[512,512]{1,0:T(8,128)(2,1)}, bf16[512,512]{1,0:T(8,128)(2,1)}, f32[...) custom-call(bf16[2048,512]{1,0:T(8,128)(2,1)} %convolution_convert_fusion.2.q_ref, ...), custom_call_target="tpu_custom_call" | custom-call | tf_op jit(solution)/shard_map/pallas_call | solution.py:86
  81.0 4.8 %pad_maximum_fusion = f32[128,64,128]{2,1,0:T(8,128)} fusion(f32[128,16,128]{2,1,0:T(8,128)} %bitcast.64, f32[128,16,128]{2,1,0:T(8,128)} %bitcast.67, f32[128,16,128]{2,1,0:T(8,128)} %bitcast.66, f32[128,16,128]{2,1,0:T(8,128)} %bitcast.65), kind=kLoop, calls=%fused_computation | loop fusion | flops 3145728 | bytes 8388608 | tf_op jit(solution)/shard_map/concatenate | solution.py:140
  85.7 0.0 copy-start.5
  85.7 0.0 copy-start.7
  85.7 5.9 %all-to-all-start.1 = ((f32[128,64,128]{2,1,0:T(8,128)}), f32[128,64,128]{2,1,0:T(8,128)}, u32[]{:S(2)}, u32[]{:S(2)}) async-start(f32[128,64,128]{2,1,0:T(8,128)} %pad_maximum_fusion), calls=%async_computation.1 | async-start | bytes 8388608 | tf_op jit(solution)/shard_map/all_to_all | solution.py:121
  91.6 0.0 copy-done.5
  91.6 0.0 copy-done.7
  91.6 0.5 fusion.9
  92.1 0.0 copy-done.4
  92.1 0.0 copy-done.6
  92.1 0.5 fusion
  92.6 0.3 reshape.138
  92.9 51.6 %all-to-all-done.1 = f32[128,64,128]{2,1,0:T(8,128)} async-done(((f32[128,64,128]{2,1,0:T(8,128)}), f32[128,64,128]{2,1,0:T(8,128)}, u32[]{:S(2)}, u32[]{:S(2)}) %all-to-all-start.1) | async-done | bytes 4194336 | tf_op jit(solution)/shard_map/all_to_all | solution.py:121
  144.6 2.5 %reduce_sum.9 = bf16[64,128]{1,0:T(8,128)(2,1)S(1)} reduce(f32[128,64,128]{2,1,0:T(8,128)} %all-to-all-done.1, f32[]{:T(128)} %constant.14.clone.1), dimensions={0}, to_apply=%region_2.3 | reduce | flops 1040384 | bytes 4210692 | tf_op jit(solution)/shard_map/reduce_sum | solution.py:141
  147.0 0.5 broadcast_in_dim.2
  147.5 1.7 pad_maximum_fusion.1
  149.3 4.3 %all-to-all-start.2 = ((bf16[128,80,128]{2,1,0:T(8,128)(2,1)}), bf16[128,80,128]{2,1,0:T(8,128)(2,1)S(1)}, u32[]{:S(2)}, u32[]{:S(2)}) async-start(bf16[128,80,128]{2,1,0:T(8,128)(2,1)} %pad_maximum_fusion.1), calls=%async_computation.2 | async-start | bytes 5242880 | tf_op jit(solution)/shard_map/all_to_all | solution.py:121
  153.5 0.1 fusion.1
  153.7 4.2 %convolution_convert_fusion = bf16[2048,512]{1,0:T(8,128)(2,1)} fusion(bf16[2048,512]{1,0:T(8,128)(2,1)} %get-tuple-element.13, bf16[512,512]{1,0:T(8,128)(2,1)S(1)} %copy-done), kind=kOutput, calls=%fused_computation.1 | convolution fusion | flops 1074790400 | bytes 4718592 | tf_op jit(solution)/shard_map/dot_general | solution.py:194
  157.9 31.9 %all-to-all-done.2 = bf16[128,80,128]{2,1,0:T(8,128)(2,1)S(1)} async-done(((bf16[128,80,128]{2,1,0:T(8,128)(2,1)}), bf16[128,80,128]{2,1,0:T(8,128)(2,1)S(1)}, u32[]{:S(2)}, u32[]{:S(2)}) %all-to-all-start.2) | async-done | bytes 2621472 | tf_op jit(solution)/shard_map/all_to_all | solution.py:121
  189.8 0.8 slice.34
  190.6 2.2 %reshape.139 = bf16[512,512]{1,0:T(8,128)(2,1)} reshape(bf16[128,16,128]{2,1,0:T(8,128)(2,1)} %slice.34) | data formatting | bytes 1048576 | tf_op jit(solution)/shard_map/reshape | solution.py:152
  192.8 0.6 slice_convert_fusion
  193.4 0.0 copy-start.1
  193.4 2.1 %fusion.8 = (f32[128,16,128]{2,1,0:T(8,128)}, f32[128,16,128]{2,1,0:T(8,128)}, f32[128,16,128]{2,1,0:T(8,128)}, f32[128,16,128]{2,1,0:T(8,128)}) fusion(f32[128,64,128]{2,1,0:T(8,128)S(1)} %slice_convert_fusion), kind=kLoop, calls=%fused_computation.20 | loop fusion | bytes 8388608 | tf_op jit(solution)/shard_map/slice | solution.py:149
  195.5 0.0 copy-done.1
  195.5 1.0 fusion.10
  (6 shorter events, 0.1 us)
Async XLA Ops:
  0.6 19.2 %copy-start = (bf16[512,512]{1,0:T(8,128)(2,1)S(1)}, bf16[512,512]{1,0:T(8,128)(2,1)}, u32[]{:S(2)}) copy-start(bf16[512,512]{1,0:T(8,128)(2,1)} %param.12) | copy-start | bytes 1572868
  0.6 15.4 %copy-start.3 = (bf16[2048,512]{1,0:T(8,128)(2,1)S(1)}, bf16[2048,512]{1,0:T(8,128)(2,1)}, u32[]{:S(2)}) copy-start(bf16[2048,512]{1,0:T(8,128)(2,1)} %c_ref.1) | copy-start | bytes 6291460
  4.5 26.3 %all-to-all-start = ((bf16[128,4,640]{2,1,0:T(4,128)(2,1)}), bf16[128,4,640]{2,1,0:T(4,128)(2,1)S(1)}, u32[]{:S(2)}, u32[]{:S(2)}) async-start(bf16[128,4,640]{2,1,0:T(4,128)(2,1)} %all_to_all.14), calls=%async_computation | async-start | bytes 1310720 | tf_op jit(solution)/shard_map/all_to_all | solution.py:121
  16.1 3.8 %copy-start.2 = (bf16[2048,512]{1,0:T(8,128)(2,1)S(1)}, bf16[2048,512]{1,0:T(8,128)(2,1)}, u32[]{:S(2)}) copy-start(bf16[2048,512]{1,0:T(8,128)(2,1)} %x_ref.1) | copy-start | bytes 6291460
  85.7 5.9 %copy-start.5 = (bf16[512,512]{1,0:T(8,128)(2,1)S(1)}, bf16[512,512]{1,0:T(8,128)(2,1)}, u32[]{:S(2)}) copy-start(bf16[512,512]{1,0:T(8,128)(2,1)} %wk_ref.1) | copy-start | bytes 1572868
  85.7 5.9 %copy-start.7 = (bf16[512,512]{1,0:T(8,128)(2,1)S(1)}, bf16[512,512]{1,0:T(8,128)(2,1)}, u32[]{:S(2)}) copy-start(bf16[512,512]{1,0:T(8,128)(2,1)} %get-tuple-element.18) | copy-start | bytes 1572868
  85.7 6.4 %copy-start.4 = (bf16[512,512]{1,0:T(8,128)(2,1)S(1)}, bf16[512,512]{1,0:T(8,128)(2,1)}, u32[]{:S(2)}) copy-start(bf16[512,512]{1,0:T(8,128)(2,1)} %wv_ref.1) | copy-start | bytes 1572868
  85.7 6.4 %copy-start.6 = (bf16[512,512]{1,0:T(8,128)(2,1)S(1)}, bf16[512,512]{1,0:T(8,128)(2,1)}, u32[]{:S(2)}) copy-start(bf16[512,512]{1,0:T(8,128)(2,1)} %get-tuple-element.19) | copy-start | bytes 1572868
  85.7 58.8 %all-to-all-start.1 = ((f32[128,64,128]{2,1,0:T(8,128)}), f32[128,64,128]{2,1,0:T(8,128)}, u32[]{:S(2)}, u32[]{:S(2)}) async-start(f32[128,64,128]{2,1,0:T(8,128)} %pad_maximum_fusion), calls=%async_computation.1 | async-start | bytes 8388608 | tf_op jit(solution)/shard_map/all_to_all | solution.py:121
  149.3 40.6 %all-to-all-start.2 = ((bf16[128,80,128]{2,1,0:T(8,128)(2,1)}), bf16[128,80,128]{2,1,0:T(8,128)(2,1)S(1)}, u32[]{:S(2)}, u32[]{:S(2)}) async-start(bf16[128,80,128]{2,1,0:T(8,128)(2,1)} %pad_maximum_fusion.1), calls=%async_computation.2 | async-start | bytes 5242880 | tf_op jit(solution)/shard_map/all_to_all | solution.py:121
  193.4 2.1 %copy-start.1 = (bf16[512,512]{1,0:T(8,128)(2,1)S(1)}, bf16[512,512]{1,0:T(8,128)(2,1)}, u32[]{:S(2)}) copy-start(bf16[512,512]{1,0:T(8,128)(2,1)} %reshape.139) | copy-start | bytes 1572868

commit v11 on v10

--- a/solution.py
+++ b/solution.py
@@ -20,7 +20,8 @@
 
 def attention_kernel(
     q_ref, g_ref, f_ref, wk_ref, wv_ref, live_ref, x_ref, c_ref,
-    o_ref, dq_ref, dk_ref, dv_ref, po_ref, pq_ref, pk_ref, pv_ref, k_ref, v_ref, dk_acc, dv_acc,
+    o_ref, dq_ref, dk_ref, dv_ref, pieces_ref,
+    k_ref, v_ref, dk_acc, dv_acc, pq_ref, pk_ref, pv_ref, po_ref,
 ):
     step = pl.program_id(0)
     width = q_ref.shape[1]
@@ -72,10 +73,25 @@
         dv_ref[...] = value_grad
         pk_ref[...] = lax.dot_general(f_ref[...], key_grad, tn, preferred_element_type=jnp.float32)
         pv_ref[...] = lax.dot_general(f_ref[...], value_grad, tn, preferred_element_type=jnp.float32)
+        parts = (pq_ref, pk_ref, pv_ref, po_ref)
+        col_tiles = width // 128
+        per_device = (width // 8) * col_tiles // pieces_ref.shape[0]
+        depth = 8 * per_device
+
+        def scatter_row(r, carry):
+            for c in range(col_tiles):
+                tile = r * col_tiles + c
+                for i, part in enumerate(parts):
+                    pieces_ref[tile // per_device, pl.ds(i * depth + (c % per_device) * 8, 8), :] = (
+                        part[pl.ds(r * 8, 8), pl.ds(c * 128, 128)]
+                    )
+            return carry
+
+        lax.fori_loop(0, width // 8, scatter_row, 0)
 
 
 def fused_attention(
-    queries, out_grad, feat_tile, key_weight, value_weight, live, grid_rows, upstream, block=512
+    queries, out_grad, feat_tile, key_weight, value_weight, live, grid_rows, upstream, count, block=512
 ):
     rows, width = queries.shape
     slots = feat_tile.shape[0]
@@ -83,6 +99,7 @@
     slot_block = pl.BlockSpec((slots, width), lambda i: (0, 0))
     live_block = pl.BlockSpec((1, slots), lambda i: (0, 0))
     weight_block = pl.BlockSpec((width, width), lambda i: (0, 0))
+    depth = 4 * width * width // (count * 128)
     return pl.pallas_call(
         attention_kernel,
         grid=(rows // block,),
@@ -92,23 +109,24 @@
         ],
         out_specs=[
             row_block, row_block, slot_block, slot_block,
-            weight_block, weight_block, weight_block, weight_block,
+            pl.BlockSpec((count, depth, 128), lambda i: (0, 0, 0)),
         ],
         out_shape=[
             jax.ShapeDtypeStruct((rows, width), jnp.bfloat16),
             jax.ShapeDtypeStruct((rows, width), jnp.bfloat16),
             jax.ShapeDtypeStruct((slots, width), jnp.bfloat16),
             jax.ShapeDtypeStruct((slots, width), jnp.bfloat16),
-            jax.ShapeDtypeStruct((width, width), jnp.float32),
-            jax.ShapeDtypeStruct((width, width), jnp.float32),
-            jax.ShapeDtypeStruct((width, width), jnp.float32),
-            jax.ShapeDtypeStruct((width, width), jnp.float32),
+            jax.ShapeDtypeStruct((count, depth, 128), jnp.float32),
         ],
         scratch_shapes=[
             pltpu.VMEM((slots, width), jnp.bfloat16),
             pltpu.VMEM((slots, width), jnp.bfloat16),
             pltpu.VMEM((slots, width), jnp.float32),
             pltpu.VMEM((slots, width), jnp.float32),
+            pltpu.VMEM((width, width), jnp.float32),
+            pltpu.VMEM((width, width), jnp.float32),
+            pltpu.VMEM((width, width), jnp.float32),
+            pltpu.VMEM((width, width), jnp.float32),
         ],
         compiler_params=pltpu.CompilerParams(dimension_semantics=("arbitrary",)),
     )(
@@ -124,20 +142,13 @@
     return arrived
 
 
-def as_tiles(part):
-    rows, cols = part.shape
-    return part.reshape(rows // 8, 8, cols // 128, 128).transpose(0, 2, 1, 3)
-
-
 def from_tiles(tiles, shape):
     return tiles.reshape(shape[0] // 8, shape[1] // 128, 8, 128).transpose(0, 2, 1, 3).reshape(shape)
 
 
-def sum_over_devices(parts, rider):
-    count = lax.axis_size("inline") * lax.axis_size("crosslin")
-    tiled = [as_tiles(part).reshape(count, -1, 128) for part in parts]
-    depth = tiled[0].shape[1]
-    pieces = jnp.concatenate(tiled, axis=1)
+def sum_over_devices(pieces, shape, rider):
+    count = pieces.shape[0]
+    depth = pieces.shape[1] // 4
     mine = send_slots(pieces).sum(axis=0, keepdims=True).astype(jnp.bfloat16)
     rider_rows = rider.size // (count * 128)
     payload = jnp.concatenate(
@@ -145,10 +156,7 @@
     )
     arrived = send_slots(payload)
     gathered = arrived[:, : pieces.shape[1]].astype(jnp.float32)
-    sums = tuple(
-        from_tiles(gathered[:, i * depth : (i + 1) * depth], part.shape)
-        for i, part in enumerate(parts)
-    )
+    sums = tuple(from_tiles(gathered[:, i * depth : (i + 1) * depth], shape) for i in range(4))
     return sums, arrived[:, pieces.shape[1] :].reshape(rider.shape)
 
 
@@ -180,16 +188,16 @@
     out_grad = jnp.dot(cotangent, output_weight.T, preferred_element_type=jnp.float32).astype(
         jnp.bfloat16
     )
-    outs = fused_attention(
-        queries, out_grad, feat_tile, key_weight, value_weight, live_slots, grid_feat, cotangent
-    )
-    attn_out, query_grad, key_grad, value_grad, part_output, part_query, part_key, part_value = outs
+    attn_out, query_grad, key_grad, value_grad, pieces = fused_attention(
+        queries, out_grad, feat_tile, key_weight, value_weight, live_slots, grid_feat, cotangent,
+        tile_count,
+    )
     slot_trace = jnp.dot(key_grad, key_weight.T, preferred_element_type=jnp.float32)
     slot_trace = slot_trace + jnp.dot(
         value_grad, value_weight.T, preferred_element_type=jnp.float32
     )
     (grad_query, grad_key, grad_value, grad_output), returned = sum_over_devices(
-        (part_query, part_key, part_value, part_output), slot_trace.astype(jnp.bfloat16)
+        pieces, (model_width, model_width), slot_trace.astype(jnp.bfloat16)
     )
     grad_grid = jnp.dot(query_grad, query_weight.T, preferred_element_type=jnp.float32).astype(
         jnp.bfloat16

time: 197 us -> 194 us (0.985)
  other arithmetic: 11.4 us -> 6.56 us
    concatenate x1 -> x0, other arithmetic: 4.77 us -> none  [sum_over_devices(): pieces = jnp.concatenate(tiled, axis=1)]
where the time goes in v11:
time: 194 us
  waiting for transfers between devices  91.3 us (47%)
  Pallas kernels  50 us (26%)
  starting transfers between devices  21.9 us (11%)
  matrix products  13.9 us (7%)
  local copies, waits for them, and re-layouts  9.07 us (5%)
  other arithmetic  6.56 us (3%)
    all_to_all x3, waiting for transfers between devices, send_slots(): lax.all_to_all(outgoing, ('inline', 'crosslin'), split_axis=0, concat_axi...  91.3 us
    pallas_call x1, Pallas kernels, fused_attention(): pl.pallas_call(attention_kernel, grid=(rows // block,), in_specs=[row_blo...  50 us
    all_to_all x3, starting transfers between devices, send_slots(): lax.all_to_all(outgoing, ('inline', 'crosslin'), split_axis=0, concat_axi...  21.9 us
    dot_general x1, matrix products, on_device(): jnp.dot(query_grad, query_weight.T, preferred_element_type=jnp.float32)  4.2 us
  transfers between devices with their start and end apart: 3, of which 3 were waited for; matrix products, arithmetic and copies ran while one was open for 6% of the time, Pallas kernels for 0%

profile of v11, /device:TPU:1, one launch (start us, length us, event | category | flops | bytes accessed | tf_op | source)
XLA Modules:
  0.0 193.5 jit_solution(15307882509293647708)
XLA Ops:
  0.6 0.0 copy-start
  0.6 0.8 fusion.6
  1.5 0.1 copy.20
  1.6 0.2 reduce_window_sum.11
  1.8 0.1 copy.21
  1.9 0.0 copy-start.3
  1.9 0.1 eq.50
  2.0 0.1 and.22
  2.2 1.4 convolution_convert_fusion.3
  3.6 1.0 all_to_all.14
  4.6 11.5 %all-to-all-start = ((bf16[128,4,640]{2,1,0:T(4,128)(2,1)}), bf16[128,4,640]{2,1,0:T(4,128)(2,1)S(1)}, u32[]{:S(2)}, u32[]{:S(2)}) async-start(bf16[128,4,640]{2,1,0:T(4,128)(2,1)} %all_to_all.14), calls=%async_computation | async-start | bytes 1310720 | tf_op jit(solution)/shard_map/all_to_all | solution.py:139
  16.1 0.0 copy-done.3
  16.1 0.0 copy-start.2
  16.1 3.8 %convolution_convert_fusion.1.g_ref = bf16[2048,512]{1,0:T(8,128)(2,1)} fusion(bf16[2048,512]{1,0:T(8,128)(2,1)S(1)} %copy-done.3, bf16[512,512]{1,0:T(8,128)(2,1)} %param.15), kind=kOutput, calls=%fused_computation.1 | convolution fusion | flops 1074790400 | bytes 4718592 | tf_op jit(solution)/shard_map/dot_general | solution.py:188
  19.9 0.0 copy-done
  19.9 0.0 copy-done.2
  19.9 2.6 %convolution_convert_fusion.2.q_ref = bf16[2048,512]{1,0:T(8,128)(2,1)} fusion(bf16[2048,512]{1,0:T(8,128)(2,1)S(1)} %copy-done.2, bf16[512,512]{1,0:T(8,128)(2,1)S(1)} %copy-done), kind=kOutput, calls=%fused_computation.2 | convolution fusion | flops 1074790400 | bytes 4718592 | tf_op jit(solution)/shard_map/dot_general | solution.py:185
  22.5 8.4 %all-to-all-done = bf16[128,4,640]{2,1,0:T(4,128)(2,1)S(1)} async-done(((bf16[128,4,640]{2,1,0:T(4,128)(2,1)}), bf16[128,4,640]{2,1,0:T(4,128)(2,1)S(1)}, u32[]{:S(2)}, u32[]{:S(2)}) %all-to-all-start) | async-done | bytes 655392 | tf_op jit(solution)/shard_map/all_to_all | solution.py:139
  30.9 0.1 all_to_all.16
  31.0 0.7 convert_reduce_fusion
  31.7 0.8 slice.32.f_ref
  32.6 50.0 %shard_map.127 = (bf16[2048,512]{1,0:T(8,128)(2,1)}, bf16[2048,512]{1,0:T(8,128)(2,1)}, bf16[512,512]{1,0:T(8,128)(2,1)}, bf16[512,512]{1,0:T(8,128)(2,1)}, f32[128,64,128]{2,1,0:T(8,128)}) custom-call(bf16[2048,512]{1,0:T(8,128)(2,1)} %convolution_convert_fusion.2.q_ref, bf16[2048,512]{1,0:T(8,128)(2,1)} %convolution_convert_fusion.1.g_ref, ...), custom_call_target="tpu_custom_call" | custom-call | tf_op jit(solution)/shard_map/pallas_call | solution.py:103
  82.5 0.0 copy-start.5
  82.5 0.0 copy-start.7
  82.5 6.1 %all-to-all-start.1 = ((f32[128,64,128]{2,1,0:T(8,128)}), f32[128,64,128]{2,1,0:T(8,128)}, u32[]{:S(2)}, u32[]{:S(2)}) async-start(f32[128,64,128]{2,1,0:T(8,128)} %get-tuple-element.11), calls=%async_computation.1 | async-start | bytes 8388608 | tf_op jit(solution)/shard_map/all_to_all | solution.py:139
  88.7 0.0 copy-start.4
  88.7 0.0 copy-start.6
  88.7 0.0 copy-done.5
  88.7 0.0 copy-done.7
  88.7 0.5 fusion.9
  89.2 0.5 copy-done.4
  89.7 0.2 copy-done.6
  89.9 0.5 fusion
  90.3 0.3 reshape.106
  90.7 50.9 %all-to-all-done.1 = f32[128,64,128]{2,1,0:T(8,128)} async-done(((f32[128,64,128]{2,1,0:T(8,128)}), f32[128,64,128]{2,1,0:T(8,128)}, u32[]{:S(2)}, u32[]{:S(2)}) %all-to-all-start.1) | async-done | bytes 4194336 | tf_op jit(solution)/shard_map/all_to_all | solution.py:139
  141.6 2.5 %reduce_sum.9 = bf16[64,128]{1,0:T(8,128)(2,1)S(1)} reduce(f32[128,64,128]{2,1,0:T(8,128)} %all-to-all-done.1, f32[]{:T(128)} %constant.14.clone.1), dimensions={0}, to_apply=%region_2.3 | reduce | flops 1040384 | bytes 4210692 | tf_op jit(solution)/shard_map/reduce_sum | solution.py:152
  144.1 0.5 broadcast_in_dim.2
  144.6 1.7 pad_maximum_fusion
  146.3 4.3 %all-to-all-start.2 = ((bf16[128,80,128]{2,1,0:T(8,128)(2,1)}), bf16[128,80,128]{2,1,0:T(8,128)(2,1)S(1)}, u32[]{:S(2)}, u32[]{:S(2)}) async-start(bf16[128,80,128]{2,1,0:T(8,128)(2,1)} %pad_maximum_fusion), calls=%async_computation.2 | async-start | bytes 5242880 | tf_op jit(solution)/shard_map/all_to_all | solution.py:139
  150.6 0.1 fusion.1
  150.7 4.2 %convolution_convert_fusion = bf16[2048,512]{1,0:T(8,128)(2,1)} fusion(bf16[2048,512]{1,0:T(8,128)(2,1)} %get-tuple-element.10, bf16[512,512]{1,0:T(8,128)(2,1)S(1)} %copy-done), kind=kOutput, calls=%fused_computation | convolution fusion | flops 1074790400 | bytes 4718592 | tf_op jit(solution)/shard_map/dot_general | solution.py:202
  154.9 31.9 %all-to-all-done.2 = bf16[128,80,128]{2,1,0:T(8,128)(2,1)S(1)} async-done(((bf16[128,80,128]{2,1,0:T(8,128)(2,1)}), bf16[128,80,128]{2,1,0:T(8,128)(2,1)S(1)}, u32[]{:S(2)}, u32[]{:S(2)}) %all-to-all-start.2) | async-done | bytes 2621472 | tf_op jit(solution)/shard_map/all_to_all | solution.py:139
  186.8 0.8 slice.34
  187.7 2.2 %reshape.107 = bf16[512,512]{1,0:T(8,128)(2,1)} reshape(bf16[128,16,128]{2,1,0:T(8,128)(2,1)} %slice.34) | data formatting | bytes 1048576 | tf_op jit(solution)/shard_map/reshape | solution.py:160
  189.8 0.6 slice_convert_fusion
  190.4 0.0 copy-start.1
  190.4 2.1 %fusion.8 = (f32[128,16,128]{2,1,0:T(8,128)}, f32[128,16,128]{2,1,0:T(8,128)}, f32[128,16,128]{2,1,0:T(8,128)}, f32[128,16,128]{2,1,0:T(8,128)}) fusion(f32[128,64,128]{2,1,0:T(8,128)S(1)} %slice_convert_fusion), kind=kLoop, calls=%fused_computation.19 | loop fusion | bytes 8388608 | tf_op jit(solution)/shard_map/slice | solution.py:159
  192.5 1.0 fusion.10
  (5 shorter events, 0.1 us)
Async XLA Ops:
  0.6 19.3 %copy-start = (bf16[512,512]{1,0:T(8,128)(2,1)S(1)}, bf16[512,512]{1,0:T(8,128)(2,1)}, u32[]{:S(2)}) copy-start(bf16[512,512]{1,0:T(8,128)(2,1)} %param.12) | copy-start | bytes 1572868
  1.9 14.2 %copy-start.3 = (bf16[2048,512]{1,0:T(8,128)(2,1)S(1)}, bf16[2048,512]{1,0:T(8,128)(2,1)}, u32[]{:S(2)}) copy-start(bf16[2048,512]{1,0:T(8,128)(2,1)} %c_ref.1) | copy-start | bytes 6291460
  4.6 26.3 %all-to-all-start = ((bf16[128,4,640]{2,1,0:T(4,128)(2,1)}), bf16[128,4,640]{2,1,0:T(4,128)(2,1)S(1)}, u32[]{:S(2)}, u32[]{:S(2)}) async-start(bf16[128,4,640]{2,1,0:T(4,128)(2,1)} %all_to_all.14), calls=%async_computation | async-start | bytes 1310720 | tf_op jit(solution)/shard_map/all_to_all | solution.py:139
  16.1 3.8 %copy-start.2 = (bf16[2048,512]{1,0:T(8,128)(2,1)S(1)}, bf16[2048,512]{1,0:T(8,128)(2,1)}, u32[]{:S(2)}) copy-start(bf16[2048,512]{1,0:T(8,128)(2,1)} %x_ref.1) | copy-start | bytes 6291460
  82.5 6.2 %copy-start.5 = (bf16[512,512]{1,0:T(8,128)(2,1)S(1)}, bf16[512,512]{1,0:T(8,128)(2,1)}, u32[]{:S(2)}) copy-start(bf16[512,512]{1,0:T(8,128)(2,1)} %wk_ref.1) | copy-start | bytes 1572868
  82.5 6.2 %copy-start.7 = (bf16[512,512]{1,0:T(8,128)(2,1)S(1)}, bf16[512,512]{1,0:T(8,128)(2,1)}, u32[]{:S(2)}) copy-start(bf16[512,512]{1,0:T(8,128)(2,1)} %get-tuple-element.12) | copy-start | bytes 1572868
  82.5 59.1 %all-to-all-start.1 = ((f32[128,64,128]{2,1,0:T(8,128)}), f32[128,64,128]{2,1,0:T(8,128)}, u32[]{:S(2)}, u32[]{:S(2)}) async-start(f32[128,64,128]{2,1,0:T(8,128)} %get-tuple-element.11), calls=%async_computation.1 | async-start | bytes 8388608 | tf_op jit(solution)/shard_map/all_to_all | solution.py:139
  88.7 1.0 copy-start.4
  88.7 1.2 copy-start.6
  146.3 40.6 %all-to-all-start.2 = ((bf16[128,80,128]{2,1,0:T(8,128)(2,1)}), bf16[128,80,128]{2,1,0:T(8,128)(2,1)S(1)}, u32[]{:S(2)}, u32[]{:S(2)}) async-start(bf16[128,80,128]{2,1,0:T(8,128)(2,1)} %pad_maximum_fusion), calls=%async_computation.2 | async-start | bytes 5242880 | tf_op jit(solution)/shard_map/all_to_all | solution.py:139
  190.4 2.1 %copy-start.1 = (bf16[512,512]{1,0:T(8,128)(2,1)S(1)}, bf16[512,512]{1,0:T(8,128)(2,1)}, u32[]{:S(2)}) copy-start(bf16[512,512]{1,0:T(8,128)(2,1)} %reshape.107) | copy-start | bytes 1572868

commit v12 on v11

--- a/solution.py
+++ b/solution.py
@@ -91,7 +91,7 @@
 
 
 def fused_attention(
-    queries, out_grad, feat_tile, key_weight, value_weight, live, grid_rows, upstream, count, block=512
+    queries, out_grad, feat_tile, key_weight, value_weight, live, grid_rows, upstream, count, block=1024
 ):
     rows, width = queries.shape
     slots = feat_tile.shape[0]
@@ -157,7 +157,7 @@
     arrived = send_slots(payload)
     gathered = arrived[:, : pieces.shape[1]].astype(jnp.float32)
     sums = tuple(from_tiles(gathered[:, i * depth : (i + 1) * depth], shape) for i in range(4))
-    return sums, arrived[:, pieces.shape[1] :].reshape(rider.shape)
+    return sums, arrived[:, pieces.shape[1] :].reshape(count * rider_rows, 128)
 
 
 def on_device(
@@ -202,7 +202,14 @@
     grad_grid = jnp.dot(query_grad, query_weight.T, preferred_element_type=jnp.float32).astype(
         jnp.bfloat16
     )
-    grad_trace = jnp.dot(picker.T, returned, preferred_element_type=jnp.float32)
+    col_blocks = model_width // 128
+    spread = picker.reshape(tile_count * capacity, 1, 1, trace_rows) * jnp.eye(
+        col_blocks, dtype=picker.dtype
+    )[None, :, :, None]
+    spread = spread.reshape(tile_count * capacity * col_blocks, col_blocks, trace_rows)
+    grad_trace = jnp.einsum(
+        "kcr,kl->rcl", spread, returned, preferred_element_type=jnp.float32
+    ).reshape(trace_rows, model_width)
     return (grad_grid, grad_trace, grad_query, grad_key, grad_value, grad_output)
 
 

time: 194 us -> 193 us (level)
  waiting for transfers between devices: 91.3 us -> 88.7 us
    mul x0 -> x3, local copies, waits for them, and re-layouts: none -> 2.81 us  [on_device(): picker.reshape(tile_count * capacity, 1, 1, trace_rows)]
    all_to_all x3, waiting for transfers between devices: 91.3 us -> 88.7 us  [send_slots(): lax.all_to_all(outgoing, ('inline', 'crosslin'), split_axis=0, concat_axi...]
    reshape x1 -> x0, local copies, waits for them, and re-layouts: 2.15 us -> none  [sum_over_devices(): return (sums, arrived[:, pieces.shape[1]:].reshape(rider.shape))]
  transfers between devices with their start and end apart: 3 -> 3, of which waited for: 3 -> 3; matrix products, arithmetic and copies ran while one was open for 6% -> 8% of each run, Pallas kernels for 0% -> 0%
where the time goes in v12:
time: 193 us
  waiting for transfers between devices  88.7 us (46%)
  Pallas kernels  50.6 us (26%)
  starting transfers between devices  21.7 us (11%)
  matrix products  14.3 us (7%)
  local copies, waits for them, and re-layouts  9.77 us (5%)
  other arithmetic  6.59 us (3%)
    all_to_all x3, waiting for transfers between devices, send_slots(): lax.all_to_all(outgoing, ('inline', 'crosslin'), split_axis=0, concat_axi...  88.7 us
    pallas_call x1, Pallas kernels, fused_attention(): pl.pallas_call(attention_kernel, grid=(rows // block,), in_specs=[row_blo...  50.6 us
    all_to_all x3, starting transfers between devices, send_slots(): lax.all_to_all(outgoing, ('inline', 'crosslin'), split_axis=0, concat_axi...  21.7 us
    dot_general x1, matrix products, on_device(): jnp.dot(query_grad, query_weight.T, preferred_element_type=jnp.float32)  4.2 us
  transfers between devices with their start and end apart: 3, of which 3 were waited for; matrix products, arithmetic and copies ran while one was open for 8% of the time, Pallas kernels for 0%

profile of v12, /device:TPU:1, one launch (start us, length us, event | category | flops | bytes accessed | tf_op | source)
XLA Modules:
  0.0 192.5 jit_solution(9275231751135424863)
XLA Ops:
  0.6 0.0 copy-start
  0.6 0.8 fusion.6
  1.5 0.2 reduce_window_sum.11
  1.7 0.1 copy.29
  1.8 0.1 copy.28
  1.9 0.1 eq.50
  2.1 0.0 copy-start.2
  2.1 0.1 and.15
  2.2 0.1 fusion.9
  2.3 1.4 convolution_convert_fusion.3
  3.7 1.0 all_to_all.14
  4.7 11.5 %all-to-all-start = ((bf16[128,4,640]{2,1,0:T(4,128)(2,1)}), bf16[128,4,640]{2,1,0:T(4,128)(2,1)S(1)}, u32[]{:S(2)}, u32[]{:S(2)}) async-start(bf16[128,4,640]{2,1,0:T(4,128)(2,1)} %all_to_all.14), calls=%async_computation | async-start | bytes 1310720 | tf_op jit(solution)/shard_map/all_to_all | solution.py:139
  16.2 0.0 copy-done.2
  16.2 0.0 copy-start.1
  16.2 3.8 %convolution_convert_fusion.1.g_ref = bf16[2048,512]{1,0:T(8,128)(2,1)} fusion(bf16[2048,512]{1,0:T(8,128)(2,1)S(1)} %copy-done.2, bf16[512,512]{1,0:T(8,128)(2,1)} %param.15), kind=kOutput, calls=%fused_computation.1 | convolution fusion | flops 1074790400 | bytes 4718592 | tf_op jit(solution)/shard_map/dot_general | solution.py:188
  20.0 0.0 copy-done
  20.0 0.0 copy-done.1
  20.0 2.6 %convolution_convert_fusion.2.q_ref = bf16[2048,512]{1,0:T(8,128)(2,1)} fusion(bf16[2048,512]{1,0:T(8,128)(2,1)S(1)} %copy-done.1, bf16[512,512]{1,0:T(8,128)(2,1)S(1)} %copy-done), kind=kOutput, calls=%fused_computation.2 | convolution fusion | flops 1074790400 | bytes 4718592 | tf_op jit(solution)/shard_map/dot_general | solution.py:185
  22.6 8.4 %all-to-all-done = bf16[128,4,640]{2,1,0:T(4,128)(2,1)S(1)} async-done(((bf16[128,4,640]{2,1,0:T(4,128)(2,1)}), bf16[128,4,640]{2,1,0:T(4,128)(2,1)S(1)}, u32[]{:S(2)}, u32[]{:S(2)}) %all-to-all-start) | async-done | bytes 655392 | tf_op jit(solution)/shard_map/all_to_all | solution.py:139
  31.0 0.1 all_to_all.16
  31.1 0.8 slice.32.f_ref
  31.9 0.7 convert_reduce_fusion
  32.6 50.6 %shard_map.127 = (bf16[2048,512]{1,0:T(8,128)(2,1)}, bf16[2048,512]{1,0:T(8,128)(2,1)}, bf16[512,512]{1,0:T(8,128)(2,1)}, bf16[512,512]{1,0:T(8,128)(2,1)}, f32[128,64,128]{2,1,0:T(8,128)}) custom-call(bf16[2048,512]{1,0:T(8,128)(2,1)} %convolution_convert_fusion.2.q_ref, bf16[2048,512]{1,0:T(8,128)(2,1)} %convolution_convert_fusion.1.g_ref, ...), custom_call_target="tpu_custom_call" | custom-call | tf_op jit(solution)/shard_map/pallas_call | solution.py:103
  83.2 0.0 copy-start.4
  83.2 0.0 copy-start.6
  83.2 5.9 %all-to-all-start.1 = ((f32[128,64,128]{2,1,0:T(8,128)}), f32[128,64,128]{2,1,0:T(8,128)}, u32[]{:S(2)}, u32[]{:S(2)}) async-start(f32[128,64,128]{2,1,0:T(8,128)} %get-tuple-element.11), calls=%async_computation.1 | async-start | bytes 8388608 | tf_op jit(solution)/shard_map/all_to_all | solution.py:139
  89.1 0.0 copy-start.3
  89.1 0.0 copy-start.5
  89.2 0.0 copy-done.4
  89.2 0.5 fusion.11
  89.6 0.5 copy-done.3
  90.2 0.2 copy-done.5
  90.3 0.5 fusion.2
  90.8 0.3 reshape.109
  91.1 50.9 %all-to-all-done.1 = f32[128,64,128]{2,1,0:T(8,128)} async-done(((f32[128,64,128]{2,1,0:T(8,128)}), f32[128,64,128]{2,1,0:T(8,128)}, u32[]{:S(2)}, u32[]{:S(2)}) %all-to-all-start.1) | async-done | bytes 4194336 | tf_op jit(solution)/shard_map/all_to_all | solution.py:139
  142.1 2.5 %reduce_sum.9 = bf16[64,128]{1,0:T(8,128)(2,1)S(1)} reduce(f32[128,64,128]{2,1,0:T(8,128)} %all-to-all-done.1, f32[]{:T(128)} %constant.14.clone.1), dimensions={0}, to_apply=%region_2.3 | reduce | flops 1040384 | bytes 4210692 | tf_op jit(solution)/shard_map/reduce_sum | solution.py:152
  144.5 0.5 broadcast_in_dim.2
  145.1 1.7 pad_maximum_fusion
  146.8 4.3 %all-to-all-start.2 = ((bf16[128,80,128]{2,1,0:T(8,128)(2,1)}), bf16[128,80,128]{2,1,0:T(8,128)(2,1)S(1)}, u32[]{:S(2)}, u32[]{:S(2)}) async-start(bf16[128,80,128]{2,1,0:T(8,128)(2,1)} %pad_maximum_fusion), calls=%async_computation.2 | async-start | bytes 5242880 | tf_op jit(solution)/shard_map/all_to_all | solution.py:139
  151.1 0.9 mul.25
  151.9 1.8 mul.26
  153.7 4.2 %convolution_convert_fusion = bf16[2048,512]{1,0:T(8,128)(2,1)} fusion(bf16[2048,512]{1,0:T(8,128)(2,1)} %get-tuple-element.10, bf16[512,512]{1,0:T(8,128)(2,1)S(1)} %copy-done), kind=kOutput, calls=%fused_computation | convolution fusion | flops 1074790400 | bytes 4718592 | tf_op jit(solution)/shard_map/dot_general | solution.py:202
  157.9 29.4 %all-to-all-done.2 = bf16[128,80,128]{2,1,0:T(8,128)(2,1)S(1)} async-done(((bf16[128,80,128]{2,1,0:T(8,128)(2,1)}), bf16[128,80,128]{2,1,0:T(8,128)(2,1)S(1)}, u32[]{:S(2)}, u32[]{:S(2)}) %all-to-all-start.2) | async-done | bytes 2621472 | tf_op jit(solution)/shard_map/all_to_all | solution.py:139
  187.3 0.6 slice_convert_fusion
  187.9 2.1 %fusion.10 = (f32[128,16,128]{2,1,0:T(8,128)}, f32[128,16,128]{2,1,0:T(8,128)}, f32[128,16,128]{2,1,0:T(8,128)}, f32[128,16,128]{2,1,0:T(8,128)}) fusion(f32[128,64,128]{2,1,0:T(8,128)S(1)} %slice_convert_fusion), kind=kLoop, calls=%fused_computation.22 | loop fusion | bytes 8388608 | tf_op jit(solution)/shard_map/slice | solution.py:159
  190.1 0.1 mul.22
  190.2 1.5 fusion
  191.7 0.8 copy.31
  (7 shorter events, 0.1 us)
Async XLA Ops:
  0.6 19.4 %copy-start = (bf16[512,512]{1,0:T(8,128)(2,1)S(1)}, bf16[512,512]{1,0:T(8,128)(2,1)}, u32[]{:S(2)}) copy-start(bf16[512,512]{1,0:T(8,128)(2,1)} %param.12) | copy-start | bytes 1572868
  2.1 14.1 %copy-start.2 = (bf16[2048,512]{1,0:T(8,128)(2,1)S(1)}, bf16[2048,512]{1,0:T(8,128)(2,1)}, u32[]{:S(2)}) copy-start(bf16[2048,512]{1,0:T(8,128)(2,1)} %c_ref.1) | copy-start | bytes 6291460
  4.7 26.3 %all-to-all-start = ((bf16[128,4,640]{2,1,0:T(4,128)(2,1)}), bf16[128,4,640]{2,1,0:T(4,128)(2,1)S(1)}, u32[]{:S(2)}, u32[]{:S(2)}) async-start(bf16[128,4,640]{2,1,0:T(4,128)(2,1)} %all_to_all.14), calls=%async_computation | async-start | bytes 1310720 | tf_op jit(solution)/shard_map/all_to_all | solution.py:139
  16.2 3.8 %copy-start.1 = (bf16[2048,512]{1,0:T(8,128)(2,1)S(1)}, bf16[2048,512]{1,0:T(8,128)(2,1)}, u32[]{:S(2)}) copy-start(bf16[2048,512]{1,0:T(8,128)(2,1)} %x_ref.1) | copy-start | bytes 6291460
  83.2 5.9 %copy-start.4 = (bf16[512,512]{1,0:T(8,128)(2,1)S(1)}, bf16[512,512]{1,0:T(8,128)(2,1)}, u32[]{:S(2)}) copy-start(bf16[512,512]{1,0:T(8,128)(2,1)} %wk_ref.1) | copy-start | bytes 1572868
  83.2 5.9 %copy-start.6 = (bf16[512,512]{1,0:T(8,128)(2,1)S(1)}, bf16[512,512]{1,0:T(8,128)(2,1)}, u32[]{:S(2)}) copy-start(bf16[512,512]{1,0:T(8,128)(2,1)} %get-tuple-element.12) | copy-start | bytes 1572868
  83.2 58.8 %all-to-all-start.1 = ((f32[128,64,128]{2,1,0:T(8,128)}), f32[128,64,128]{2,1,0:T(8,128)}, u32[]{:S(2)}, u32[]{:S(2)}) async-start(f32[128,64,128]{2,1,0:T(8,128)} %get-tuple-element.11), calls=%async_computation.1 | async-start | bytes 8388608 | tf_op jit(solution)/shard_map/all_to_all | solution.py:139
  89.1 1.0 copy-start.3
  89.1 1.2 copy-start.5
  146.8 40.6 %all-to-all-start.2 = ((bf16[128,80,128]{2,1,0:T(8,128)(2,1)}), bf16[128,80,128]{2,1,0:T(8,128)(2,1)S(1)}, u32[]{:S(2)}, u32[]{:S(2)}) async-start(bf16[128,80,128]{2,1,0:T(8,128)(2,1)} %pad_maximum_fusion), calls=%async_computation.2 | async-start | bytes 5242880 | tf_op jit(solution)/shard_map/all_to_all | solution.py:139

commit v13 on v12

--- a/solution.py
+++ b/solution.py
@@ -91,7 +91,7 @@
 
 
 def fused_attention(
-    queries, out_grad, feat_tile, key_weight, value_weight, live, grid_rows, upstream, count, block=1024
+    queries, out_grad, feat_tile, key_weight, value_weight, live, grid_rows, upstream, count, block=512
 ):
     rows, width = queries.shape
     slots = feat_tile.shape[0]

time: 193 us -> 192 us (level)
  no operation moved by 1% of the time
where the time goes in v13:
time: 192 us
  waiting for transfers between devices  88.7 us (46%)
  Pallas kernels  49.8 us (26%)
  starting transfers between devices  21.9 us (11%)
  matrix products  14.3 us (7%)
  local copies, waits for them, and re-layouts  9.77 us (5%)
  other arithmetic  6.59 us (3%)
    all_to_all x3, waiting for transfers between devices, send_slots(): lax.all_to_all(outgoing, ('inline', 'crosslin'), split_axis=0, concat_axi...  88.7 us
    pallas_call x1, Pallas kernels, fused_attention(): pl.pallas_call(attention_kernel, grid=(rows // block,), in_specs=[row_blo...  49.8 us
    all_to_all x3, starting transfers between devices, send_slots(): lax.all_to_all(outgoing, ('inline', 'crosslin'), split_axis=0, concat_axi...  21.9 us
    dot_general x1, matrix products, on_device(): jnp.dot(query_grad, query_weight.T, preferred_element_type=jnp.float32)  4.2 us
  transfers between devices with their start and end apart: 3, of which 3 were waited for; matrix products, arithmetic and copies ran while one was open for 8% of the time, Pallas kernels for 0%

profile of v13, /device:TPU:1, one launch (start us, length us, event | category | flops | bytes accessed | tf_op | source)
XLA Modules:
  0.0 192.0 jit_solution(5364881944472206284)
XLA Ops:
  0.6 0.0 copy-start
  0.6 0.8 fusion.6
  1.5 0.2 reduce_window_sum.11
  1.7 0.1 copy.29
  1.8 0.1 copy.28
  1.9 0.1 eq.50
  2.1 0.0 copy-start.2
  2.1 0.1 and.15
  2.2 0.1 fusion.9
  2.3 1.4 convolution_convert_fusion.3
  3.7 1.0 all_to_all.14
  4.7 11.5 %all-to-all-start = ((bf16[128,4,640]{2,1,0:T(4,128)(2,1)}), bf16[128,4,640]{2,1,0:T(4,128)(2,1)S(1)}, u32[]{:S(2)}, u32[]{:S(2)}) async-start(bf16[128,4,640]{2,1,0:T(4,128)(2,1)} %all_to_all.14), calls=%async_computation | async-start | bytes 1310720 | tf_op jit(solution)/shard_map/all_to_all | solution.py:139
  16.2 0.0 copy-done.2
  16.2 0.0 copy-start.1
  16.2 3.8 %convolution_convert_fusion.1.g_ref = bf16[2048,512]{1,0:T(8,128)(2,1)} fusion(bf16[2048,512]{1,0:T(8,128)(2,1)S(1)} %copy-done.2, bf16[512,512]{1,0:T(8,128)(2,1)} %param.15), kind=kOutput, calls=%fused_computation.1 | convolution fusion | flops 1074790400 | bytes 4718592 | tf_op jit(solution)/shard_map/dot_general | solution.py:188
  20.0 0.0 copy-done
  20.0 0.0 copy-done.1
  20.0 2.6 %convolution_convert_fusion.2.q_ref = bf16[2048,512]{1,0:T(8,128)(2,1)} fusion(bf16[2048,512]{1,0:T(8,128)(2,1)S(1)} %copy-done.1, bf16[512,512]{1,0:T(8,128)(2,1)S(1)} %copy-done), kind=kOutput, calls=%fused_computation.2 | convolution fusion | flops 1074790400 | bytes 4718592 | tf_op jit(solution)/shard_map/dot_general | solution.py:185
  22.6 8.4 %all-to-all-done = bf16[128,4,640]{2,1,0:T(4,128)(2,1)S(1)} async-done(((bf16[128,4,640]{2,1,0:T(4,128)(2,1)}), bf16[128,4,640]{2,1,0:T(4,128)(2,1)S(1)}, u32[]{:S(2)}, u32[]{:S(2)}) %all-to-all-start) | async-done | bytes 655392 | tf_op jit(solution)/shard_map/all_to_all | solution.py:139
  31.0 0.1 all_to_all.16
  31.1 0.8 slice.32.f_ref
  31.9 0.7 convert_reduce_fusion
  32.6 49.8 %shard_map.127 = (bf16[2048,512]{1,0:T(8,128)(2,1)}, bf16[2048,512]{1,0:T(8,128)(2,1)}, bf16[512,512]{1,0:T(8,128)(2,1)}, bf16[512,512]{1,0:T(8,128)(2,1)}, f32[128,64,128]{2,1,0:T(8,128)}) custom-call(bf16[2048,512]{1,0:T(8,128)(2,1)} %convolution_convert_fusion.2.q_ref, bf16[2048,512]{1,0:T(8,128)(2,1)} %convolution_convert_fusion.1.g_ref, ...), custom_call_target="tpu_custom_call" | custom-call | tf_op jit(solution)/shard_map/pallas_call | solution.py:103
  82.4 0.0 copy-start.4
  82.5 0.0 copy-start.6
  82.5 6.1 %all-to-all-start.1 = ((f32[128,64,128]{2,1,0:T(8,128)}), f32[128,64,128]{2,1,0:T(8,128)}, u32[]{:S(2)}, u32[]{:S(2)}) async-start(f32[128,64,128]{2,1,0:T(8,128)} %get-tuple-element.11), calls=%async_computation.1 | async-start | bytes 8388608 | tf_op jit(solution)/shard_map/all_to_all | solution.py:139
  88.6 0.0 copy-start.3
  88.6 0.0 copy-start.5
  88.6 0.0 copy-done.4
  88.6 0.5 fusion.11
  89.1 0.5 copy-done.3
  89.6 0.2 copy-done.5
  89.8 0.5 fusion.2
  90.2 0.3 reshape.109
  90.6 50.9 %all-to-all-done.1 = f32[128,64,128]{2,1,0:T(8,128)} async-done(((f32[128,64,128]{2,1,0:T(8,128)}), f32[128,64,128]{2,1,0:T(8,128)}, u32[]{:S(2)}, u32[]{:S(2)}) %all-to-all-start.1) | async-done | bytes 4194336 | tf_op jit(solution)/shard_map/all_to_all | solution.py:139
  141.5 2.5 %reduce_sum.9 = bf16[64,128]{1,0:T(8,128)(2,1)S(1)} reduce(f32[128,64,128]{2,1,0:T(8,128)} %all-to-all-done.1, f32[]{:T(128)} %constant.14.clone.1), dimensions={0}, to_apply=%region_2.3 | reduce | flops 1040384 | bytes 4210692 | tf_op jit(solution)/shard_map/reduce_sum | solution.py:152
  144.0 0.5 broadcast_in_dim.2
  144.5 1.7 pad_maximum_fusion
  146.2 4.3 %all-to-all-start.2 = ((bf16[128,80,128]{2,1,0:T(8,128)(2,1)}), bf16[128,80,128]{2,1,0:T(8,128)(2,1)S(1)}, u32[]{:S(2)}, u32[]{:S(2)}) async-start(bf16[128,80,128]{2,1,0:T(8,128)(2,1)} %pad_maximum_fusion), calls=%async_computation.2 | async-start | bytes 5242880 | tf_op jit(solution)/shard_map/all_to_all | solution.py:139
  150.5 0.9 mul.25
  151.4 1.8 mul.26
  153.2 4.2 %convolution_convert_fusion = bf16[2048,512]{1,0:T(8,128)(2,1)} fusion(bf16[2048,512]{1,0:T(8,128)(2,1)} %get-tuple-element.10, bf16[512,512]{1,0:T(8,128)(2,1)S(1)} %copy-done), kind=kOutput, calls=%fused_computation | convolution fusion | flops 1074790400 | bytes 4718592 | tf_op jit(solution)/shard_map/dot_general | solution.py:202
  157.4 29.4 %all-to-all-done.2 = bf16[128,80,128]{2,1,0:T(8,128)(2,1)S(1)} async-done(((bf16[128,80,128]{2,1,0:T(8,128)(2,1)}), bf16[128,80,128]{2,1,0:T(8,128)(2,1)S(1)}, u32[]{:S(2)}, u32[]{:S(2)}) %all-to-all-start.2) | async-done | bytes 2621472 | tf_op jit(solution)/shard_map/all_to_all | solution.py:139
  186.8 0.6 slice_convert_fusion
  187.3 2.1 %fusion.10 = (f32[128,16,128]{2,1,0:T(8,128)}, f32[128,16,128]{2,1,0:T(8,128)}, f32[128,16,128]{2,1,0:T(8,128)}, f32[128,16,128]{2,1,0:T(8,128)}) fusion(f32[128,64,128]{2,1,0:T(8,128)S(1)} %slice_convert_fusion), kind=kLoop, calls=%fused_computation.22 | loop fusion | bytes 8388608 | tf_op jit(solution)/shard_map/slice | solution.py:159
  189.5 0.1 mul.22
  189.6 1.5 fusion
  191.1 0.8 copy.31
  (7 shorter events, 0.1 us)
Async XLA Ops:
  0.6 19.4 %copy-start = (bf16[512,512]{1,0:T(8,128)(2,1)S(1)}, bf16[512,512]{1,0:T(8,128)(2,1)}, u32[]{:S(2)}) copy-start(bf16[512,512]{1,0:T(8,128)(2,1)} %param.12) | copy-start | bytes 1572868
  2.1 14.1 %copy-start.2 = (bf16[2048,512]{1,0:T(8,128)(2,1)S(1)}, bf16[2048,512]{1,0:T(8,128)(2,1)}, u32[]{:S(2)}) copy-start(bf16[2048,512]{1,0:T(8,128)(2,1)} %c_ref.1) | copy-start | bytes 6291460
  4.7 26.3 %all-to-all-start = ((bf16[128,4,640]{2,1,0:T(4,128)(2,1)}), bf16[128,4,640]{2,1,0:T(4,128)(2,1)S(1)}, u32[]{:S(2)}, u32[]{:S(2)}) async-start(bf16[128,4,640]{2,1,0:T(4,128)(2,1)} %all_to_all.14), calls=%async_computation | async-start | bytes 1310720 | tf_op jit(solution)/shard_map/all_to_all | solution.py:139
  16.2 3.8 %copy-start.1 = (bf16[2048,512]{1,0:T(8,128)(2,1)S(1)}, bf16[2048,512]{1,0:T(8,128)(2,1)}, u32[]{:S(2)}) copy-start(bf16[2048,512]{1,0:T(8,128)(2,1)} %x_ref.1) | copy-start | bytes 6291460
  82.4 6.2 %copy-start.4 = (bf16[512,512]{1,0:T(8,128)(2,1)S(1)}, bf16[512,512]{1,0:T(8,128)(2,1)}, u32[]{:S(2)}) copy-start(bf16[512,512]{1,0:T(8,128)(2,1)} %wk_ref.1) | copy-start | bytes 1572868
  82.5 6.2 %copy-start.6 = (bf16[512,512]{1,0:T(8,128)(2,1)S(1)}, bf16[512,512]{1,0:T(8,128)(2,1)}, u32[]{:S(2)}) copy-start(bf16[512,512]{1,0:T(8,128)(2,1)} %get-tuple-element.12) | copy-start | bytes 1572868
  82.5 59.1 %all-to-all-start.1 = ((f32[128,64,128]{2,1,0:T(8,128)}), f32[128,64,128]{2,1,0:T(8,128)}, u32[]{:S(2)}, u32[]{:S(2)}) async-start(f32[128,64,128]{2,1,0:T(8,128)} %get-tuple-element.11), calls=%async_computation.1 | async-start | bytes 8388608 | tf_op jit(solution)/shard_map/all_to_all | solution.py:139
  88.6 1.0 copy-start.3
  88.6 1.2 copy-start.5
  146.2 40.6 %all-to-all-start.2 = ((bf16[128,80,128]{2,1,0:T(8,128)(2,1)}), bf16[128,80,128]{2,1,0:T(8,128)(2,1)S(1)}, u32[]{:S(2)}, u32[]{:S(2)}) async-start(bf16[128,80,128]{2,1,0:T(8,128)(2,1)} %pad_maximum_fusion), calls=%async_computation.2 | async-start | bytes 5242880 | tf_op jit(solution)/shard_map/all_to_all | solution.py:139

commit v14 on v13

--- a/solution.py
+++ b/solution.py
@@ -149,11 +149,12 @@
 def sum_over_devices(pieces, shape, rider):
     count = pieces.shape[0]
     depth = pieces.shape[1] // 4
-    mine = send_slots(pieces).sum(axis=0, keepdims=True).astype(jnp.bfloat16)
     rider_rows = rider.size // (count * 128)
-    payload = jnp.concatenate(
-        [jnp.broadcast_to(mine, pieces.shape), rider.reshape(count, rider_rows, 128)], axis=1
-    )
+    blank = jnp.zeros(pieces.shape, jnp.bfloat16)
+    payload = jnp.concatenate([blank, rider.reshape(count, rider_rows, 128)], axis=1)
+    received, payload = lax.optimization_barrier((send_slots(pieces), payload))
+    mine = received.sum(axis=0, keepdims=True).astype(jnp.bfloat16)
+    payload = lax.dynamic_update_slice(payload, jnp.broadcast_to(mine, pieces.shape), (0, 0, 0))
     arrived = send_slots(payload)
     gathered = arrived[:, : pieces.shape[1]].astype(jnp.float32)
     sums = tuple(from_tiles(gathered[:, i * depth : (i + 1) * depth], shape) for i in range(4))

time: 192 us -> 192 us (level)
  local copies, waits for them, and re-layouts: 9.77 us -> 13 us
  transfers between devices with their start and end apart: 3 -> 3, of which waited for: 3 -> 3; matrix products, arithmetic and copies ran while one was open for 8% -> 9% of each run, Pallas kernels for 0% -> 0%
where the time goes in v14:
time: 192 us
  waiting for transfers between devices  86.8 us (45%)
  Pallas kernels  49.8 us (26%)
  starting transfers between devices  21.9 us (11%)
  matrix products  14.3 us (7%)
  local copies, waits for them, and re-layouts  13 us (7%)
  other arithmetic  4.89 us (3%)
    all_to_all x3, waiting for transfers between devices, send_slots(): lax.all_to_all(outgoing, ('inline', 'crosslin'), split_axis=0, concat_axi...  86.8 us
    pallas_call x1, Pallas kernels, fused_attention(): pl.pallas_call(attention_kernel, grid=(rows // block,), in_specs=[row_blo...  49.8 us
    all_to_all x3, starting transfers between devices, send_slots(): lax.all_to_all(outgoing, ('inline', 'crosslin'), split_axis=0, concat_axi...  21.9 us
    dot_general x1, matrix products, on_device(): jnp.dot(query_grad, query_weight.T, preferred_element_type=jnp.float32)  4.2 us
  transfers between devices with their start and end apart: 3, of which 3 were waited for; matrix products, arithmetic and copies ran while one was open for 9% of the time, Pallas kernels for 0%

profile of v14, /device:TPU:1, one launch (start us, length us, event | category | flops | bytes accessed | tf_op | source)
XLA Modules:
  0.0 191.6 jit_solution(2534810845234230773)
XLA Ops:
  0.6 0.0 copy-start
  0.6 0.8 fusion.6
  1.5 0.2 reduce_window_sum.11
  1.7 0.1 copy.25
  1.8 0.1 copy.24
  1.9 0.1 eq.50
  2.1 0.0 copy-start.2
  2.1 0.1 and.15
  2.2 0.1 fusion.9
  2.3 1.4 convolution_convert_fusion.3
  3.7 1.0 all_to_all.14
  4.7 11.5 %all-to-all-start = ((bf16[128,4,640]{2,1,0:T(4,128)(2,1)}), bf16[128,4,640]{2,1,0:T(4,128)(2,1)S(1)}, u32[]{:S(2)}, u32[]{:S(2)}) async-start(bf16[128,4,640]{2,1,0:T(4,128)(2,1)} %all_to_all.14), calls=%async_computation | async-start | bytes 1310720 | tf_op jit(solution)/shard_map/all_to_all | solution.py:139
  16.2 0.0 copy-done.2
  16.2 0.0 copy-start.1
  16.2 3.8 %convolution_convert_fusion.1.g_ref = bf16[2048,512]{1,0:T(8,128)(2,1)} fusion(bf16[2048,512]{1,0:T(8,128)(2,1)S(1)} %copy-done.2, bf16[512,512]{1,0:T(8,128)(2,1)} %param.15), kind=kOutput, calls=%fused_computation.1 | convolution fusion | flops 1074790400 | bytes 4718592 | tf_op jit(solution)/shard_map/dot_general | solution.py:189
  20.0 0.0 copy-done
  20.0 0.0 copy-done.1
  20.0 2.6 %convolution_convert_fusion.2.q_ref = bf16[2048,512]{1,0:T(8,128)(2,1)} fusion(bf16[2048,512]{1,0:T(8,128)(2,1)S(1)} %copy-done.1, bf16[512,512]{1,0:T(8,128)(2,1)S(1)} %copy-done), kind=kOutput, calls=%fused_computation.2 | convolution fusion | flops 1074790400 | bytes 4718592 | tf_op jit(solution)/shard_map/dot_general | solution.py:186
  22.6 8.4 %all-to-all-done = bf16[128,4,640]{2,1,0:T(4,128)(2,1)S(1)} async-done(((bf16[128,4,640]{2,1,0:T(4,128)(2,1)}), bf16[128,4,640]{2,1,0:T(4,128)(2,1)S(1)}, u32[]{:S(2)}, u32[]{:S(2)}) %all-to-all-start) | async-done | bytes 655392 | tf_op jit(solution)/shard_map/all_to_all | solution.py:139
  31.0 0.1 all_to_all.16
  31.1 0.8 slice.32.f_ref
  31.9 0.7 convert_reduce_fusion
  32.6 49.8 %shard_map.127 = (bf16[2048,512]{1,0:T(8,128)(2,1)}, bf16[2048,512]{1,0:T(8,128)(2,1)}, bf16[512,512]{1,0:T(8,128)(2,1)}, bf16[512,512]{1,0:T(8,128)(2,1)}, f32[128,64,128]{2,1,0:T(8,128)}) custom-call(bf16[2048,512]{1,0:T(8,128)(2,1)} %convolution_convert_fusion.2.q_ref, bf16[2048,512]{1,0:T(8,128)(2,1)} %convolution_convert_fusion.1.g_ref, ...), custom_call_target="tpu_custom_call" | custom-call | tf_op jit(solution)/shard_map/pallas_call | solution.py:103
  82.4 0.0 copy-start.4
  82.5 0.0 copy-start.6
  82.5 6.1 %all-to-all-start.1 = ((f32[128,64,128]{2,1,0:T(8,128)}), f32[128,64,128]{2,1,0:T(8,128)}, u32[]{:S(2)}, u32[]{:S(2)}) async-start(f32[128,64,128]{2,1,0:T(8,128)} %get-tuple-element.13), calls=%async_computation.1 | async-start | bytes 8388608 | tf_op jit(solution)/shard_map/all_to_all | solution.py:139
  88.6 0.0 copy-start.3
  88.6 0.0 copy-start.5
  88.6 0.0 copy-done.4
  88.6 0.5 fusion.11
  89.1 0.5 copy-done.3
  89.6 0.2 copy-done.5
  89.8 0.5 fusion.2
  90.2 0.3 reshape.109
  90.6 1.9 concatenate.7
  92.4 49.1 %all-to-all-done.1 = f32[128,64,128]{2,1,0:T(8,128)} async-done(((f32[128,64,128]{2,1,0:T(8,128)}), f32[128,64,128]{2,1,0:T(8,128)}, u32[]{:S(2)}, u32[]{:S(2)}) %all-to-all-start.1) | async-done | bytes 4194336 | tf_op jit(solution)/shard_map/all_to_all | solution.py:139
  141.5 2.5 %reduce_sum.9 = bf16[64,128]{1,0:T(8,128)(2,1)S(1)} reduce(f32[128,64,128]{2,1,0:T(8,128)} %all-to-all-done.1, f32[]{:T(128)} %constant.17.clone.1), dimensions={0}, to_apply=%region_2.3 | reduce | flops 1040384 | bytes 4210692 | tf_op jit(solution)/shard_map/reduce_sum | solution.py:156
  144.0 1.9 broadcast_dynamic-update-slice_fusion
  145.8 4.3 %all-to-all-start.2 = ((bf16[128,80,128]{2,1,0:T(8,128)(2,1)}), bf16[128,80,128]{2,1,0:T(8,128)(2,1)S(1)}, u32[]{:S(2)}, u32[]{:S(2)}) async-start(bf16[128,80,128]{2,1,0:T(8,128)(2,1)} %broadcast_dynamic-update-slice_fusion), calls=%async_computation.2 | async-start | bytes 5242880 | tf_op jit(solution)/shard_map/all_to_all | solution.py:139
  150.2 0.9 mul.25
  151.0 1.8 mul.26
  152.8 4.2 %convolution_convert_fusion = bf16[2048,512]{1,0:T(8,128)(2,1)} fusion(bf16[2048,512]{1,0:T(8,128)(2,1)} %get-tuple-element.12, bf16[512,512]{1,0:T(8,128)(2,1)S(1)} %copy-done), kind=kOutput, calls=%fused_computation | convolution fusion | flops 1074790400 | bytes 4718592 | tf_op jit(solution)/shard_map/dot_general | solution.py:203
  157.0 29.4 %all-to-all-done.2 = bf16[128,80,128]{2,1,0:T(8,128)(2,1)S(1)} async-done(((bf16[128,80,128]{2,1,0:T(8,128)(2,1)}), bf16[128,80,128]{2,1,0:T(8,128)(2,1)S(1)}, u32[]{:S(2)}, u32[]{:S(2)}) %all-to-all-start.2) | async-done | bytes 2621472 | tf_op jit(solution)/shard_map/all_to_all | solution.py:139
  186.4 0.6 slice_convert_fusion
  187.0 2.1 %fusion.10 = (f32[128,16,128]{2,1,0:T(8,128)}, f32[128,16,128]{2,1,0:T(8,128)}, f32[128,16,128]{2,1,0:T(8,128)}, f32[128,16,128]{2,1,0:T(8,128)}) fusion(f32[128,64,128]{2,1,0:T(8,128)S(1)} %slice_convert_fusion), kind=kLoop, calls=%fused_computation.22 | loop fusion | bytes 8388608 | tf_op jit(solution)/shard_map/slice | solution.py:160
  189.1 0.1 mul.22
  189.3 1.5 fusion
  190.8 0.8 copy.27
  (7 shorter events, 0.1 us)
Async XLA Ops:
  0.6 19.4 %copy-start = (bf16[512,512]{1,0:T(8,128)(2,1)S(1)}, bf16[512,512]{1,0:T(8,128)(2,1)}, u32[]{:S(2)}) copy-start(bf16[512,512]{1,0:T(8,128)(2,1)} %param.12) | copy-start | bytes 1572868
  2.1 14.1 %copy-start.2 = (bf16[2048,512]{1,0:T(8,128)(2,1)S(1)}, bf16[2048,512]{1,0:T(8,128)(2,1)}, u32[]{:S(2)}) copy-start(bf16[2048,512]{1,0:T(8,128)(2,1)} %c_ref.1) | copy-start | bytes 6291460
  4.7 26.3 %all-to-all-start = ((bf16[128,4,640]{2,1,0:T(4,128)(2,1)}), bf16[128,4,640]{2,1,0:T(4,128)(2,1)S(1)}, u32[]{:S(2)}, u32[]{:S(2)}) async-start(bf16[128,4,640]{2,1,0:T(4,128)(2,1)} %all_to_all.14), calls=%async_computation | async-start | bytes 1310720 | tf_op jit(solution)/shard_map/all_to_all | solution.py:139
  16.2 3.8 %copy-start.1 = (bf16[2048,512]{1,0:T(8,128)(2,1)S(1)}, bf16[2048,512]{1,0:T(8,128)(2,1)}, u32[]{:S(2)}) copy-start(bf16[2048,512]{1,0:T(8,128)(2,1)} %x_ref.1) | copy-start | bytes 6291460
  82.4 6.2 %copy-start.4 = (bf16[512,512]{1,0:T(8,128)(2,1)S(1)}, bf16[512,512]{1,0:T(8,128)(2,1)}, u32[]{:S(2)}) copy-start(bf16[512,512]{1,0:T(8,128)(2,1)} %wk_ref.1) | copy-start | bytes 1572868
  82.5 6.2 %copy-start.6 = (bf16[512,512]{1,0:T(8,128)(2,1)S(1)}, bf16[512,512]{1,0:T(8,128)(2,1)}, u32[]{:S(2)}) copy-start(bf16[512,512]{1,0:T(8,128)(2,1)} %get-tuple-element.14) | copy-start | bytes 1572868
  82.5 59.1 %all-to-all-start.1 = ((f32[128,64,128]{2,1,0:T(8,128)}), f32[128,64,128]{2,1,0:T(8,128)}, u32[]{:S(2)}, u32[]{:S(2)}) async-start(f32[128,64,128]{2,1,0:T(8,128)} %get-tuple-element.13), calls=%async_computation.1 | async-start | bytes 8388608 | tf_op jit(solution)/shard_map/all_to_all | solution.py:139
  88.6 1.0 copy-start.3
  88.6 1.2 copy-start.5
  145.8 40.6 %all-to-all-start.2 = ((bf16[128,80,128]{2,1,0:T(8,128)(2,1)}), bf16[128,80,128]{2,1,0:T(8,128)(2,1)S(1)}, u32[]{:S(2)}, u32[]{:S(2)}) async-start(bf16[128,80,128]{2,1,0:T(8,128)(2,1)} %broadcast_dynamic-update-slice_fusion), calls=%async_computation.2 | async-start | bytes 5242880 | tf_op jit(solution)/shard_map/all_to_all | solution.py:139
